TPU v7x, 128 devices: a whole 4x4x4 slice. The times are simulated.
128 devices in a mesh: row: 8 (over x, y_hi), col: 16 (over y_lo, z, core).
Axes of the slice: x: 4, y: 4 (y_hi: 2, y_lo: 2; y = y_hi * 2 + y_lo), z: 4, core: 2. Of those that a mesh axis runs over, the one named last changes fastest.
Arguments:
- flat_gradient: bfloat16 [8, 16, 524288], P('row', 'col'), may hold values from -6 to 6
- range_rows: int32 [8, 16], replicated, may hold values from 1 to 64, 512 in all within a row
- left_stat: float32 [4096, 4096], P('row', 'col'), may hold values from -6 to 6
- right_stat: float32 [8192, 8192], P('col', 'row'), may hold values from -6 to 6
- left_root: bfloat16 [4096, 4096], P('row'), as said below
- right_root: bfloat16 [8192, 8192], P('col'), as said below
Outputs:
- left_new: float32 [4096, 4096], P('row', 'col')
- right_new: float32 [8192, 8192], P('col', 'row')
- update: bfloat16 [4096, 8192], P('row', 'col')
Inputs may be any that keep to these rules, and one draw needn't show every extreme that they name: In each row r the entries sum to 512; the largest entry of every row is exactly 64. Slots of flat_gradient beyond a device's range_rows rows are padding. left_root equals its transpose. right_root equals its transpose.
All inputs are finite; a program needn't handle non-finite values.
Results may differ from a plain program's by a relative error of at most 0.014.
Values may be sent and summed in bfloat16 or wider, within the bound.
No kernel may reach another device: no remote copies, remote signals or barrier semaphores. Data moves between devices by JAX's collectives and lax.ppermute only.
A program may use at most 192 MiB of HBM per device.

v0:
```python
import math

import jax
import jax.numpy as jnp
from jax import lax
from jax.sharding import Mesh
from jax.sharding import PartitionSpec as P

HQ = 4096
DIN = 8192


stat_decay = 0.9

COL = ("chip", "core")


def slot_index(row_counts, tile_rows, capacity):
    offsets = jnp.cumsum(row_counts) - row_counts
    target = jnp.arange(tile_rows, dtype=jnp.int32)
    covered = target[:, None] >= offsets[None, :]
    source = jnp.sum(covered.astype(jnp.int32), axis=1) - 1
    begins = jnp.max(jnp.where(covered, offsets[None, :], 0), axis=1)
    return source * capacity + target - begins


def partner(block):
    return lax.ppermute(block, "core", [(0, 1), (1, 0)])


def shards(flat_gradient, range_rows, left_stat, right_stat, left_root, right_root):
    row_count = lax.axis_size("row")
    chip_count = lax.axis_size("chip")
    col_count = chip_count * 2
    row_index = lax.axis_index("row")
    core = lax.axis_index("core")
    tile_rows = HQ // row_count
    tile_cols = DIN // col_count
    slice_rows = tile_rows // col_count
    block_cols = DIN // row_count
    chunk = HQ // col_count
    capacity = flat_gradient.shape[2] // DIN
    held_rows = flat_gradient.reshape(capacity, DIN)
    received = lax.all_to_all(held_rows, COL, split_axis=1, concat_axis=0, tiled=True)
    row_counts = lax.dynamic_index_in_dim(range_rows, row_index, 0, keepdims=False)
    grad_tile = jnp.take(received, slot_index(row_counts, tile_rows, capacity), axis=0)
    row_slice = lax.all_to_all(grad_tile, COL, split_axis=0, concat_axis=1, tiled=True)
    block_piece = lax.all_to_all(row_slice, "row", split_axis=1, concat_axis=0, tiled=True)
    row_block = lax.all_gather(block_piece, COL, axis=0, tiled=True)
    shifted_tiles = [grad_tile] + [
        lax.ppermute(grad_tile, "row", [(i, (i + s) % row_count) for i in range(row_count)])
        for s in range(1, row_count)
    ]
    order = (row_index - jnp.arange(row_count, dtype=jnp.int32)) % row_count
    column_panel = jnp.take(jnp.stack(shifted_tiles), order, axis=0).reshape(HQ, tile_cols)
    panel_chunks = column_panel.reshape(chip_count, 2, chunk, tile_cols)
    keep_rows = lax.dynamic_index_in_dim(panel_chunks, core, 1, keepdims=False)
    send_rows = lax.dynamic_index_in_dim(panel_chunks, 1 - core, 1, keepdims=False)
    contract = (((1,), (2,)), ((), ()))
    keep = lax.dot_general(grad_tile, keep_rows, contract, preferred_element_type=jnp.float32)
    send = lax.dot_general(grad_tile, send_rows, contract, preferred_element_type=jnp.float32)
    chip_sum = keep + partner(send.astype(jnp.bfloat16)).astype(jnp.float32)
    left_sum = lax.psum_scatter(
        chip_sum.astype(jnp.bfloat16), "chip", scatter_dimension=1, tiled=True
    ).reshape(tile_rows, chunk).astype(jnp.float32)
    panel_reordered = (
        column_panel.reshape(row_count, col_count, slice_rows, tile_cols)
        .transpose(1, 0, 2, 3)
        .reshape(HQ, tile_cols)
    )
    right_gram = lax.dot_general(
        panel_reordered, row_block, (((0,), (0,)), ((), ())), preferred_element_type=jnp.float32
    )
    right_new = stat_decay * right_stat + right_gram * (1.0 / math.sqrt(HQ))
    left_mixed = jnp.dot(left_root, column_panel, preferred_element_type=jnp.float32).astype(
        jnp.bfloat16
    )
    update_sum = lax.dot_general(
        lax.all_gather(left_mixed, COL, axis=1, tiled=True),
        right_root,
        (((1,), (1,)), ((), ())),
        preferred_element_type=jnp.float32,
    )
    left_new = stat_decay * left_stat + left_sum * (1.0 / math.sqrt(DIN))
    return (left_new, right_new, update_sum.astype(jnp.bfloat16))


def solution(mesh):
    rows, cols = mesh.devices.shape
    split_mesh = Mesh(mesh.devices.reshape(rows, cols // 2, 2), ("row", "chip", "core"))
    in_specs = (
        P("row", COL, None),
        P(),
        P("row", COL),
        P(COL, "row"),
        P("row", None),
        P(COL, None),
    )
    out_specs = (P("row", COL), P(COL, "row"), P("row", COL))
    return jax.shard_map(
        shards, mesh=split_mesh, in_specs=in_specs, out_specs=out_specs, check_vma=False
    )
```

profile of v0, /device:TPU:1, one launch (start us, length us, event | category | flops | bytes accessed | tf_op | source)
XLA Modules:
  0.0 305.0 jit_solution(13569481022520142437)
XLA Ops:
  8.0 22.8 %reduce = bf16[524288]{0:T(1024)(128)(2,1)S(1)} reduce(bf16[1,1,524288]{2,1,0:T(2,128)(2,1)} %param.6, bf16[]{:T(256)} %constant.90), dimensions={0,1}, to_apply=%param.6.reduce_sub_computation | reduce | bytes 2097154 | tf_op args[0]
  31.5 1.5 copy.27
  33.0 7.8 %all-to-all-start = ((bf16[64,16,512]{2,0,1:T(8,128)(2,1)}), bf16[64,16,512]{2,0,1:T(8,128)(2,1)S(1)}, u32[]{:S(2)}, u32[]{:S(2)}) async-start(bf16[64,16,512]{2,0,1:T(8,128)(2,1)} %copy.27), calls=%async_computation | async-start | bytes 2097152 | tf_op jit(solution)/shard_map/all_to_all | solution.py:44
  42.6 14.0 %all-to-all-done = bf16[64,16,512]{2,0,1:T(8,128)(2,1)S(1)} async-done(((bf16[64,16,512]{2,0,1:T(8,128)(2,1)}), bf16[64,16,512]{2,0,1:T(8,128)(2,1)S(1)}, u32[]{:S(2)}, u32[]{:S(2)}) %all-to-all-start) | async-done | bytes 1048608 | tf_op jit(solution)/shard_map/all_to_all | solution.py:44
  56.7 2.0 gather_fusion
  58.8 2.7 collective-permute-start
  62.8 2.0 collective-permute-start.2
  65.8 1.7 collective-permute-start.3
  67.5 4.2 %collective-permute-start.4 = (bf16[512,512]{1,0:T(8,128)(2,1)S(1)}, bf16[512,512]{1,0:T(8,128)(2,1)S(1)}, u32[]{:S(2)}, u32[]{:S(2)}) collective-permute-start(bf16[512,512]{1,0:T(8,128)(2,1)S(1)} %broadcast_select_fusion), channel_id=1, source_target_pairs={{0,80},{16,96},{32,112},{48,0},{64,16},{80,32},{96,48},{112,64},{1... | collective-permute-start | bytes 1572872 | tf_op jit(solution)/shard_map/ppermute | solution.py:51
  71.7 3.4 %collective-permute-done = bf16[512,512]{1,0:T(8,128)(2,1)S(1)} collective-permute-done((bf16[512,512]{1,0:T(8,128)(2,1)S(1)}, bf16[512,512]{1,0:T(8,128)(2,1)S(1)}, u32[]{:S(2)}, u32[]{:S(2)}) %collective-permute-start) | collective-permute-done | bytes 524320 | tf_op jit(solution)/shard_map/ppermute | solution.py:51
  75.1 9.3 %collective-permute-start.5 = (bf16[512,512]{1,0:T(8,128)(2,1)S(1)}, bf16[512,512]{1,0:T(8,128)(2,1)S(1)}, u32[]{:S(2)}, u32[]{:S(2)}) collective-permute-start(bf16[512,512]{1,0:T(8,128)(2,1)S(1)} %broadcast_select_fusion), channel_id=1, source_target_pairs={{0,96},{16,112},{32,0},{48,16},{64,32},{80,48},{96,64},{112,80},{1... | collective-permute-start | bytes 1572872 | tf_op jit(solution)/shard_map/ppermute | solution.py:51
  85.2 10.0 %collective-permute-start.6 = (bf16[512,512]{1,0:T(8,128)(2,1)S(1)}, bf16[512,512]{1,0:T(8,128)(2,1)S(1)}, u32[]{:S(2)}, u32[]{:S(2)}) collective-permute-start(bf16[512,512]{1,0:T(8,128)(2,1)S(1)} %broadcast_select_fusion), channel_id=1, source_target_pairs={{0,112},{16,0},{32,16},{48,32},{64,48},{80,64},{96,80},{112,96},{1... | collective-permute-start | bytes 1572872 | tf_op jit(solution)/shard_map/ppermute | solution.py:51
  96.1 15.2 %collective-permute-done.2 = bf16[512,512]{1,0:T(8,128)(2,1)S(1)} collective-permute-done((bf16[512,512]{1,0:T(8,128)(2,1)S(1)}, bf16[512,512]{1,0:T(8,128)(2,1)S(1)}, u32[]{:S(2)}, u32[]{:S(2)}) %collective-permute-start.2) | collective-permute-done | bytes 524320 | tf_op jit(solution)/shard_map/ppermute | solution.py:51
  112.9 4.4 %collective-permute-done.4 = bf16[512,512]{1,0:T(8,128)(2,1)S(1)} collective-permute-done((bf16[512,512]{1,0:T(8,128)(2,1)S(1)}, bf16[512,512]{1,0:T(8,128)(2,1)S(1)}, u32[]{:S(2)}, u32[]{:S(2)}) %collective-permute-start.4) | collective-permute-done | bytes 524320 | tf_op jit(solution)/shard_map/ppermute | solution.py:51
  119.0 6.4 %collective-permute-done.6 = bf16[512,512]{1,0:T(8,128)(2,1)S(1)} collective-permute-done((bf16[512,512]{1,0:T(8,128)(2,1)S(1)}, bf16[512,512]{1,0:T(8,128)(2,1)S(1)}, u32[]{:S(2)}, u32[]{:S(2)}) %collective-permute-start.6) | collective-permute-done | bytes 524320 | tf_op jit(solution)/shard_map/ppermute | solution.py:51
  126.2 4.9 %gather_fusion.1 = bf16[8,512,512]{2,1,0:T(8,128)(2,1)} fusion(bf16[8,512,512]{2,1,0:T(8,128)(2,1)} %bitcast_dynamic-update-slice_fusion, s32[1024]{0:T(1024)S(1)} %pad_clamp_fusion), kind=kCustom, calls=%fused_computation.1 | custom fusion | bytes 8388640 | tf_op jit(solution)/shard_map/jit(_take)/gather | solution.py:55
  131.1 2.7 copy_select_fusion.1
  133.8 1.9 copy-done
  135.7 2.6 fusion.8
  138.3 1.8 collective-permute-start.7
  140.2 4.1 %collective-permute-done.7 = bf16[512,8,256]{2,0,1:T(8,128)(2,1)} collective-permute-done((bf16[512,8,256]{2,0,1:T(8,128)(2,1)}, bf16[512,8,256]{2,0,1:T(8,128)(2,1)}, u32[]{:S(2)}, u32[]{:S(2)}) %collective-permute-start.7) | collective-permute-done | bytes 2097184 | tf_op jit(solution)/shard_map/ppermute | solution.py:28
  144.3 4.8 %add_convert_fusion = bf16[512,8,256]{2,0,1:T(8,128)(2,1)} fusion(bf16[512,8,256]{2,0,1:T(8,128)(2,1)} %collective-permute-done.7, bf16[8,2,256,512]{3,2,0,1:T(8,128)(2,1)} %copy-done, s32[]{:T(128)S(6)} %select_n.106, bf16[512,512]{1,0:T(8,128)(2,1)S(1)} %broadcast_select_fusion), kind=kOutput, calls=%fused_computation.5 | convolution fusion | flops 1076887552 | bytes 6815748 | tf_op jit(solution)/shard_map/dot_general | solution.py:60
  149.3 2.7 bitcast_select_fusion
  152.7 3.2 %fusion.11 = bf16[512,512]{0,1:T(8,128)(2,1)} fusion(bf16[4096,512]{1,0:T(8,128)(2,1)S(1)} %bitcast_select_fusion, bf16[512,4096]{1,0:T(8,128)(2,1)S(1)} %copy-done.2), kind=kOutput, calls=%fused_computation.16 | convolution fusion | flops 2147745792 | bytes 8912896 | tf_op jit(solution)/shard_map/dot_general | solution.py:75
  156.3 20.9 %all_to_all.51 = bf16[16,32,512]{2,1,0:T(8,128)(2,1)S(1)} all-to-all(bf16[16,32,512]{2,1,0:T(8,128)(2,1)S(1)} %broadcast_select_fusion.1), channel_id=1, replica_groups=mesh['row'=8,'chip'=8,'core'=2] {'chip','core'}, dimensions={0} | all-to-all | bytes 1048576 | tf_op jit(solution)/shard_map/all_to_all | solution.py:47
  178.0 15.5 %all_to_all.52 = bf16[32,8,1024]{2,0,1:T(8,128)(2,1)} all-to-all(bf16[32,8,1024]{2,0,1:T(8,128)(2,1)S(1)} %copy.31), channel_id=1, replica_groups=mesh['row'=8,'chip'=8,'core'=2] {'row'}, dimensions={1} | all-to-all | bytes 1048576 | tf_op jit(solution)/shard_map/all_to_all | solution.py:48
  193.5 4.7 %copy_select_fusion = bf16[8,16,32,512]{3,2,0,1:T(8,128)(2,1)} fusion(bf16[8,16,32,512]{3,2,1,0:T(8,128)(2,1)} %bitcast.69, pred[8]{0:T(512)(128)(4,1)S(1)} %compare_and_fusion.1), kind=kLoop, calls=%fused_computation.3 | loop fusion | flops 2097152 | bytes 8388616 | tf_op jit(solution)/shard_map/jit(_take)/select_n | solution.py:55
  198.2 32.6 %reduce-scatter.2.cloned.1.call-done = bf16[512,1,256]{2,0,1:T(8,128)(2,1)} async-done(((bf16[512,8,256]{2,0,1:T(8,128)(2,1)}), bf16[512,1,256]{2,0,1:T(8,128)(2,1)}) %reduce-scatter.2.cloned.1.call-update) | async-done | bytes 262160 | tf_op jit(solution)/shard_map/reduce_scatter | solution.py:63
  230.7 1.8 bitcast_add_fusion
  233.5 11.1 %convolution_convert_fusion = bf16[512,512]{1,0:T(8,128)(2,1)} fusion(bf16[512,8192]{0,1:T(8,128)(2,1)} %all-gather.5.cloned.1.call-done, bf16[512,8192]{1,0:T(8,128)(2,1)} %param.11), kind=kOutput, calls=%fused_computation.14 | convolution fusion | flops 4295229440 | bytes 17301504 | tf_op jit(solution)/shard_map/dot_general | solution.py:78
  244.6 42.5 %all-gather.3.cloned.1.call-done = bf16[4096,1024]{1,0:T(8,128)(2,1)} async-done(((bf16[256,1024]{1,0:T(8,128)(2,1)}), bf16[4096,1024]{1,0:T(8,128)(2,1)}) %all-gather.3.cloned.1.call-update) | async-done | bytes 8388624 | tf_op jit(solution)/shard_map/all_gather | solution.py:49
  287.1 10.5 %multiply_add_fusion = f32[512,1024]{1,0:T(8,128)} fusion(f32[512,1024]{1,0:T(8,128)S(1)} %copy-done.3, bf16[4096,512]{1,0:T(8,128)(2,1)} %bitcast.72, bf16[4096,1024]{1,0:T(8,128)(2,1)} %all-gather.3.cloned.1.call-done), kind=kOutput, calls=%fused_computation.10 | convolution fusion | flops 4296540160 | bytes 16777216 | tf_op jit(solution)/shard_map/dot_general | solution.py:71
  (48 shorter events, 13.6 us)
Async XLA Ops:
  33.0 23.7 %all-to-all-start = ((bf16[64,16,512]{2,0,1:T(8,128)(2,1)}), bf16[64,16,512]{2,0,1:T(8,128)(2,1)S(1)}, u32[]{:S(2)}, u32[]{:S(2)}) async-start(bf16[64,16,512]{2,0,1:T(8,128)(2,1)} %copy.27), calls=%async_computation | async-start | bytes 2097152 | tf_op jit(solution)/shard_map/all_to_all | solution.py:44
  40.9 189.9 %reduce-scatter.2.cloned.1.call-start = ((), (), s32[]{:S(2)}) async-start(), calls=%async_computation.4 | async-start | bytes 2359296 | tf_op jit(solution)/shard_map/reduce_scatter | solution.py:63
  58.8 16.2 %collective-permute-start = (bf16[512,512]{1,0:T(8,128)(2,1)S(1)}, bf16[512,512]{1,0:T(8,128)(2,1)S(1)}, u32[]{:S(2)}, u32[]{:S(2)}) collective-permute-start(bf16[512,512]{1,0:T(8,128)(2,1)S(1)} %broadcast_select_fusion), channel_id=1, source_target_pairs={{0,16},{16,32},{32,48},{48,64},{64,80},{80,96},{96,112},{112,0},{1... | collective-permute-start | bytes 1572872 | tf_op jit(solution)/shard_map/ppermute | solution.py:51
  61.5 23.7 %collective-permute-start.1 = (bf16[512,512]{1,0:T(8,128)(2,1)S(1)}, bf16[512,512]{1,0:T(8,128)(2,1)S(1)}, u32[]{:S(2)}, u32[]{:S(2)}) collective-permute-start(bf16[512,512]{1,0:T(8,128)(2,1)S(1)} %broadcast_select_fusion), channel_id=1, source_target_pairs={{0,32},{16,48},{32,64},{48,80},{64,96},{80,112},{96,0},{112,16},{1... | collective-permute-start | bytes 1572872 | tf_op jit(solution)/shard_map/ppermute | solution.py:51
  62.8 48.5 %collective-permute-start.2 = (bf16[512,512]{1,0:T(8,128)(2,1)S(1)}, bf16[512,512]{1,0:T(8,128)(2,1)S(1)}, u32[]{:S(2)}, u32[]{:S(2)}) collective-permute-start(bf16[512,512]{1,0:T(8,128)(2,1)S(1)} %broadcast_select_fusion), channel_id=1, source_target_pairs={{0,48},{16,64},{32,80},{48,96},{64,112},{80,0},{96,16},{112,32},{1... | collective-permute-start | bytes 1572872 | tf_op jit(solution)/shard_map/ppermute | solution.py:51
  65.8 46.3 %collective-permute-start.3 = (bf16[512,512]{1,0:T(8,128)(2,1)S(1)}, bf16[512,512]{1,0:T(8,128)(2,1)S(1)}, u32[]{:S(2)}, u32[]{:S(2)}) collective-permute-start(bf16[512,512]{1,0:T(8,128)(2,1)S(1)} %broadcast_select_fusion), channel_id=1, source_target_pairs={{0,64},{16,80},{32,96},{48,112},{64,0},{80,16},{96,32},{112,48},{1... | collective-permute-start | bytes 1572872 | tf_op jit(solution)/shard_map/ppermute | solution.py:51
  67.5 49.8 %collective-permute-start.4 = (bf16[512,512]{1,0:T(8,128)(2,1)S(1)}, bf16[512,512]{1,0:T(8,128)(2,1)S(1)}, u32[]{:S(2)}, u32[]{:S(2)}) collective-permute-start(bf16[512,512]{1,0:T(8,128)(2,1)S(1)} %broadcast_select_fusion), channel_id=1, source_target_pairs={{0,80},{16,96},{32,112},{48,0},{64,16},{80,32},{96,48},{112,64},{1... | collective-permute-start | bytes 1572872 | tf_op jit(solution)/shard_map/ppermute | solution.py:51
  75.1 43.1 %collective-permute-start.5 = (bf16[512,512]{1,0:T(8,128)(2,1)S(1)}, bf16[512,512]{1,0:T(8,128)(2,1)S(1)}, u32[]{:S(2)}, u32[]{:S(2)}) collective-permute-start(bf16[512,512]{1,0:T(8,128)(2,1)S(1)} %broadcast_select_fusion), channel_id=1, source_target_pairs={{0,96},{16,112},{32,0},{48,16},{64,32},{80,48},{96,64},{112,80},{1... | collective-permute-start | bytes 1572872 | tf_op jit(solution)/shard_map/ppermute | solution.py:51
  85.2 40.2 %collective-permute-start.6 = (bf16[512,512]{1,0:T(8,128)(2,1)S(1)}, bf16[512,512]{1,0:T(8,128)(2,1)S(1)}, u32[]{:S(2)}, u32[]{:S(2)}) collective-permute-start(bf16[512,512]{1,0:T(8,128)(2,1)S(1)} %broadcast_select_fusion), channel_id=1, source_target_pairs={{0,112},{16,0},{32,16},{48,32},{64,48},{80,64},{96,80},{112,96},{1... | collective-permute-start | bytes 1572872 | tf_op jit(solution)/shard_map/ppermute | solution.py:51
  133.8 1.9 copy-start
  138.3 6.0 %collective-permute-start.7 = (bf16[512,8,256]{2,0,1:T(8,128)(2,1)}, bf16[512,8,256]{2,0,1:T(8,128)(2,1)}, u32[]{:S(2)}, u32[]{:S(2)}) collective-permute-start(bf16[512,8,256]{2,0,1:T(8,128)(2,1)} %fusion.8), channel_id=1, source_target_pairs={{0,1},{1,0},{2,3},{3,2},{4,5},{5,4},{6,7},{7,6},{8,9},{9,8},{10,11... | collective-permute-start | bytes 6291464 | tf_op jit(solution)/shard_map/ppermute | solution.py:28
  149.1 84.3 %all-gather.5.cloned.1.call-start = ((), (), s32[]{:S(2)}) async-start(), calls=%async_computation.6 | async-start | bytes 8912896 | tf_op jit(solution)/shard_map/all_gather | solution.py:79
  149.3 3.5 %copy-start.2 = (bf16[512,4096]{1,0:T(8,128)(2,1)S(1)}, bf16[512,4096]{1,0:T(8,128)(2,1)}, u32[]{:S(2)}) copy-start(bf16[512,4096]{1,0:T(8,128)(2,1)} %param.10) | copy-start | bytes 12582916
  155.9 131.2 %all-gather.3.cloned.1.call-start = ((), (), s32[]{:S(2)}) async-start(), calls=%async_computation.5 | async-start | bytes 8912896 | tf_op jit(solution)/shard_map/all_gather | solution.py:49
  193.5 37.2 %copy-start.1 = (f32[512,256]{1,0:T(8,128)S(1)}, f32[512,256]{1,0:T(8,128)}, u32[]{:S(2)}) copy-start(f32[512,256]{1,0:T(8,128)} %param.8) | copy-start | bytes 1572868
  232.6 54.5 %copy-start.3 = (f32[512,1024]{1,0:T(8,128)S(1)}, f32[512,1024]{1,0:T(8,128)}, u32[]{:S(2)}) copy-start(f32[512,1024]{1,0:T(8,128)} %param.9) | copy-start | bytes 6291460
Sparse Core Ops, SparseCore 0:
  149.3 81.4 reduce-scatter.1
Sparse Core Ops, SparseCore 1:
  156.0 77.4 all-gather.4
  235.0 52.0 all-gather.2
where the time goes:
time: 305 us
  waiting for transfers between devices  124 us (41%)
  starting transfers between devices  41 us (13%)
  other arithmetic  37 us (12%)
  blocking collectives  36.4 us (12%)
  matrix products  32.2 us (11%)
  local copies, waits for them, and re-layouts  19.3 us (6%)
  between operations  15.6 us (5%)
    all_gather x1, waiting for transfers between devices, shards(): row_block = lax.all_gather(block_piece, COL, axis=0, tiled=True)  42.5 us
    reduce_scatter x1, waiting for transfers between devices, shards(): lax.psum_scatter(chip_sum.astype(jnp.bfloat16), 'chip', scatter_dimension...  32.6 us
    ppermute x7, starting transfers between devices, shards(): lax.ppermute(grad_tile, 'row', [(i, (i + s) % row_count) for i in range(r...  31.2 us
    ppermute x7, waiting for transfers between devices, shards(): lax.ppermute(grad_tile, 'row', [(i, (i + s) % row_count) for i in range(r...  29.3 us
    unnamed x2, other arithmetic  23.7 us
    all_to_all x1, blocking collectives, shards(): lax.all_to_all(grad_tile, COL, split_axis=0, concat_axis=1, tiled=True)  20.9 us
    all_to_all x1, blocking collectives, shards(): lax.all_to_all(row_slice, 'row', split_axis=1, concat_axis=0, tiled=True)  15.5 us
    all_to_all x1, waiting for transfers between devices, shards(): lax.all_to_all(held_rows, COL, split_axis=1, concat_axis=0, tiled=True)  14 us
  transfers between devices with their start and end apart: 12, of which 9 were waited for; matrix products, arithmetic and copies ran while one was open for 11% of the time, Pallas kernels for 0%

commit v1 on v0

--- a/solution.py
+++ b/solution.py
@@ -46,7 +46,6 @@
     grad_tile = jnp.take(received, slot_index(row_counts, tile_rows, capacity), axis=0)
     row_slice = lax.all_to_all(grad_tile, COL, split_axis=0, concat_axis=1, tiled=True)
     block_piece = lax.all_to_all(row_slice, "row", split_axis=1, concat_axis=0, tiled=True)
-    row_block = lax.all_gather(block_piece, COL, axis=0, tiled=True)
     shifted_tiles = [grad_tile] + [
         lax.ppermute(grad_tile, "row", [(i, (i + s) % row_count) for i in range(row_count)])
         for s in range(1, row_count)
@@ -68,15 +67,22 @@
         .transpose(1, 0, 2, 3)
         .reshape(HQ, tile_cols)
     )
+    left_mixed = jnp.dot(left_root, column_panel, preferred_element_type=jnp.float32).astype(
+        jnp.bfloat16
+    )
+    gathered = lax.all_gather(
+        jnp.stack([block_piece, left_mixed.reshape(block_piece.shape)]), COL, axis=0, tiled=False
+    )
+    row_block = gathered[:, 0].reshape(HQ, block_cols)
+    mixed_rows = (
+        gathered[:, 1].reshape(col_count, tile_rows, tile_cols).transpose(1, 0, 2).reshape(tile_rows, DIN)
+    )
     right_gram = lax.dot_general(
         panel_reordered, row_block, (((0,), (0,)), ((), ())), preferred_element_type=jnp.float32
     )
     right_new = stat_decay * right_stat + right_gram * (1.0 / math.sqrt(HQ))
-    left_mixed = jnp.dot(left_root, column_panel, preferred_element_type=jnp.float32).astype(
-        jnp.bfloat16
-    )
     update_sum = lax.dot_general(
-        lax.all_gather(left_mixed, COL, axis=1, tiled=True),
+        mixed_rows,
         right_root,
         (((1,), (1,)), ((), ())),
         preferred_element_type=jnp.float32,

time: 305 us -> 344 us (1.13)
  local copies, waits for them, and re-layouts: 19.3 us -> 57.4 us
  blocking collectives: 36.4 us -> 0 us
  waiting for transfers between devices: 124 us -> 147 us
  starting transfers between devices: 41 us -> 52.8 us
    all_gather x2 -> x1, waiting for transfers between devices: 43.4 us -> 80.1 us  [shards(): lax.all_gather(jnp.stack([block_piece, left_mixed.reshape(block_piece.sha...]
    all_to_all x2 -> x0, blocking collectives: 36.4 us -> none  [the longest x1 20.9 us: shards(): lax.all_to_all(grad_tile, COL, split_axis=0, concat_axis=1, tiled=True)]
    reduce_scatter x1, waiting for transfers between devices: 32.6 us -> 4.63 us  [shards(): lax.psum_scatter(chip_sum.astype(jnp.bfloat16), 'chip', scatter_dimension...]
    all_to_all x0 -> x2, waiting for transfers between devices: none -> 15 us  [the longest x1 12.8 us: shards(): lax.all_to_all(grad_tile, COL, split_axis=0, concat_axis=1, tiled=True)]
    another operation x0 -> x2, local copies, waits for them, and re-layouts: none -> 13.1 us  [the longest x1 13 us: shards(): gathered[:, 1].reshape(col_count, tile_rows, tile_cols).transpose(1, 0, 2)]
    transpose x0 -> x1, local copies, waits for them, and re-layouts: none -> 12.3 us  [shards(): gathered[:, 1].reshape(col_count, tile_rows, tile_cols).transpose(1, 0, 2)]
    all_to_all x0 -> x2, starting transfers between devices: none -> 11.9 us  [the longest x1 6.46 us: shards(): lax.all_to_all(row_slice, 'row', split_axis=1, concat_axis=0, tiled=True)]
    unnamed x16 -> x19, local copies, waits for them, and re-layouts: 7.72 us -> 19.5 us
  transfers between devices with their start and end apart: 12 -> 13, of which waited for: 9 -> 10; matrix products, arithmetic and copies ran while one was open for 11% -> 7% of each run, Pallas kernels for 0% -> 0%
where the time goes in v1:
time: 344 us; the launch traced here: 342 us
  waiting for transfers between devices  147 us (43%)
  local copies, waits for them, and re-layouts  57.4 us (17%)
  starting transfers between devices  52.8 us (15%)
  other arithmetic  39 us (11%)
  matrix products  30.3 us (9%)
  between operations  15.6 us (5%)
    all_gather x1, waiting for transfers between devices, shards(): lax.all_gather(jnp.stack([block_piece, left_mixed.reshape(block_piece.sha...  80.1 us
    ppermute x7, starting transfers between devices, shards(): lax.ppermute(grad_tile, 'row', [(i, (i + s) % row_count) for i in range(r...  31.2 us
    ppermute x7, waiting for transfers between devices, shards(): lax.ppermute(grad_tile, 'row', [(i, (i + s) % row_count) for i in range(r...  29.3 us
    unnamed x2, other arithmetic  23.8 us
    unnamed x19, local copies, waits for them, and re-layouts  19.5 us
    all_to_all x1, waiting for transfers between devices, shards(): lax.all_to_all(held_rows, COL, split_axis=1, concat_axis=0, tiled=True)  14 us
    another operation x1, local copies, waits for them, and re-layouts, shards(): gathered[:, 1].reshape(col_count, tile_rows, tile_cols).transpose(1, 0, 2)  13 us
    all_to_all x1, waiting for transfers between devices, shards(): lax.all_to_all(grad_tile, COL, split_axis=0, concat_axis=1, tiled=True)  12.8 us
  transfers between devices with their start and end apart: 13, of which 10 were waited for; matrix products, arithmetic and copies ran while one was open for 7% of the time, Pallas kernels for 0%

profile of v1, /device:TPU:1, one launch (start us, length us, event | category | flops | bytes accessed | tf_op | source)
XLA Modules:
  0.0 342.5 jit_solution(4792129335040408156)
XLA Ops:
  8.0 22.8 %reduce = bf16[524288]{0:T(1024)(128)(2,1)S(1)} reduce(bf16[1,1,524288]{2,1,0:T(2,128)(2,1)} %param.6, bf16[]{:T(256)} %constant.90), dimensions={0,1}, to_apply=%param.6.reduce_sub_computation | reduce | bytes 2097154 | tf_op args[0]
  33.0 7.8 %all-to-all-start = ((bf16[64,16,512]{2,0,1:T(8,128)(2,1)}), bf16[64,16,512]{2,0,1:T(8,128)(2,1)S(1)}, u32[]{:S(2)}, u32[]{:S(2)}) async-start(bf16[64,16,512]{2,0,1:T(8,128)(2,1)} %copy.34), calls=%async_computation | async-start | bytes 2097152 | tf_op jit(solution)/shard_map/all_to_all | solution.py:44
  42.6 14.0 %all-to-all-done = bf16[64,16,512]{2,0,1:T(8,128)(2,1)S(1)} async-done(((bf16[64,16,512]{2,0,1:T(8,128)(2,1)}), bf16[64,16,512]{2,0,1:T(8,128)(2,1)S(1)}, u32[]{:S(2)}, u32[]{:S(2)}) %all-to-all-start) | async-done | bytes 1048608 | tf_op jit(solution)/shard_map/all_to_all | solution.py:44
  56.7 2.0 gather_fusion
  58.8 2.7 collective-permute-start
  62.8 2.0 collective-permute-start.2
  67.5 4.2 %collective-permute-start.4 = (bf16[512,512]{1,0:T(8,128)(2,1)S(1)}, bf16[512,512]{1,0:T(8,128)(2,1)S(1)}, u32[]{:S(2)}, u32[]{:S(2)}) collective-permute-start(bf16[512,512]{1,0:T(8,128)(2,1)S(1)} %broadcast_select_fusion), channel_id=1, source_target_pairs={{0,80},{16,96},{32,112},{48,0},{64,16},{80,32},{96,48},{112,64},{1... | collective-permute-start | bytes 1572872 | tf_op jit(solution)/shard_map/ppermute | solution.py:50
  71.7 3.4 collective-permute-done
  75.1 9.3 %collective-permute-start.5 = (bf16[512,512]{1,0:T(8,128)(2,1)S(1)}, bf16[512,512]{1,0:T(8,128)(2,1)S(1)}, u32[]{:S(2)}, u32[]{:S(2)}) collective-permute-start(bf16[512,512]{1,0:T(8,128)(2,1)S(1)} %broadcast_select_fusion), channel_id=1, source_target_pairs={{0,96},{16,112},{32,0},{48,16},{64,32},{80,48},{96,64},{112,80},{1... | collective-permute-start | bytes 1572872 | tf_op jit(solution)/shard_map/ppermute | solution.py:50
  85.2 10.0 %collective-permute-start.6 = (bf16[512,512]{1,0:T(8,128)(2,1)S(1)}, bf16[512,512]{1,0:T(8,128)(2,1)S(1)}, u32[]{:S(2)}, u32[]{:S(2)}) collective-permute-start(bf16[512,512]{1,0:T(8,128)(2,1)S(1)} %broadcast_select_fusion), channel_id=1, source_target_pairs={{0,112},{16,0},{32,16},{48,32},{64,48},{80,64},{96,80},{112,96},{1... | collective-permute-start | bytes 1572872 | tf_op jit(solution)/shard_map/ppermute | solution.py:50
  96.1 15.2 %collective-permute-done.2 = bf16[512,512]{1,0:T(8,128)(2,1)S(1)} collective-permute-done((bf16[512,512]{1,0:T(8,128)(2,1)S(1)}, bf16[512,512]{1,0:T(8,128)(2,1)S(1)}, u32[]{:S(2)}, u32[]{:S(2)}) %collective-permute-start.2) | collective-permute-done | bytes 524320 | tf_op jit(solution)/shard_map/ppermute | solution.py:50
  113.0 4.3 %collective-permute-done.4 = bf16[512,512]{1,0:T(8,128)(2,1)S(1)} collective-permute-done((bf16[512,512]{1,0:T(8,128)(2,1)S(1)}, bf16[512,512]{1,0:T(8,128)(2,1)S(1)}, u32[]{:S(2)}, u32[]{:S(2)}) %collective-permute-start.4) | collective-permute-done | bytes 524320 | tf_op jit(solution)/shard_map/ppermute | solution.py:50
  119.0 6.4 %collective-permute-done.6 = bf16[512,512]{1,0:T(8,128)(2,1)S(1)} collective-permute-done((bf16[512,512]{1,0:T(8,128)(2,1)S(1)}, bf16[512,512]{1,0:T(8,128)(2,1)S(1)}, u32[]{:S(2)}, u32[]{:S(2)}) %collective-permute-start.6) | collective-permute-done | bytes 524320 | tf_op jit(solution)/shard_map/ppermute | solution.py:50
  126.1 4.9 %gather_fusion.1 = bf16[8,512,512]{2,1,0:T(8,128)(2,1)} fusion(bf16[8,512,512]{2,1,0:T(8,128)(2,1)} %bitcast_dynamic-update-slice_fusion, s32[1024]{0:T(1024)S(1)} %pad_clamp_fusion), kind=kCustom, calls=%fused_computation.1 | custom fusion | bytes 8388640 | tf_op jit(solution)/shard_map/jit(_take)/gather | solution.py:54
  131.1 2.7 copy_select_fusion.1
  135.7 2.6 fusion.8
  140.2 4.1 %collective-permute-done.7 = bf16[512,8,256]{2,0,1:T(8,128)(2,1)} collective-permute-done((bf16[512,8,256]{2,0,1:T(8,128)(2,1)}, bf16[512,8,256]{2,0,1:T(8,128)(2,1)}, u32[]{:S(2)}, u32[]{:S(2)}) %collective-permute-start.7) | collective-permute-done | bytes 2097184 | tf_op jit(solution)/shard_map/ppermute | solution.py:28
  144.3 4.8 %add_convert_fusion = bf16[512,8,256]{2,0,1:T(8,128)(2,1)} fusion(bf16[512,8,256]{2,0,1:T(8,128)(2,1)} %collective-permute-done.7, bf16[8,2,256,512]{3,2,0,1:T(8,128)(2,1)} %copy-done.1, s32[]{:T(128)S(6)} %select_n.106, bf16[512,512]{1,0:T(8,128)(2,1)S(1)} %broadcast_select_fusion), kind=kOutput, calls=%fused_computation.6 | convolution fusion | flops 1076887552 | bytes 6815748 | tf_op jit(solution)/shard_map/dot_general | solution.py:59
  150.2 5.4 %all-to-all-start.1 = ((bf16[16,32,512]{2,1,0:T(8,128)(2,1)}), bf16[16,32,512]{2,1,0:T(8,128)(2,1)S(1)}, u32[]{:S(2)}, u32[]{:S(2)}) async-start(bf16[16,32,512]{2,1,0:T(8,128)(2,1)} %broadcast_select_fusion.1), calls=%async_computation.2 | async-start | bytes 1048576 | tf_op jit(solution)/shard_map/all_to_all | solution.py:47
  155.8 12.8 %all-to-all-done.1 = bf16[16,32,512]{2,1,0:T(8,128)(2,1)S(1)} async-done(((bf16[16,32,512]{2,1,0:T(8,128)(2,1)}), bf16[16,32,512]{2,1,0:T(8,128)(2,1)S(1)}, u32[]{:S(2)}, u32[]{:S(2)}) %all-to-all-start.1) | async-done | bytes 524320 | tf_op jit(solution)/shard_map/all_to_all | solution.py:47
  170.1 6.5 %all-to-all-start.2 = ((bf16[32,8,1024]{2,0,1:T(8,128)(2,1)}), bf16[32,8,1024]{2,0,1:T(8,128)(2,1)S(1)}, u32[]{:S(2)}, u32[]{:S(2)}) async-start(bf16[32,8,1024]{2,0,1:T(8,128)(2,1)} %copy.38), calls=%async_computation.3 | async-start | bytes 1048576 | tf_op jit(solution)/shard_map/all_to_all | solution.py:48
  176.6 2.8 bitcast_select_fusion
  180.1 2.4 fusion.11
  182.9 2.3 all-to-all-done.2
  186.3 4.8 %copy_select_fusion = bf16[8,16,32,512]{3,2,0,1:T(8,128)(2,1)} fusion(bf16[8,16,32,512]{3,2,1,0:T(8,128)(2,1)} %bitcast.79, pred[8]{0:T(512)(128)(4,1)S(1)} %compare_and_fusion.1), kind=kLoop, calls=%fused_computation.4 | loop fusion | flops 2097152 | bytes 8388616 | tf_op jit(solution)/shard_map/jit(_take)/select_n | solution.py:54
  191.1 4.6 %reduce-scatter.2.cloned.1.call-done = bf16[512,1,256]{2,0,1:T(8,128)(2,1)} async-done(((bf16[512,8,256]{2,0,1:T(8,128)(2,1)}), bf16[512,1,256]{2,0,1:T(8,128)(2,1)}) %reduce-scatter.2.cloned.1.call-update) | async-done | bytes 262160 | tf_op jit(solution)/shard_map/reduce_scatter | solution.py:62
  197.5 80.1 %all-gather.3.cloned.1.call-done = bf16[32,256,1024]{2,1,0:T(8,128)(2,1)} async-done(((bf16[2,256,1024]{2,1,0:T(8,128)(2,1)}), bf16[32,256,1024]{2,1,0:T(8,128)(2,1)}) %all-gather.3.cloned.1.call-update) | async-done | bytes 16777232 | tf_op jit(solution)/shard_map/all_gather | solution.py:73
  277.7 11.6 %slice_bitcast_fusion = (bf16[16,1,256,1024]{3,2,0,1:T(8,128)(2,1)}, bf16[16,1,256,1024]{3,2,1,0:T(8,128)(2,1)}) fusion(bf16[16,2,256,1024]{3,2,1,0:T(8,128)(2,1)} %bitcast.82), kind=kLoop, calls=%fused_computation.2 | loop fusion | bytes 33554432
  289.3 13.0 %reshape_squeeze.7 = bf16[16,512,512]{2,1,0:T(8,128)(2,1)} reshape(bf16[16,1,256,1024]{3,2,0,1:T(8,128)(2,1)} %get-tuple-element.5) | data formatting | bytes 16777216 | tf_op jit(solution)/shard_map/reshape;squeeze | solution.py:78
  302.3 12.3 %copy.41 = bf16[512,16,512]{0,2,1:T(8,128)(2,1)} copy(bf16[512,16,512]{2,0,1:T(8,128)(2,1)} %bitcast.80) | data formatting | bytes 16777216 | tf_op jit(solution)/shard_map/transpose | solution.py:78
  314.6 11.3 %convolution_convert_fusion = bf16[512,512]{1,0:T(8,128)(2,1)} fusion(bf16[512,8192]{0,1:T(8,128)(2,1)} %bitcast.83, bf16[512,8192]{1,0:T(8,128)(2,1)} %param.11), kind=kOutput, calls=%fused_computation.15 | convolution fusion | flops 4295229440 | bytes 17301504 | tf_op jit(solution)/shard_map/dot_general | solution.py:84
  325.8 9.2 %multiply_add_fusion = f32[512,1024]{1,0:T(8,128)} fusion(f32[512,1024]{1,0:T(8,128)S(1)} %copy-done.4, bf16[4096,512]{1,0:T(8,128)(2,1)S(1)} %bitcast.86, bf16[4096,1024]{1,0:T(8,128)(2,1)} %bitcast.85), kind=kOutput, calls=%fused_computation.11 | convolution fusion | flops 4296540160 | bytes 16777216 | tf_op jit(solution)/shard_map/dot_general | solution.py:80
  (55 shorter events, 24.6 us)
Async XLA Ops:
  33.0 23.7 %all-to-all-start = ((bf16[64,16,512]{2,0,1:T(8,128)(2,1)}), bf16[64,16,512]{2,0,1:T(8,128)(2,1)S(1)}, u32[]{:S(2)}, u32[]{:S(2)}) async-start(bf16[64,16,512]{2,0,1:T(8,128)(2,1)} %copy.34), calls=%async_computation | async-start | bytes 2097152 | tf_op jit(solution)/shard_map/all_to_all | solution.py:44
  40.9 154.9 %reduce-scatter.2.cloned.1.call-start = ((), (), s32[]{:S(2)}) async-start(), calls=%async_computation.4 | async-start | bytes 2359296 | tf_op jit(solution)/shard_map/reduce_scatter | solution.py:62
  58.8 16.2 %collective-permute-start = (bf16[512,512]{1,0:T(8,128)(2,1)S(1)}, bf16[512,512]{1,0:T(8,128)(2,1)S(1)}, u32[]{:S(2)}, u32[]{:S(2)}) collective-permute-start(bf16[512,512]{1,0:T(8,128)(2,1)S(1)} %broadcast_select_fusion), channel_id=1, source_target_pairs={{0,16},{16,32},{32,48},{48,64},{64,80},{80,96},{96,112},{112,0},{1... | collective-permute-start | bytes 1572872 | tf_op jit(solution)/shard_map/ppermute | solution.py:50
  61.5 23.7 %collective-permute-start.1 = (bf16[512,512]{1,0:T(8,128)(2,1)S(1)}, bf16[512,512]{1,0:T(8,128)(2,1)S(1)}, u32[]{:S(2)}, u32[]{:S(2)}) collective-permute-start(bf16[512,512]{1,0:T(8,128)(2,1)S(1)} %broadcast_select_fusion), channel_id=1, source_target_pairs={{0,32},{16,48},{32,64},{48,80},{64,96},{80,112},{96,0},{112,16},{1... | collective-permute-start | bytes 1572872 | tf_op jit(solution)/shard_map/ppermute | solution.py:50
  62.8 48.5 %collective-permute-start.2 = (bf16[512,512]{1,0:T(8,128)(2,1)S(1)}, bf16[512,512]{1,0:T(8,128)(2,1)S(1)}, u32[]{:S(2)}, u32[]{:S(2)}) collective-permute-start(bf16[512,512]{1,0:T(8,128)(2,1)S(1)} %broadcast_select_fusion), channel_id=1, source_target_pairs={{0,48},{16,64},{32,80},{48,96},{64,112},{80,0},{96,16},{112,32},{1... | collective-permute-start | bytes 1572872 | tf_op jit(solution)/shard_map/ppermute | solution.py:50
  65.8 46.4 %collective-permute-start.3 = (bf16[512,512]{1,0:T(8,128)(2,1)S(1)}, bf16[512,512]{1,0:T(8,128)(2,1)S(1)}, u32[]{:S(2)}, u32[]{:S(2)}) collective-permute-start(bf16[512,512]{1,0:T(8,128)(2,1)S(1)} %broadcast_select_fusion), channel_id=1, source_target_pairs={{0,64},{16,80},{32,96},{48,112},{64,0},{80,16},{96,32},{112,48},{1... | collective-permute-start | bytes 1572872 | tf_op jit(solution)/shard_map/ppermute | solution.py:50
  67.5 49.8 %collective-permute-start.4 = (bf16[512,512]{1,0:T(8,128)(2,1)S(1)}, bf16[512,512]{1,0:T(8,128)(2,1)S(1)}, u32[]{:S(2)}, u32[]{:S(2)}) collective-permute-start(bf16[512,512]{1,0:T(8,128)(2,1)S(1)} %broadcast_select_fusion), channel_id=1, source_target_pairs={{0,80},{16,96},{32,112},{48,0},{64,16},{80,32},{96,48},{112,64},{1... | collective-permute-start | bytes 1572872 | tf_op jit(solution)/shard_map/ppermute | solution.py:50
  75.1 43.1 %collective-permute-start.5 = (bf16[512,512]{1,0:T(8,128)(2,1)S(1)}, bf16[512,512]{1,0:T(8,128)(2,1)S(1)}, u32[]{:S(2)}, u32[]{:S(2)}) collective-permute-start(bf16[512,512]{1,0:T(8,128)(2,1)S(1)} %broadcast_select_fusion), channel_id=1, source_target_pairs={{0,96},{16,112},{32,0},{48,16},{64,32},{80,48},{96,64},{112,80},{1... | collective-permute-start | bytes 1572872 | tf_op jit(solution)/shard_map/ppermute | solution.py:50
  85.2 40.1 %collective-permute-start.6 = (bf16[512,512]{1,0:T(8,128)(2,1)S(1)}, bf16[512,512]{1,0:T(8,128)(2,1)S(1)}, u32[]{:S(2)}, u32[]{:S(2)}) collective-permute-start(bf16[512,512]{1,0:T(8,128)(2,1)S(1)} %broadcast_select_fusion), channel_id=1, source_target_pairs={{0,112},{16,0},{32,16},{48,32},{64,48},{80,64},{96,80},{112,96},{1... | collective-permute-start | bytes 1572872 | tf_op jit(solution)/shard_map/ppermute | solution.py:50
  133.7 2.0 copy-start.1
  138.3 6.0 %collective-permute-start.7 = (bf16[512,8,256]{2,0,1:T(8,128)(2,1)}, bf16[512,8,256]{2,0,1:T(8,128)(2,1)}, u32[]{:S(2)}, u32[]{:S(2)}) collective-permute-start(bf16[512,8,256]{2,0,1:T(8,128)(2,1)} %fusion.8), channel_id=1, source_target_pairs={{0,1},{1,0},{2,3},{3,2},{4,5},{5,4},{6,7},{7,6},{8,9},{9,8},{10,11... | collective-permute-start | bytes 6291464 | tf_op jit(solution)/shard_map/ppermute | solution.py:28
  150.2 18.3 %all-to-all-start.1 = ((bf16[16,32,512]{2,1,0:T(8,128)(2,1)}), bf16[16,32,512]{2,1,0:T(8,128)(2,1)S(1)}, u32[]{:S(2)}, u32[]{:S(2)}) async-start(bf16[16,32,512]{2,1,0:T(8,128)(2,1)} %broadcast_select_fusion.1), calls=%async_computation.2 | async-start | bytes 1048576 | tf_op jit(solution)/shard_map/all_to_all | solution.py:47
  170.1 15.1 %all-to-all-start.2 = ((bf16[32,8,1024]{2,0,1:T(8,128)(2,1)}), bf16[32,8,1024]{2,0,1:T(8,128)(2,1)S(1)}, u32[]{:S(2)}, u32[]{:S(2)}) async-start(bf16[32,8,1024]{2,0,1:T(8,128)(2,1)} %copy.38), calls=%async_computation.3 | async-start | bytes 1048576 | tf_op jit(solution)/shard_map/all_to_all | solution.py:48
  176.5 101.1 %all-gather.3.cloned.1.call-start = ((), (), s32[]{:S(2)}) async-start(), calls=%async_computation.5 | async-start | bytes 17825792 | tf_op jit(solution)/shard_map/all_gather | solution.py:73
  176.6 3.5 %copy-start.3 = (bf16[512,4096]{1,0:T(8,128)(2,1)S(1)}, bf16[512,4096]{1,0:T(8,128)(2,1)}, u32[]{:S(2)}) copy-start(bf16[512,4096]{1,0:T(8,128)(2,1)} %param.10) | copy-start | bytes 12582916
  186.3 9.4 %copy-start.2 = (f32[512,256]{1,0:T(8,128)S(1)}, f32[512,256]{1,0:T(8,128)}, u32[]{:S(2)}) copy-start(f32[512,256]{1,0:T(8,128)} %param.8) | copy-start | bytes 1572868
  314.6 11.3 %copy-start = (bf16[8,16,32,512]{3,2,0,1:T(8,128)(2,1)S(1)}, bf16[8,16,32,512]{3,2,0,1:T(8,128)(2,1)}, u32[]{:S(2)}) copy-start(bf16[8,16,32,512]{3,2,0,1:T(8,128)(2,1)} %copy_select_fusion) | copy-start | bytes 12582916
  314.6 11.3 %copy-start.4 = (f32[512,1024]{1,0:T(8,128)S(1)}, f32[512,1024]{1,0:T(8,128)}, u32[]{:S(2)}) copy-start(f32[512,1024]{1,0:T(8,128)} %param.9) | copy-start | bytes 6291460
Sparse Core Ops, SparseCore 0:
  149.3 46.4 reduce-scatter.1
Sparse Core Ops, SparseCore 1:
  186.4 91.3 all-gather.2

commit v2 on v0

--- a/solution.py
+++ b/solution.py
@@ -44,15 +44,33 @@
     received = lax.all_to_all(held_rows, COL, split_axis=1, concat_axis=0, tiled=True)
     row_counts = lax.dynamic_index_in_dim(range_rows, row_index, 0, keepdims=False)
     grad_tile = jnp.take(received, slot_index(row_counts, tile_rows, capacity), axis=0)
-    row_slice = lax.all_to_all(grad_tile, COL, split_axis=0, concat_axis=1, tiled=True)
-    block_piece = lax.all_to_all(row_slice, "row", split_axis=1, concat_axis=0, tiled=True)
+    col_index = lax.axis_index(COL)
+    device_count = row_count * col_count
+    pieces = []
+    for k in range(col_count):
+        target_col = (col_index + k + 2 * row_index) % col_count
+        piece = lax.dynamic_slice_in_dim(grad_tile, target_col * slice_rows, slice_rows, 0)
+        route = []
+        for source in range(device_count):
+            r, c = divmod(source, col_count)
+            route.append((source, (c // 2) * col_count + (c + k + 2 * r) % col_count))
+        pieces.append(lax.ppermute(piece, ("row", "chip", "core"), route))
+    source_rows = jnp.arange(row_count, dtype=jnp.int32)[:, None]
+    halves = jnp.arange(2, dtype=jnp.int32)[None, :]
+    arrival = (col_index - 2 * row_index - halves - 2 * source_rows) % col_count
+    block_piece = (
+        jnp.take(jnp.stack(pieces), arrival, axis=0)
+        .transpose(0, 2, 1, 3)
+        .reshape(row_count * slice_rows, block_cols)
+    )
     row_block = lax.all_gather(block_piece, COL, axis=0, tiled=True)
-    shifted_tiles = [grad_tile] + [
-        lax.ppermute(grad_tile, "row", [(i, (i + s) % row_count) for i in range(row_count)])
-        for s in range(1, row_count)
-    ]
-    order = (row_index - jnp.arange(row_count, dtype=jnp.int32)) % row_count
-    column_panel = jnp.take(jnp.stack(shifted_tiles), order, axis=0).reshape(HQ, tile_cols)
+    column_panel = lax.all_to_all(
+        jnp.broadcast_to(grad_tile[None], (row_count,) + grad_tile.shape),
+        "row",
+        split_axis=0,
+        concat_axis=0,
+        tiled=True,
+    ).reshape(HQ, tile_cols)
     panel_chunks = column_panel.reshape(chip_count, 2, chunk, tile_cols)
     keep_rows = lax.dynamic_index_in_dim(panel_chunks, core, 1, keepdims=False)
     send_rows = lax.dynamic_index_in_dim(panel_chunks, 1 - core, 1, keepdims=False)

time: 305 us -> 329 us (1.079)
  waiting for transfers between devices: 124 us -> 167 us
  blocking collectives: 36.4 us -> 0 us
  starting transfers between devices: 41 us -> 68.5 us
  other arithmetic: 37 us -> 26.6 us
  local copies, waits for them, and re-layouts: 19.3 us -> 13.8 us
  matrix products: 32.2 us -> 36 us
    all_to_all x0 -> x1, waiting for transfers between devices: none -> 58.8 us  [shards(): lax.all_to_all(jnp.broadcast_to(grad_tile[None], (row_count,) + grad_tile...]
    all_gather x1, waiting for transfers between devices: 0.9 us -> 44.2 us  [shards(): lax.all_gather(left_mixed, COL, axis=1, tiled=True)]
    all_to_all x2 -> x0, blocking collectives: 36.4 us -> none  [the longest x1 20.9 us: shards(): lax.all_to_all(grad_tile, COL, split_axis=0, concat_axis=1, tiled=True)]
    reduce_scatter x1, waiting for transfers between devices: 32.6 us -> 0.01 us  [shards(): lax.psum_scatter(chip_sum.astype(jnp.bfloat16), 'chip', scatter_dimension...]
    ppermute x7 -> x16, waiting for transfers between devices: 29.3 us -> 5.48 us  [shards(): pieces.append(lax.ppermute(piece, ('row', 'chip', 'core'), route))]
    ppermute x7 -> x16, starting transfers between devices: 31.2 us -> 52.2 us  [shards(): pieces.append(lax.ppermute(piece, ('row', 'chip', 'core'), route))]
    select_n x4 -> x2, other arithmetic: 10.1 us -> 0.73 us  [shards(): jnp.take(jnp.stack(pieces), arrival, axis=0).transpose(0, 2, 1, 3)]
    unnamed x16 -> x20, local copies, waits for them, and re-layouts: 7.72 us -> 0.95 us
  transfers between devices with their start and end apart: 12 -> 22, of which waited for: 9 -> 7; matrix products, arithmetic and copies ran while one was open for 11% -> 9% of each run, Pallas kernels for 0% -> 0%
where the time goes in v2:
time: 329 us; the launch traced here: 328 us
  waiting for transfers between devices  167 us (51%)
  starting transfers between devices  68.5 us (21%)
  matrix products  36 us (11%)
  other arithmetic  26.6 us (8%)
  between operations  16.1 us (5%)
  local copies, waits for them, and re-layouts  13.8 us (4%)
    all_to_all x1, waiting for transfers between devices, shards(): lax.all_to_all(jnp.broadcast_to(grad_tile[None], (row_count,) + grad_tile...  58.8 us
    ppermute x16, starting transfers between devices, shards(): pieces.append(lax.ppermute(piece, ('row', 'chip', 'core'), route))  52.2 us
    all_gather x1, waiting for transfers between devices, shards(): lax.all_gather(left_mixed, COL, axis=1, tiled=True)  44.2 us
    all_gather x1, waiting for transfers between devices, shards(): row_block = lax.all_gather(block_piece, COL, axis=0, tiled=True)  40.6 us
    unnamed x1, other arithmetic  22.8 us
    all_to_all x1, waiting for transfers between devices, shards(): lax.all_to_all(held_rows, COL, split_axis=1, concat_axis=0, tiled=True)  14.1 us
    dot_general x1, matrix products, shards(): lax.dot_general(lax.all_gather(left_mixed, COL, axis=1, tiled=True), righ...  11.1 us
    dot_general x1, matrix products, shards(): lax.dot_general(panel_reordered, row_block, (((0,), (0,)), ((), ())), pre...  10.5 us
  transfers between devices with their start and end apart: 22, of which 7 were waited for; matrix products, arithmetic and copies ran while one was open for 9% of the time, Pallas kernels for 0%

profile of v2, /device:TPU:1, one launch (start us, length us, event | category | flops | bytes accessed | tf_op | source)
XLA Modules:
  0.0 328.1 jit_solution(3994355232059415254)
XLA Ops:
  8.0 22.8 %reduce = bf16[524288]{0:T(1024)(128)(2,1)S(1)} reduce(bf16[1,1,524288]{2,1,0:T(2,128)(2,1)} %param.6, bf16[]{:T(256)} %constant.186), dimensions={0,1}, to_apply=%param.6.reduce_sub_computation | reduce | bytes 2097154 | tf_op args[0]
  31.5 1.5 copy.13
  33.0 7.8 %all-to-all-start = ((bf16[64,16,512]{2,0,1:T(8,128)(2,1)}), bf16[64,16,512]{2,0,1:T(8,128)(2,1)S(1)}, u32[]{:S(2)}, u32[]{:S(2)}) async-start(bf16[64,16,512]{2,0,1:T(8,128)(2,1)} %copy.13), calls=%async_computation | async-start | bytes 2097152 | tf_op jit(solution)/shard_map/all_to_all | solution.py:44
  42.6 14.1 %all-to-all-done = bf16[64,16,512]{2,0,1:T(8,128)(2,1)S(1)} async-done(((bf16[64,16,512]{2,0,1:T(8,128)(2,1)}), bf16[64,16,512]{2,0,1:T(8,128)(2,1)S(1)}, u32[]{:S(2)}, u32[]{:S(2)}) %all-to-all-start) | async-done | bytes 1048608 | tf_op jit(solution)/shard_map/all_to_all | solution.py:44
  56.7 2.0 gather_fusion
  58.8 2.3 broadcast_in_dim.44
  61.1 6.4 %all-to-all-start.1 = ((bf16[8,512,512]{2,1,0:T(8,128)(2,1)}), bf16[8,512,512]{2,1,0:T(8,128)(2,1)}, u32[]{:S(2)}, u32[]{:S(2)}) async-start(bf16[8,512,512]{2,1,0:T(8,128)(2,1)} %broadcast_in_dim.44), calls=%async_computation.1 | async-start | bytes 8388608 | tf_op jit(solution)/shard_map/all_to_all | solution.py:67
  67.5 58.8 %all-to-all-done.1 = bf16[8,512,512]{2,1,0:T(8,128)(2,1)} async-done(((bf16[8,512,512]{2,1,0:T(8,128)(2,1)}), bf16[8,512,512]{2,1,0:T(8,128)(2,1)}, u32[]{:S(2)}, u32[]{:S(2)}) %all-to-all-start.1) | async-done | bytes 4194336 | tf_op jit(solution)/shard_map/all_to_all | solution.py:67
  126.3 2.9 fusion.8
  129.2 1.8 collective-permute-start
  131.1 3.8 %collective-permute-done = bf16[512,8,256]{2,0,1:T(8,128)(2,1)} collective-permute-done((bf16[512,8,256]{2,0,1:T(8,128)(2,1)S(1)}, bf16[512,8,256]{2,0,1:T(8,128)(2,1)}, u32[]{:S(2)}, u32[]{:S(2)}) %collective-permute-start) | collective-permute-done | bytes 2097184 | tf_op jit(solution)/shard_map/ppermute | solution.py:28
  134.9 4.8 %add_convert_fusion = bf16[512,8,256]{2,0,1:T(8,128)(2,1)} fusion(bf16[512,8,256]{2,0,1:T(8,128)(2,1)} %collective-permute-done, bf16[8,2,256,512]{3,2,1,0:T(8,128)(2,1)} %bitcast.7, s32[]{:T(128)S(6)} %select_n.200, bf16[512,512]{1,0:T(8,128)(2,1)S(1)} %broadcast_select_fusion.1), kind=kOutput, calls=%fused_computation.2 | convolution fusion | flops 1076887552 | bytes 6815748 | tf_op jit(solution)/shard_map/dot_general | solution.py:78
  141.0 3.1 collective-permute-start.2
  144.1 4.4 %collective-permute-start.3 = (bf16[32,512]{1,0:T(8,128)(2,1)S(1)}, bf16[32,512]{1,0:T(8,128)(2,1)S(1)}, u32[]{:S(2)}, u32[]{:S(2)}) collective-permute-start(bf16[32,512]{1,0:T(8,128)(2,1)S(1)} %get-tuple-element.18), channel_id=1, source_target_pairs={{0,2},{1,3},{2,20},{3,21},{4,38},{5,39},{6,56},{7,57},{8,74},{9,75... | collective-permute-start | bytes 98312 | tf_op jit(solution)/shard_map/ppermute | solution.py:57
  149.8 5.5 %collective-permute-start.5 = (bf16[32,512]{1,0:T(8,128)(2,1)S(1)}, bf16[32,512]{1,0:T(8,128)(2,1)S(1)}, u32[]{:S(2)}, u32[]{:S(2)}) collective-permute-start(bf16[32,512]{1,0:T(8,128)(2,1)S(1)} %get-tuple-element.16), channel_id=1, source_target_pairs={{0,4},{1,5},{2,22},{3,23},{4,40},{5,41},{6,58},{7,59},{8,76},{9,77... | collective-permute-start | bytes 98312 | tf_op jit(solution)/shard_map/ppermute | solution.py:57
  155.3 5.5 %collective-permute-start.6 = (bf16[32,512]{1,0:T(8,128)(2,1)S(1)}, bf16[32,512]{1,0:T(8,128)(2,1)S(1)}, u32[]{:S(2)}, u32[]{:S(2)}) collective-permute-start(bf16[32,512]{1,0:T(8,128)(2,1)S(1)} %get-tuple-element.15), channel_id=1, source_target_pairs={{0,5},{1,6},{2,23},{3,24},{4,41},{5,42},{6,59},{7,60},{8,77},{9,78... | collective-permute-start | bytes 98312 | tf_op jit(solution)/shard_map/ppermute | solution.py:57
  160.8 4.8 %collective-permute-start.7 = (bf16[32,512]{1,0:T(8,128)(2,1)S(1)}, bf16[32,512]{1,0:T(8,128)(2,1)S(1)}, u32[]{:S(2)}, u32[]{:S(2)}) collective-permute-start(bf16[32,512]{1,0:T(8,128)(2,1)S(1)} %get-tuple-element.14), channel_id=1, source_target_pairs={{0,6},{1,7},{2,24},{3,25},{4,42},{5,43},{6,60},{7,61},{8,78},{9,79... | collective-permute-start | bytes 98312 | tf_op jit(solution)/shard_map/ppermute | solution.py:57
  165.9 2.7 collective-permute-start.9
  168.7 2.5 collective-permute-start.10
  171.2 6.1 %collective-permute-start.11 = (bf16[32,512]{1,0:T(8,128)(2,1)S(1)}, bf16[32,512]{1,0:T(8,128)(2,1)S(1)}, u32[]{:S(2)}, u32[]{:S(2)}) collective-permute-start(bf16[32,512]{1,0:T(8,128)(2,1)S(1)} %get-tuple-element.10), channel_id=1, source_target_pairs={{0,10},{1,11},{2,28},{3,29},{4,46},{5,47},{6,48},{7,49},{8,66},{9,... | collective-permute-start | bytes 98312 | tf_op jit(solution)/shard_map/ppermute | solution.py:57
  177.3 5.2 %collective-permute-start.12 = (bf16[32,512]{1,0:T(8,128)(2,1)S(1)}, bf16[32,512]{1,0:T(8,128)(2,1)S(1)}, u32[]{:S(2)}, u32[]{:S(2)}) collective-permute-start(bf16[32,512]{1,0:T(8,128)(2,1)S(1)} %get-tuple-element.9), channel_id=1, source_target_pairs={{0,11},{1,12},{2,29},{3,30},{4,47},{5,32},{6,49},{7,50},{8,67},{9,... | collective-permute-start | bytes 98312 | tf_op jit(solution)/shard_map/ppermute | solution.py:57
  182.5 1.9 collective-permute-start.13
  184.5 1.8 collective-permute-start.14
  186.3 6.4 %collective-permute-start.15 = (bf16[32,512]{1,0:T(8,128)(2,1)S(1)}, bf16[32,512]{1,0:T(8,128)(2,1)S(1)}, u32[]{:S(2)}, u32[]{:S(2)}) collective-permute-start(bf16[32,512]{1,0:T(8,128)(2,1)S(1)} %get-tuple-element.6), channel_id=1, source_target_pairs={{0,14},{1,15},{2,16},{3,17},{4,34},{5,35},{6,52},{7,53},{8,70},{9,... | collective-permute-start | bytes 98312 | tf_op jit(solution)/shard_map/ppermute | solution.py:57
  193.7 4.6 %collective-permute-done.16 = bf16[32,512]{1,0:T(8,128)(2,1)S(1)} collective-permute-done((bf16[32,512]{1,0:T(8,128)(2,1)S(1)}, bf16[32,512]{1,0:T(8,128)(2,1)S(1)}, u32[]{:S(2)}, u32[]{:S(2)}) %collective-permute-start.16) | collective-permute-done | bytes 32800 | tf_op jit(solution)/shard_map/ppermute | solution.py:57
  200.7 6.7 %fusion.11 = bf16[512,512]{0,1:T(8,128)(2,1)} fusion(bf16[4096,512]{1,0:T(8,128)(2,1)} %bitcast.32, bf16[512,4096]{1,0:T(8,128)(2,1)} %param.10), kind=kOutput, calls=%fused_computation.13 | convolution fusion | flops 2147745792 | bytes 8912896 | tf_op jit(solution)/shard_map/dot_general | solution.py:93
  207.4 4.9 %copy.14 = bf16[8,16,32,512]{3,2,0,1:T(8,128)(2,1)} copy(bf16[8,16,32,512]{3,2,1,0:T(8,128)(2,1)} %bitcast.11) | data formatting | bytes 8388608 | tf_op jit(solution)/shard_map/reshape;reshape | solution.py:85
  212.4 1.8 bitcast_add_fusion
  214.2 40.6 %all-gather.3.cloned.1.call-done = bf16[4096,1024]{1,0:T(8,128)(2,1)} async-done(((bf16[256,1024]{1,0:T(8,128)(2,1)}), bf16[4096,1024]{1,0:T(8,128)(2,1)}) %all-gather.3.cloned.1.call-update) | async-done | bytes 8388624 | tf_op jit(solution)/shard_map/all_gather | solution.py:66
  254.8 10.5 %multiply_add_fusion = f32[512,1024]{1,0:T(8,128)} fusion(f32[512,1024]{1,0:T(8,128)S(1)} %copy-done.1, bf16[4096,512]{1,0:T(8,128)(2,1)} %bitcast.79, bf16[4096,1024]{1,0:T(8,128)(2,1)} %all-gather.3.cloned.1.call-done), kind=kOutput, calls=%fused_computation.7 | convolution fusion | flops 4296540160 | bytes 16777216 | tf_op jit(solution)/shard_map/dot_general | solution.py:89
  265.3 44.2 %all-gather.5.cloned.1.call-done = bf16[512,8192]{0,1:T(8,128)(2,1)} async-done(((bf16[512,512]{0,1:T(8,128)(2,1)}), bf16[512,8192]{0,1:T(8,128)(2,1)}) %all-gather.5.cloned.1.call-update) | async-done | bytes 8388624 | tf_op jit(solution)/shard_map/all_gather | solution.py:97
  309.5 11.1 %convolution_convert_fusion = bf16[512,512]{1,0:T(8,128)(2,1)} fusion(bf16[512,8192]{0,1:T(8,128)(2,1)} %all-gather.5.cloned.1.call-done, bf16[512,8192]{1,0:T(8,128)(2,1)} %param.11), kind=kOutput, calls=%fused_computation.11 | convolution fusion | flops 4295229440 | bytes 17301504 | tf_op jit(solution)/shard_map/dot_general | solution.py:96
  (66 shorter events, 8.6 us)
Async XLA Ops:
  33.0 23.7 %all-to-all-start = ((bf16[64,16,512]{2,0,1:T(8,128)(2,1)}), bf16[64,16,512]{2,0,1:T(8,128)(2,1)S(1)}, u32[]{:S(2)}, u32[]{:S(2)}) async-start(bf16[64,16,512]{2,0,1:T(8,128)(2,1)} %copy.13), calls=%async_computation | async-start | bytes 2097152 | tf_op jit(solution)/shard_map/all_to_all | solution.py:44
  61.1 65.2 %all-to-all-start.1 = ((bf16[8,512,512]{2,1,0:T(8,128)(2,1)}), bf16[8,512,512]{2,1,0:T(8,128)(2,1)}, u32[]{:S(2)}, u32[]{:S(2)}) async-start(bf16[8,512,512]{2,1,0:T(8,128)(2,1)} %broadcast_in_dim.44), calls=%async_computation.1 | async-start | bytes 8388608 | tf_op jit(solution)/shard_map/all_to_all | solution.py:67
  67.5 144.9 %reduce-scatter.2.cloned.1.call-start = ((), (), s32[]{:S(2)}) async-start(), calls=%async_computation.3 | async-start | bytes 2359296 | tf_op jit(solution)/shard_map/reduce_scatter | solution.py:81
  129.2 5.7 %collective-permute-start = (bf16[512,8,256]{2,0,1:T(8,128)(2,1)S(1)}, bf16[512,8,256]{2,0,1:T(8,128)(2,1)}, u32[]{:S(2)}, u32[]{:S(2)}) collective-permute-start(bf16[512,8,256]{2,0,1:T(8,128)(2,1)S(1)} %fusion.8), channel_id=1, source_target_pairs={{0,1},{1,0},{2,3},{3,2},{4,5},{5,4},{6,7},{7,6},{8,9},{9,8},{10,11... | collective-permute-start | bytes 6291464 | tf_op jit(solution)/shard_map/ppermute | solution.py:28
  139.8 115.1 %all-gather.3.cloned.1.call-start = ((), (), s32[]{:S(2)}) async-start(), calls=%async_computation.4 | async-start | bytes 8912896 | tf_op jit(solution)/shard_map/all_gather | solution.py:66
  140.3 14.9 %collective-permute-start.1 = (bf16[32,512]{1,0:T(8,128)(2,1)S(1)}, bf16[32,512]{1,0:T(8,128)(2,1)S(1)}, u32[]{:S(2)}, u32[]{:S(2)}) collective-permute-start(bf16[32,512]{1,0:T(8,128)(2,1)S(1)} %get-tuple-element.20), channel_id=1, source_target_pairs={{0,0},{1,1},{2,18},{3,19},{4,36},{5,37},{6,54},{7,55},{8,72},{9,73... | collective-permute-start | bytes 98312 | tf_op jit(solution)/shard_map/ppermute | solution.py:57
  141.0 19.8 %collective-permute-start.2 = (bf16[32,512]{1,0:T(8,128)(2,1)S(1)}, bf16[32,512]{1,0:T(8,128)(2,1)S(1)}, u32[]{:S(2)}, u32[]{:S(2)}) collective-permute-start(bf16[32,512]{1,0:T(8,128)(2,1)S(1)} %get-tuple-element.19), channel_id=1, source_target_pairs={{0,1},{1,2},{2,19},{3,20},{4,37},{5,38},{6,55},{7,56},{8,73},{9,74... | collective-permute-start | bytes 98312 | tf_op jit(solution)/shard_map/ppermute | solution.py:57
  144.1 21.5 %collective-permute-start.3 = (bf16[32,512]{1,0:T(8,128)(2,1)S(1)}, bf16[32,512]{1,0:T(8,128)(2,1)S(1)}, u32[]{:S(2)}, u32[]{:S(2)}) collective-permute-start(bf16[32,512]{1,0:T(8,128)(2,1)S(1)} %get-tuple-element.18), channel_id=1, source_target_pairs={{0,2},{1,3},{2,20},{3,21},{4,38},{5,39},{6,56},{7,57},{8,74},{9,75... | collective-permute-start | bytes 98312 | tf_op jit(solution)/shard_map/ppermute | solution.py:57
  148.5 17.4 %collective-permute-start.4 = (bf16[32,512]{1,0:T(8,128)(2,1)S(1)}, bf16[32,512]{1,0:T(8,128)(2,1)S(1)}, u32[]{:S(2)}, u32[]{:S(2)}) collective-permute-start(bf16[32,512]{1,0:T(8,128)(2,1)S(1)} %get-tuple-element.17), channel_id=1, source_target_pairs={{0,3},{1,4},{2,21},{3,22},{4,39},{5,40},{6,57},{7,58},{8,75},{9,76... | collective-permute-start | bytes 98312 | tf_op jit(solution)/shard_map/ppermute | solution.py:57
  149.8 18.9 %collective-permute-start.5 = (bf16[32,512]{1,0:T(8,128)(2,1)S(1)}, bf16[32,512]{1,0:T(8,128)(2,1)S(1)}, u32[]{:S(2)}, u32[]{:S(2)}) collective-permute-start(bf16[32,512]{1,0:T(8,128)(2,1)S(1)} %get-tuple-element.16), channel_id=1, source_target_pairs={{0,4},{1,5},{2,22},{3,23},{4,40},{5,41},{6,58},{7,59},{8,76},{9,77... | collective-permute-start | bytes 98312 | tf_op jit(solution)/shard_map/ppermute | solution.py:57
  155.3 16.0 %collective-permute-start.6 = (bf16[32,512]{1,0:T(8,128)(2,1)S(1)}, bf16[32,512]{1,0:T(8,128)(2,1)S(1)}, u32[]{:S(2)}, u32[]{:S(2)}) collective-permute-start(bf16[32,512]{1,0:T(8,128)(2,1)S(1)} %get-tuple-element.15), channel_id=1, source_target_pairs={{0,5},{1,6},{2,23},{3,24},{4,41},{5,42},{6,59},{7,60},{8,77},{9,78... | collective-permute-start | bytes 98312 | tf_op jit(solution)/shard_map/ppermute | solution.py:57
  160.8 16.5 %collective-permute-start.7 = (bf16[32,512]{1,0:T(8,128)(2,1)S(1)}, bf16[32,512]{1,0:T(8,128)(2,1)S(1)}, u32[]{:S(2)}, u32[]{:S(2)}) collective-permute-start(bf16[32,512]{1,0:T(8,128)(2,1)S(1)} %get-tuple-element.14), channel_id=1, source_target_pairs={{0,6},{1,7},{2,24},{3,25},{4,42},{5,43},{6,60},{7,61},{8,78},{9,79... | collective-permute-start | bytes 98312 | tf_op jit(solution)/shard_map/ppermute | solution.py:57
  165.7 16.9 %collective-permute-start.8 = (bf16[32,512]{1,0:T(8,128)(2,1)S(1)}, bf16[32,512]{1,0:T(8,128)(2,1)S(1)}, u32[]{:S(2)}, u32[]{:S(2)}) collective-permute-start(bf16[32,512]{1,0:T(8,128)(2,1)S(1)} %get-tuple-element.13), channel_id=1, source_target_pairs={{0,7},{1,8},{2,25},{3,26},{4,43},{5,44},{6,61},{7,62},{8,79},{9,64... | collective-permute-start | bytes 98312 | tf_op jit(solution)/shard_map/ppermute | solution.py:57
  165.9 18.5 %collective-permute-start.9 = (bf16[32,512]{1,0:T(8,128)(2,1)S(1)}, bf16[32,512]{1,0:T(8,128)(2,1)S(1)}, u32[]{:S(2)}, u32[]{:S(2)}) collective-permute-start(bf16[32,512]{1,0:T(8,128)(2,1)S(1)} %get-tuple-element.12), channel_id=1, source_target_pairs={{0,8},{1,9},{2,26},{3,27},{4,44},{5,45},{6,62},{7,63},{8,64},{9,65... | collective-permute-start | bytes 98312 | tf_op jit(solution)/shard_map/ppermute | solution.py:57
  168.7 17.6 %collective-permute-start.10 = (bf16[32,512]{1,0:T(8,128)(2,1)S(1)}, bf16[32,512]{1,0:T(8,128)(2,1)S(1)}, u32[]{:S(2)}, u32[]{:S(2)}) collective-permute-start(bf16[32,512]{1,0:T(8,128)(2,1)S(1)} %get-tuple-element.11), channel_id=1, source_target_pairs={{0,9},{1,10},{2,27},{3,28},{4,45},{5,46},{6,63},{7,48},{8,65},{9,6... | collective-permute-start | bytes 98312 | tf_op jit(solution)/shard_map/ppermute | solution.py:57
  171.2 21.4 %collective-permute-start.11 = (bf16[32,512]{1,0:T(8,128)(2,1)S(1)}, bf16[32,512]{1,0:T(8,128)(2,1)S(1)}, u32[]{:S(2)}, u32[]{:S(2)}) collective-permute-start(bf16[32,512]{1,0:T(8,128)(2,1)S(1)} %get-tuple-element.10), channel_id=1, source_target_pairs={{0,10},{1,11},{2,28},{3,29},{4,46},{5,47},{6,48},{7,49},{8,66},{9,... | collective-permute-start | bytes 98312 | tf_op jit(solution)/shard_map/ppermute | solution.py:57
  177.3 15.5 %collective-permute-start.12 = (bf16[32,512]{1,0:T(8,128)(2,1)S(1)}, bf16[32,512]{1,0:T(8,128)(2,1)S(1)}, u32[]{:S(2)}, u32[]{:S(2)}) collective-permute-start(bf16[32,512]{1,0:T(8,128)(2,1)S(1)} %get-tuple-element.9), channel_id=1, source_target_pairs={{0,11},{1,12},{2,29},{3,30},{4,47},{5,32},{6,49},{7,50},{8,67},{9,... | collective-permute-start | bytes 98312 | tf_op jit(solution)/shard_map/ppermute | solution.py:57
  182.5 10.3 %collective-permute-start.13 = (bf16[32,512]{1,0:T(8,128)(2,1)S(1)}, bf16[32,512]{1,0:T(8,128)(2,1)S(1)}, u32[]{:S(2)}, u32[]{:S(2)}) collective-permute-start(bf16[32,512]{1,0:T(8,128)(2,1)S(1)} %get-tuple-element.8), channel_id=1, source_target_pairs={{0,12},{1,13},{2,30},{3,31},{4,32},{5,33},{6,50},{7,51},{8,68},{9,... | collective-permute-start | bytes 98312 | tf_op jit(solution)/shard_map/ppermute | solution.py:57
  184.5 8.4 %collective-permute-start.14 = (bf16[32,512]{1,0:T(8,128)(2,1)S(1)}, bf16[32,512]{1,0:T(8,128)(2,1)S(1)}, u32[]{:S(2)}, u32[]{:S(2)}) collective-permute-start(bf16[32,512]{1,0:T(8,128)(2,1)S(1)} %get-tuple-element.7), channel_id=1, source_target_pairs={{0,13},{1,14},{2,31},{3,16},{4,33},{5,34},{6,51},{7,52},{8,69},{9,... | collective-permute-start | bytes 98312 | tf_op jit(solution)/shard_map/ppermute | solution.py:57
  186.3 7.4 %collective-permute-start.15 = (bf16[32,512]{1,0:T(8,128)(2,1)S(1)}, bf16[32,512]{1,0:T(8,128)(2,1)S(1)}, u32[]{:S(2)}, u32[]{:S(2)}) collective-permute-start(bf16[32,512]{1,0:T(8,128)(2,1)S(1)} %get-tuple-element.6), channel_id=1, source_target_pairs={{0,14},{1,15},{2,16},{3,17},{4,34},{5,35},{6,52},{7,53},{8,70},{9,... | collective-permute-start | bytes 98312 | tf_op jit(solution)/shard_map/ppermute | solution.py:57
  192.7 5.6 %collective-permute-start.16 = (bf16[32,512]{1,0:T(8,128)(2,1)S(1)}, bf16[32,512]{1,0:T(8,128)(2,1)S(1)}, u32[]{:S(2)}, u32[]{:S(2)}) collective-permute-start(bf16[32,512]{1,0:T(8,128)(2,1)S(1)} %get-tuple-element.5), channel_id=1, source_target_pairs={{0,15},{1,0},{2,17},{3,18},{4,35},{5,36},{6,53},{7,54},{8,71},{9,7... | collective-permute-start | bytes 98312 | tf_op jit(solution)/shard_map/ppermute | solution.py:57
  200.4 109.1 %all-gather.5.cloned.1.call-start = ((), (), s32[]{:S(2)}) async-start(), calls=%async_computation.5 | async-start | bytes 8912896 | tf_op jit(solution)/shard_map/all_gather | solution.py:97
  207.4 4.9 %copy-start = (f32[512,256]{1,0:T(8,128)S(1)}, f32[512,256]{1,0:T(8,128)}, u32[]{:S(2)}) copy-start(f32[512,256]{1,0:T(8,128)} %param.8) | copy-start | bytes 1572868
  207.4 47.4 %copy-start.1 = (f32[512,1024]{1,0:T(8,128)S(1)}, f32[512,1024]{1,0:T(8,128)}, u32[]{:S(2)}) copy-start(f32[512,1024]{1,0:T(8,128)} %param.9) | copy-start | bytes 6291460
Sparse Core Ops, SparseCore 0:
  139.9 44.0 reduce-scatter.1
Sparse Core Ops, SparseCore 1:
  200.5 54.3 all-gather.2
  256.4 53.1 all-gather.4

commit v3 on v0

--- a/solution.py
+++ b/solution.py
@@ -13,6 +13,7 @@
 stat_decay = 0.9
 
 COL = ("chip", "core")
+ROW = ("x", "yh")
 
 
 def slot_index(row_counts, tile_rows, capacity):
@@ -29,10 +30,13 @@
 
 
 def shards(flat_gradient, range_rows, left_stat, right_stat, left_root, right_root):
-    row_count = lax.axis_size("row")
+    x_count = lax.axis_size("x")
+    row_count = x_count * 2
     chip_count = lax.axis_size("chip")
     col_count = chip_count * 2
-    row_index = lax.axis_index("row")
+    row_index = lax.axis_index(ROW)
+    x_index = lax.axis_index("x")
+    y_half = lax.axis_index("yh")
     core = lax.axis_index("core")
     tile_rows = HQ // row_count
     tile_cols = DIN // col_count
@@ -45,14 +49,20 @@
     row_counts = lax.dynamic_index_in_dim(range_rows, row_index, 0, keepdims=False)
     grad_tile = jnp.take(received, slot_index(row_counts, tile_rows, capacity), axis=0)
     row_slice = lax.all_to_all(grad_tile, COL, split_axis=0, concat_axis=1, tiled=True)
-    block_piece = lax.all_to_all(row_slice, "row", split_axis=1, concat_axis=0, tiled=True)
+    block_piece = lax.all_to_all(row_slice, ROW, split_axis=1, concat_axis=0, tiled=True)
     row_block = lax.all_gather(block_piece, COL, axis=0, tiled=True)
-    shifted_tiles = [grad_tile] + [
-        lax.ppermute(grad_tile, "row", [(i, (i + s) % row_count) for i in range(row_count)])
-        for s in range(1, row_count)
-    ]
-    order = (row_index - jnp.arange(row_count, dtype=jnp.int32)) % row_count
-    column_panel = jnp.take(jnp.stack(shifted_tiles), order, axis=0).reshape(HQ, tile_cols)
+    other_half = lax.ppermute(grad_tile, "yh", [(0, 1), (1, 0)])
+    first = jnp.where(y_half == 0, grad_tile, other_half)
+    second = jnp.where(y_half == 0, other_half, grad_tile)
+    pair = jnp.stack([first, second])
+    panel_parts = jnp.zeros((row_count, tile_rows, tile_cols), grad_tile.dtype)
+    panel_parts = lax.dynamic_update_slice_in_dim(panel_parts, pair, 2 * x_index, 0)
+    for s in range(1, x_count):
+        moved = lax.ppermute(pair, "x", [(i, (i + s) % x_count) for i in range(x_count)])
+        panel_parts = lax.dynamic_update_slice_in_dim(
+            panel_parts, moved, 2 * ((x_index - s) % x_count), 0
+        )
+    column_panel = panel_parts.reshape(HQ, tile_cols)
     panel_chunks = column_panel.reshape(chip_count, 2, chunk, tile_cols)
     keep_rows = lax.dynamic_index_in_dim(panel_chunks, core, 1, keepdims=False)
     send_rows = lax.dynamic_index_in_dim(panel_chunks, 1 - core, 1, keepdims=False)
@@ -87,16 +97,18 @@
 
 def solution(mesh):
     rows, cols = mesh.devices.shape
-    split_mesh = Mesh(mesh.devices.reshape(rows, cols // 2, 2), ("row", "chip", "core"))
+    split_mesh = Mesh(
+        mesh.devices.reshape(rows // 2, 2, cols // 2, 2), ("x", "yh", "chip", "core")
+    )
     in_specs = (
-        P("row", COL, None),
+        P(ROW, COL, None),
         P(),
-        P("row", COL),
-        P(COL, "row"),
-        P("row", None),
+        P(ROW, COL),
+        P(COL, ROW),
+        P(ROW, None),
         P(COL, None),
     )
-    out_specs = (P("row", COL), P(COL, "row"), P("row", COL))
+    out_specs = (P(ROW, COL), P(COL, ROW), P(ROW, COL))
     return jax.shard_map(
         shards, mesh=split_mesh, in_specs=in_specs, out_specs=out_specs, check_vma=False
     )

time: 305 us -> 300 us (0.984)
  waiting for transfers between devices: 124 us -> 155 us
  starting transfers between devices: 41 us -> 18.2 us
  other arithmetic: 37 us -> 27.6 us
  blocking collectives: 36.4 us -> 29.6 us
  matrix products: 32.2 us -> 36.7 us
    all_gather x1, waiting for transfers between devices: 0.9 us -> 44.2 us  [shards(): lax.all_gather(left_mixed, COL, axis=1, tiled=True)]
    reduce_scatter x1, waiting for transfers between devices: 32.6 us -> 4.81 us  [shards(): lax.psum_scatter(chip_sum.astype(jnp.bfloat16), 'chip', scatter_dimension...]
    ppermute x7 -> x4, starting transfers between devices: 31.2 us -> 7.54 us  [the longest x3 4.84 us: shards(): lax.ppermute(pair, 'x', [(i, (i + s) % x_count) for i in range(x_count)])]
    ppermute x7 -> x4, waiting for transfers between devices: 29.3 us -> 52.1 us  [the longest x3 40.7 us: shards(): lax.ppermute(pair, 'x', [(i, (i + s) % x_count) for i in range(x_count)])]
    select_n x4 -> x0, other arithmetic: 10.1 us -> none  [shards(): jnp.take(jnp.stack(shifted_tiles), order, axis=0).reshape(HQ, tile_cols)]
    unnamed x16 -> x4, local copies, waits for them, and re-layouts: 7.72 us -> 0.01 us
    all_gather x1, waiting for transfers between devices: 42.5 us -> 35.5 us  [shards(): row_block = lax.all_gather(block_piece, COL, axis=0, tiled=True)]
    gather x1 -> x0, local copies, waits for them, and re-layouts: 4.94 us -> none  [shards(): jnp.take(jnp.stack(shifted_tiles), order, axis=0).reshape(HQ, tile_cols)]
  transfers between devices with their start and end apart: 12 -> 9, of which waited for: 9 -> 8; matrix products, arithmetic and copies ran while one was open for 11% -> 10% of each run, Pallas kernels for 0% -> 0%
where the time goes in v3:
time: 300 us
  waiting for transfers between devices  155 us (52%)
  matrix products  36.7 us (12%)
  blocking collectives  29.6 us (10%)
  other arithmetic  27.6 us (9%)
  starting transfers between devices  18.2 us (6%)
  local copies, waits for them, and re-layouts  17.5 us (6%)
  between operations  15.6 us (5%)
    all_gather x1, waiting for transfers between devices, shards(): lax.all_gather(left_mixed, COL, axis=1, tiled=True)  44.2 us
    ppermute x3, waiting for transfers between devices, shards(): lax.ppermute(pair, 'x', [(i, (i + s) % x_count) for i in range(x_count)])  40.7 us
    all_gather x1, waiting for transfers between devices, shards(): row_block = lax.all_gather(block_piece, COL, axis=0, tiled=True)  35.5 us
    unnamed x1, other arithmetic  22.8 us
    all_to_all x1, blocking collectives, shards(): lax.all_to_all(grad_tile, COL, split_axis=0, concat_axis=1, tiled=True)  16.7 us
    all_to_all x1, waiting for transfers between devices, shards(): lax.all_to_all(held_rows, COL, split_axis=1, concat_axis=0, tiled=True)  14 us
    all_to_all x1, blocking collectives, shards(): lax.all_to_all(row_slice, ROW, split_axis=1, concat_axis=0, tiled=True)  12.9 us
    ppermute x1, waiting for transfers between devices, shards(): other_half = lax.ppermute(grad_tile, 'yh', [(0, 1), (1, 0)])  11.4 us
  transfers between devices with their start and end apart: 9, of which 8 were waited for; matrix products, arithmetic and copies ran while one was open for 10% of the time, Pallas kernels for 0%

profile of v3, /device:TPU:1, one launch (start us, length us, event | category | flops | bytes accessed | tf_op | source)
XLA Modules:
  0.0 299.8 jit_solution(16834498089542529537)
XLA Ops:
  8.0 22.8 %reduce = bf16[524288]{0:T(1024)(128)(2,1)S(1)} reduce(bf16[1,1,524288]{2,1,0:T(2,128)(2,1)} %param.6, bf16[]{:T(256)} %constant.96), dimensions={0,1}, to_apply=%param.6.reduce_sub_computation | reduce | bytes 2097154 | tf_op args[0]
  31.5 1.5 copy.23
  33.0 7.8 %all-to-all-start = ((bf16[64,16,512]{2,0,1:T(8,128)(2,1)}), bf16[64,16,512]{2,0,1:T(8,128)(2,1)S(1)}, u32[]{:S(2)}, u32[]{:S(2)}) async-start(bf16[64,16,512]{2,0,1:T(8,128)(2,1)} %copy.23), calls=%async_computation | async-start | bytes 2097152 | tf_op jit(solution)/shard_map/all_to_all | solution.py:48
  40.9 0.7 constant_dynamic-slice_fusion
  42.6 14.0 %all-to-all-done = bf16[64,16,512]{2,0,1:T(8,128)(2,1)S(1)} async-done(((bf16[64,16,512]{2,0,1:T(8,128)(2,1)}), bf16[64,16,512]{2,0,1:T(8,128)(2,1)S(1)}, u32[]{:S(2)}, u32[]{:S(2)}) %all-to-all-start) | async-done | bytes 1048608 | tf_op jit(solution)/shard_map/all_to_all | solution.py:48
  56.7 2.0 gather_fusion
  58.8 2.7 collective-permute-start
  61.5 11.4 %collective-permute-done = bf16[512,512]{1,0:T(8,128)(2,1)S(1)} collective-permute-done((bf16[512,512]{1,0:T(8,128)(2,1)S(1)}, bf16[512,512]{1,0:T(8,128)(2,1)S(1)}, u32[]{:S(2)}, u32[]{:S(2)}) %collective-permute-start) | collective-permute-done | bytes 524320 | tf_op jit(solution)/shard_map/ppermute | solution.py:54
  73.1 2.3 broadcast_in_dim.33
  75.4 1.5 pad_maximum_fusion
  76.9 1.2 collective-permute-start.1
  78.2 2.5 collective-permute-start.2
  80.6 1.1 collective-permute-start.3
  81.8 19.6 %collective-permute-done.1 = bf16[2,512,512]{2,1,0:T(8,128)(2,1)} collective-permute-done((bf16[2,512,512]{2,1,0:T(8,128)(2,1)}, bf16[2,512,512]{2,1,0:T(8,128)(2,1)}, u32[]{:S(2)}, u32[]{:S(2)}) %collective-permute-start.1) | collective-permute-done | bytes 1048608 | tf_op jit(solution)/shard_map/ppermute | solution.py:61
  101.3 2.3 constant_dynamic-update-slice_fusion.2
  103.6 21.1 %collective-permute-done.2 = bf16[2,512,512]{2,1,0:T(8,128)(2,1)S(1)} collective-permute-done((bf16[2,512,512]{2,1,0:T(8,128)(2,1)}, bf16[2,512,512]{2,1,0:T(8,128)(2,1)S(1)}, u32[]{:S(2)}, u32[]{:S(2)}) %collective-permute-start.2) | collective-permute-done | bytes 1048608 | tf_op jit(solution)/shard_map/ppermute | solution.py:61
  124.7 1.1 constant_dynamic-update-slice_fusion.1
  125.8 1.1 constant_dynamic-update-slice_fusion
  126.9 4.2 %fusion.5 = bf16[512,8,256]{2,0,1:T(8,128)(2,1)} fusion(bf16[8,2,256,512]{3,2,1,0:T(8,128)(2,1)} %bitcast.9, s32[]{:T(128)S(6)} %select_n.96, bf16[512,512]{1,0:T(8,128)(2,1)S(1)} %broadcast_select_fusion), kind=kOutput, calls=%fused_computation.8 | convolution fusion | flops 1074790400 | bytes 4718596 | tf_op jit(solution)/shard_map/dot_general | solution.py:71
  131.1 2.7 collective-permute-start.4
  133.8 4.0 %collective-permute-done.4 = bf16[512,8,256]{2,0,1:T(8,128)(2,1)S(1)} collective-permute-done((bf16[512,8,256]{2,0,1:T(8,128)(2,1)}, bf16[512,8,256]{2,0,1:T(8,128)(2,1)S(1)}, u32[]{:S(2)}, u32[]{:S(2)}) %collective-permute-start.4) | collective-permute-done | bytes 2097184 | tf_op jit(solution)/shard_map/ppermute | solution.py:29
  137.8 4.2 %add_convert_fusion = bf16[512,8,256]{2,0,1:T(8,128)(2,1)} fusion(bf16[512,8,256]{2,0,1:T(8,128)(2,1)S(1)} %collective-permute-done.4, bf16[8,2,256,512]{3,2,1,0:T(8,128)(2,1)} %bitcast.9, s32[]{:T(128)S(6)} %select_n.95, bf16[512,512]{1,0:T(8,128)(2,1)S(1)} %broadcast_select_fusion), kind=kOutput, calls=%fused_computation.1 | convolution fusion | flops 1076887552 | bytes 6815748 | tf_op jit(solution)/shard_map/dot_general | solution.py:70
  142.3 16.7 %all_to_all.51 = bf16[16,32,512]{2,1,0:T(8,128)(2,1)S(1)} all-to-all(bf16[16,32,512]{2,1,0:T(8,128)(2,1)S(1)} %broadcast_select_fusion.1), channel_id=1, replica_groups=mesh['x'=4,'yh'=2,'chip'=8,'core'=2] {'chip','core'}, dimensions={0} | all-to-all | bytes 1048576 | tf_op jit(solution)/shard_map/all_to_all | solution.py:51
  159.8 12.9 %all_to_all.52 = bf16[32,8,1024]{2,0,1:T(8,128)(2,1)} all-to-all(bf16[32,8,1024]{2,0,1:T(8,128)(2,1)S(1)} %copy.26), channel_id=1, replica_groups=mesh['x'=4,'yh'=2,'chip'=8,'core'=2] {'x','yh'}, dimensions={1} | all-to-all | bytes 1048576 | tf_op jit(solution)/shard_map/all_to_all | solution.py:52
  172.8 6.7 %fusion.8 = bf16[512,512]{0,1:T(8,128)(2,1)} fusion(bf16[4096,512]{1,0:T(8,128)(2,1)} %bitcast.20, bf16[512,4096]{1,0:T(8,128)(2,1)} %param.10), kind=kOutput, calls=%fused_computation.11 | convolution fusion | flops 2147745792 | bytes 8912896 | tf_op jit(solution)/shard_map/dot_general | solution.py:85
  179.6 4.9 %copy.24 = bf16[8,16,32,512]{3,2,0,1:T(8,128)(2,1)} copy(bf16[8,16,32,512]{3,2,1,0:T(8,128)(2,1)} %bitcast.13) | data formatting | bytes 8388608 | tf_op jit(solution)/shard_map/reshape;reshape | solution.py:77
  184.5 4.8 %reduce-scatter.2.cloned.1.call-done = bf16[512,1,256]{2,0,1:T(8,128)(2,1)} async-done(((bf16[512,8,256]{2,0,1:T(8,128)(2,1)}), bf16[512,1,256]{2,0,1:T(8,128)(2,1)}) %reduce-scatter.2.cloned.1.call-update) | async-done | bytes 262160 | tf_op jit(solution)/shard_map/reduce_scatter | solution.py:73
  189.3 1.8 bitcast_add_fusion
  191.1 35.5 %all-gather.3.cloned.1.call-done = bf16[4096,1024]{1,0:T(8,128)(2,1)} async-done(((bf16[256,1024]{1,0:T(8,128)(2,1)}), bf16[4096,1024]{1,0:T(8,128)(2,1)}) %all-gather.3.cloned.1.call-update) | async-done | bytes 8388624 | tf_op jit(solution)/shard_map/all_gather | solution.py:53
  226.6 10.5 %multiply_add_fusion = f32[512,1024]{1,0:T(8,128)} fusion(f32[512,1024]{1,0:T(8,128)S(1)} %copy-done.1, bf16[4096,512]{1,0:T(8,128)(2,1)} %bitcast.48, bf16[4096,1024]{1,0:T(8,128)(2,1)} %all-gather.3.cloned.1.call-done), kind=kOutput, calls=%fused_computation.5 | convolution fusion | flops 4296540160 | bytes 16777216 | tf_op jit(solution)/shard_map/dot_general | solution.py:81
  237.1 44.2 %all-gather.5.cloned.1.call-done = bf16[512,8192]{0,1:T(8,128)(2,1)} async-done(((bf16[512,512]{0,1:T(8,128)(2,1)}), bf16[512,8192]{0,1:T(8,128)(2,1)}) %all-gather.5.cloned.1.call-update) | async-done | bytes 8388624 | tf_op jit(solution)/shard_map/all_gather | solution.py:89
  281.3 11.1 %convolution_convert_fusion = bf16[512,512]{1,0:T(8,128)(2,1)} fusion(bf16[512,8192]{0,1:T(8,128)(2,1)} %all-gather.5.cloned.1.call-done, bf16[512,8192]{1,0:T(8,128)(2,1)} %param.11), kind=kOutput, calls=%fused_computation.9 | convolution fusion | flops 4295229440 | bytes 17301504 | tf_op jit(solution)/shard_map/dot_general | solution.py:88
  (28 shorter events, 3.2 us)
Async XLA Ops:
  33.0 23.7 %all-to-all-start = ((bf16[64,16,512]{2,0,1:T(8,128)(2,1)}), bf16[64,16,512]{2,0,1:T(8,128)(2,1)S(1)}, u32[]{:S(2)}, u32[]{:S(2)}) async-start(bf16[64,16,512]{2,0,1:T(8,128)(2,1)} %copy.23), calls=%async_computation | async-start | bytes 2097152 | tf_op jit(solution)/shard_map/all_to_all | solution.py:48
  40.9 148.4 %reduce-scatter.2.cloned.1.call-start = ((), (), s32[]{:S(2)}) async-start(), calls=%async_computation.4 | async-start | bytes 2359296 | tf_op jit(solution)/shard_map/reduce_scatter | solution.py:73
  58.8 14.2 %collective-permute-start = (bf16[512,512]{1,0:T(8,128)(2,1)S(1)}, bf16[512,512]{1,0:T(8,128)(2,1)S(1)}, u32[]{:S(2)}, u32[]{:S(2)}) collective-permute-start(bf16[512,512]{1,0:T(8,128)(2,1)S(1)} %broadcast_select_fusion), channel_id=1, source_target_pairs={{0,16},{16,0},{1,17},{17,1},{2,18},{18,2},{3,19},{19,3},{4,20},{20... | collective-permute-start | bytes 1572872 | tf_op jit(solution)/shard_map/ppermute | solution.py:54
  76.9 24.4 %collective-permute-start.1 = (bf16[2,512,512]{2,1,0:T(8,128)(2,1)}, bf16[2,512,512]{2,1,0:T(8,128)(2,1)}, u32[]{:S(2)}, u32[]{:S(2)}) collective-permute-start(bf16[2,512,512]{2,1,0:T(8,128)(2,1)} %get-tuple-element.5), channel_id=1, source_target_pairs={{0,32},{32,64},{64,96},{96,0},{1,33},{33,65},{65,97},{97,1},{2,34}... | collective-permute-start | bytes 3145736 | tf_op jit(solution)/shard_map/ppermute | solution.py:61
  78.2 46.6 %collective-permute-start.2 = (bf16[2,512,512]{2,1,0:T(8,128)(2,1)}, bf16[2,512,512]{2,1,0:T(8,128)(2,1)S(1)}, u32[]{:S(2)}, u32[]{:S(2)}) collective-permute-start(bf16[2,512,512]{2,1,0:T(8,128)(2,1)} %get-tuple-element.5), channel_id=1, source_target_pairs={{0,64},{32,96},{64,0},{96,32},{1,65},{33,97},{65,1},{97,33},{2,66}... | collective-permute-start | bytes 3145736 | tf_op jit(solution)/shard_map/ppermute | solution.py:61
  80.6 45.2 %collective-permute-start.3 = (bf16[2,512,512]{2,1,0:T(8,128)(2,1)}, bf16[2,512,512]{2,1,0:T(8,128)(2,1)S(1)}, u32[]{:S(2)}, u32[]{:S(2)}) collective-permute-start(bf16[2,512,512]{2,1,0:T(8,128)(2,1)} %get-tuple-element.5), channel_id=1, source_target_pairs={{0,96},{32,0},{64,32},{96,64},{1,97},{33,1},{65,33},{97,65},{2,98}... | collective-permute-start | bytes 3145736 | tf_op jit(solution)/shard_map/ppermute | solution.py:61
  131.1 6.7 %collective-permute-start.4 = (bf16[512,8,256]{2,0,1:T(8,128)(2,1)}, bf16[512,8,256]{2,0,1:T(8,128)(2,1)S(1)}, u32[]{:S(2)}, u32[]{:S(2)}) collective-permute-start(bf16[512,8,256]{2,0,1:T(8,128)(2,1)} %fusion.5), channel_id=1, source_target_pairs={{0,1},{1,0},{2,3},{3,2},{4,5},{5,4},{6,7},{7,6},{8,9},{9,8},{10,11... | collective-permute-start | bytes 6291464 | tf_op jit(solution)/shard_map/ppermute | solution.py:29
  142.0 84.6 %all-gather.3.cloned.1.call-start = ((), (), s32[]{:S(2)}) async-start(), calls=%async_computation.5 | async-start | bytes 8912896 | tf_op jit(solution)/shard_map/all_gather | solution.py:53
  172.7 108.5 %all-gather.5.cloned.1.call-start = ((), (), s32[]{:S(2)}) async-start(), calls=%async_computation.6 | async-start | bytes 8912896 | tf_op jit(solution)/shard_map/all_gather | solution.py:89
  179.5 9.7 %copy-start = (f32[512,256]{1,0:T(8,128)S(1)}, f32[512,256]{1,0:T(8,128)}, u32[]{:S(2)}) copy-start(f32[512,256]{1,0:T(8,128)} %param.8) | copy-start | bytes 1572868
  179.5 47.0 %copy-start.1 = (f32[512,1024]{1,0:T(8,128)S(1)}, f32[512,1024]{1,0:T(8,128)}, u32[]{:S(2)}) copy-start(f32[512,1024]{1,0:T(8,128)} %param.9) | copy-start | bytes 6291460
Sparse Core Ops, SparseCore 0:
  142.1 47.1 reduce-scatter.1
Sparse Core Ops, SparseCore 1:
  172.8 53.7 all-gather.2
  228.7 52.5 all-gather.4

commit v4 on v3

--- a/solution.py
+++ b/solution.py
@@ -50,7 +50,13 @@
     grad_tile = jnp.take(received, slot_index(row_counts, tile_rows, capacity), axis=0)
     row_slice = lax.all_to_all(grad_tile, COL, split_axis=0, concat_axis=1, tiled=True)
     block_piece = lax.all_to_all(row_slice, ROW, split_axis=1, concat_axis=0, tiled=True)
-    row_block = lax.all_gather(block_piece, COL, axis=0, tiled=True)
+    row_block = lax.all_to_all(
+        jnp.broadcast_to(block_piece[None], (col_count,) + block_piece.shape),
+        COL,
+        split_axis=0,
+        concat_axis=0,
+        tiled=True,
+    ).reshape(HQ, block_cols)
     other_half = lax.ppermute(grad_tile, "yh", [(0, 1), (1, 0)])
     first = jnp.where(y_half == 0, grad_tile, other_half)
     second = jnp.where(y_half == 0, other_half, grad_tile)

time: 300 us -> 361 us (1.20)
  waiting for transfers between devices: 155 us -> 199 us
  starting transfers between devices: 18.2 us -> 26.3 us
  blocking collectives: 29.6 us -> 34.3 us
  local copies, waits for them, and re-layouts: 17.5 us -> 21.7 us
    all_to_all x0 -> x1, waiting for transfers between devices: none -> 90.2 us  [shards(): lax.all_to_all(jnp.broadcast_to(block_piece[None], (col_count,) + block_p...]
    all_gather x1, waiting for transfers between devices: 44.2 us -> 0.01 us  [shards(): lax.all_gather(left_mixed, COL, axis=1, tiled=True)]
    all_gather x1 -> x0, waiting for transfers between devices: 35.5 us -> none  [shards(): row_block = lax.all_gather(block_piece, COL, axis=0, tiled=True)]
    reduce_scatter x1, waiting for transfers between devices: 4.81 us -> 38.2 us  [shards(): lax.psum_scatter(chip_sum.astype(jnp.bfloat16), 'chip', scatter_dimension...]
    all_to_all x0 -> x1, starting transfers between devices: none -> 8.03 us  [shards(): lax.all_to_all(jnp.broadcast_to(block_piece[None], (col_count,) + block_p...]
    broadcast_in_dim x0 -> x1, local copies, waits for them, and re-layouts: none -> 4.3 us  [shards(): jnp.broadcast_to(block_piece[None], (col_count,) + block_piece.shape)]
  transfers between devices with their start and end apart: 9 -> 9, of which waited for: 8 -> 7; matrix products, arithmetic and copies ran while one was open for 10% -> 9% of each run, Pallas kernels for 0% -> 0%
where the time goes in v4:
time: 361 us
  waiting for transfers between devices  199 us (55%)
  matrix products  36.6 us (10%)
  blocking collectives  34.3 us (10%)
  other arithmetic  27.6 us (8%)
  starting transfers between devices  26.3 us (7%)
  local copies, waits for them, and re-layouts  21.7 us (6%)
  between operations  15.6 us (4%)
    all_to_all x1, waiting for transfers between devices, shards(): lax.all_to_all(jnp.broadcast_to(block_piece[None], (col_count,) + block_p...  90.2 us
    ppermute x3, waiting for transfers between devices, shards(): lax.ppermute(pair, 'x', [(i, (i + s) % x_count) for i in range(x_count)])  40.6 us
    reduce_scatter x1, waiting for transfers between devices, shards(): lax.psum_scatter(chip_sum.astype(jnp.bfloat16), 'chip', scatter_dimension...  38.2 us
    unnamed x1, other arithmetic  22.8 us
    all_to_all x1, blocking collectives, shards(): lax.all_to_all(grad_tile, COL, split_axis=0, concat_axis=1, tiled=True)  19.8 us
    all_to_all x1, blocking collectives, shards(): lax.all_to_all(row_slice, ROW, split_axis=1, concat_axis=0, tiled=True)  14.5 us
    all_to_all x1, waiting for transfers between devices, shards(): lax.all_to_all(held_rows, COL, split_axis=1, concat_axis=0, tiled=True)  14 us
    ppermute x1, waiting for transfers between devices, shards(): other_half = lax.ppermute(grad_tile, 'yh', [(0, 1), (1, 0)])  11.4 us
  transfers between devices with their start and end apart: 9, of which 7 were waited for; matrix products, arithmetic and copies ran while one was open for 9% of the time, Pallas kernels for 0%

profile of v4, /device:TPU:1, one launch (start us, length us, event | category | flops | bytes accessed | tf_op | source)
XLA Modules:
  0.0 360.8 jit_solution(17894846525411730202)
XLA Ops:
  8.0 22.8 %reduce = bf16[524288]{0:T(1024)(128)(2,1)S(1)} reduce(bf16[1,1,524288]{2,1,0:T(2,128)(2,1)} %param.6, bf16[]{:T(256)} %constant.96), dimensions={0,1}, to_apply=%param.6.reduce_sub_computation | reduce | bytes 2097154 | tf_op args[0]
  31.5 1.5 copy.23
  33.0 7.8 %all-to-all-start = ((bf16[64,16,512]{2,0,1:T(8,128)(2,1)}), bf16[64,16,512]{2,0,1:T(8,128)(2,1)S(1)}, u32[]{:S(2)}, u32[]{:S(2)}) async-start(bf16[64,16,512]{2,0,1:T(8,128)(2,1)} %copy.23), calls=%async_computation | async-start | bytes 2097152 | tf_op jit(solution)/shard_map/all_to_all | solution.py:48
  42.6 14.0 %all-to-all-done = bf16[64,16,512]{2,0,1:T(8,128)(2,1)S(1)} async-done(((bf16[64,16,512]{2,0,1:T(8,128)(2,1)}), bf16[64,16,512]{2,0,1:T(8,128)(2,1)S(1)}, u32[]{:S(2)}, u32[]{:S(2)}) %all-to-all-start) | async-done | bytes 1048608 | tf_op jit(solution)/shard_map/all_to_all | solution.py:48
  56.7 2.0 gather_fusion
  58.8 2.7 collective-permute-start
  61.5 11.4 %collective-permute-done = bf16[512,512]{1,0:T(8,128)(2,1)S(1)} collective-permute-done((bf16[512,512]{1,0:T(8,128)(2,1)S(1)}, bf16[512,512]{1,0:T(8,128)(2,1)S(1)}, u32[]{:S(2)}, u32[]{:S(2)}) %collective-permute-start) | collective-permute-done | bytes 524320 | tf_op jit(solution)/shard_map/ppermute | solution.py:60
  73.1 2.3 broadcast_in_dim.41
  75.4 1.5 pad_maximum_fusion
  76.9 1.2 collective-permute-start.1
  78.1 2.5 collective-permute-start.2
  80.6 1.2 collective-permute-start.3
  81.7 19.6 %collective-permute-done.1 = bf16[2,512,512]{2,1,0:T(8,128)(2,1)} collective-permute-done((bf16[2,512,512]{2,1,0:T(8,128)(2,1)}, bf16[2,512,512]{2,1,0:T(8,128)(2,1)}, u32[]{:S(2)}, u32[]{:S(2)}) %collective-permute-start.1) | collective-permute-done | bytes 1048608 | tf_op jit(solution)/shard_map/ppermute | solution.py:67
  101.4 2.3 constant_dynamic-update-slice_fusion.2
  103.6 21.0 %collective-permute-done.2 = bf16[2,512,512]{2,1,0:T(8,128)(2,1)S(1)} collective-permute-done((bf16[2,512,512]{2,1,0:T(8,128)(2,1)}, bf16[2,512,512]{2,1,0:T(8,128)(2,1)S(1)}, u32[]{:S(2)}, u32[]{:S(2)}) %collective-permute-start.2) | collective-permute-done | bytes 1048608 | tf_op jit(solution)/shard_map/ppermute | solution.py:67
  124.7 1.1 constant_dynamic-update-slice_fusion.1
  125.7 1.0 constant_dynamic-update-slice_fusion
  126.8 4.2 %fusion.5 = bf16[512,8,256]{2,0,1:T(8,128)(2,1)} fusion(bf16[8,2,256,512]{3,2,1,0:T(8,128)(2,1)} %bitcast.9, s32[]{:T(128)S(6)} %select_n.96, bf16[512,512]{1,0:T(8,128)(2,1)S(1)} %broadcast_select_fusion), kind=kOutput, calls=%fused_computation.8 | convolution fusion | flops 1074790400 | bytes 4718596 | tf_op jit(solution)/shard_map/dot_general | solution.py:77
  131.0 2.7 collective-permute-start.4
  133.7 4.0 %collective-permute-done.4 = bf16[512,8,256]{2,0,1:T(8,128)(2,1)S(1)} collective-permute-done((bf16[512,8,256]{2,0,1:T(8,128)(2,1)}, bf16[512,8,256]{2,0,1:T(8,128)(2,1)S(1)}, u32[]{:S(2)}, u32[]{:S(2)}) %collective-permute-start.4) | collective-permute-done | bytes 2097184 | tf_op jit(solution)/shard_map/ppermute | solution.py:29
  137.7 4.2 %add_convert_fusion = bf16[512,8,256]{2,0,1:T(8,128)(2,1)} fusion(bf16[512,8,256]{2,0,1:T(8,128)(2,1)S(1)} %collective-permute-done.4, bf16[8,2,256,512]{3,2,1,0:T(8,128)(2,1)} %bitcast.9, s32[]{:T(128)S(6)} %select_n.95, bf16[512,512]{1,0:T(8,128)(2,1)S(1)} %broadcast_select_fusion), kind=kOutput, calls=%fused_computation.1 | convolution fusion | flops 1076887552 | bytes 6815748 | tf_op jit(solution)/shard_map/dot_general | solution.py:76
  142.1 6.6 %fusion.8 = bf16[512,512]{0,1:T(8,128)(2,1)} fusion(bf16[4096,512]{1,0:T(8,128)(2,1)} %bitcast.21, bf16[512,4096]{1,0:T(8,128)(2,1)} %param.10), kind=kOutput, calls=%fused_computation.11 | convolution fusion | flops 2147745792 | bytes 8912896 | tf_op jit(solution)/shard_map/dot_general | solution.py:91
  149.1 19.8 %all_to_all.53 = bf16[16,32,512]{2,1,0:T(8,128)(2,1)S(1)} all-to-all(bf16[16,32,512]{2,1,0:T(8,128)(2,1)S(1)} %broadcast_select_fusion.1), channel_id=1, replica_groups=mesh['x'=4,'yh'=2,'chip'=8,'core'=2] {'chip','core'}, dimensions={0} | all-to-all | bytes 1048576 | tf_op jit(solution)/shard_map/all_to_all | solution.py:51
  169.7 14.5 %all_to_all.54 = bf16[32,8,1024]{2,0,1:T(8,128)(2,1)S(1)} all-to-all(bf16[32,8,1024]{2,0,1:T(8,128)(2,1)S(1)} %copy.26), channel_id=1, replica_groups=mesh['x'=4,'yh'=2,'chip'=8,'core'=2] {'x','yh'}, dimensions={1} | all-to-all | bytes 1048576 | tf_op jit(solution)/shard_map/all_to_all | solution.py:52
  184.2 4.3 %broadcast_in_dim.45 = bf16[16,256,1024]{2,1,0:T(8,128)(2,1)} broadcast(bf16[256,1024]{1,0:T(8,128)(2,1)S(1)} %bitcast.50), dimensions={1,2} | broadcast | bytes 8912896 | tf_op jit(solution)/shard_map/broadcast_in_dim | solution.py:54
  188.5 8.0 %all-to-all-start.3 = ((bf16[16,256,1024]{2,1,0:T(8,128)(2,1)}), bf16[16,256,1024]{2,1,0:T(8,128)(2,1)}, u32[]{:S(2)}, u32[]{:S(2)}) async-start(bf16[16,256,1024]{2,1,0:T(8,128)(2,1)} %broadcast_in_dim.45), calls=%async_computation.4 | async-start | bytes 16777216 | tf_op jit(solution)/shard_map/all_to_all | solution.py:53
  196.6 4.9 %copy.24 = bf16[8,16,32,512]{3,2,0,1:T(8,128)(2,1)} copy(bf16[8,16,32,512]{3,2,1,0:T(8,128)(2,1)} %bitcast.13) | data formatting | bytes 8388608 | tf_op jit(solution)/shard_map/reshape;reshape | solution.py:83
  201.5 38.2 %reduce-scatter.2.cloned.1.call-done = bf16[512,1,256]{2,0,1:T(8,128)(2,1)} async-done(((bf16[512,8,256]{2,0,1:T(8,128)(2,1)}), bf16[512,1,256]{2,0,1:T(8,128)(2,1)}) %reduce-scatter.2.cloned.1.call-update) | async-done | bytes 262160 | tf_op jit(solution)/shard_map/reduce_scatter | solution.py:79
  239.7 1.8 bitcast_add_fusion
  241.5 90.2 %all-to-all-done.3 = bf16[16,256,1024]{2,1,0:T(8,128)(2,1)} async-done(((bf16[16,256,1024]{2,1,0:T(8,128)(2,1)}), bf16[16,256,1024]{2,1,0:T(8,128)(2,1)}, u32[]{:S(2)}, u32[]{:S(2)}) %all-to-all-start.3) | async-done | bytes 8388640 | tf_op jit(solution)/shard_map/all_to_all | solution.py:53
  331.7 10.5 %multiply_add_fusion = f32[512,1024]{1,0:T(8,128)} fusion(f32[512,1024]{1,0:T(8,128)S(1)} %copy-done.1, bf16[4096,512]{1,0:T(8,128)(2,1)} %bitcast.49, bf16[4096,1024]{1,0:T(8,128)(2,1)} %bitcast.20), kind=kOutput, calls=%fused_computation.5 | convolution fusion | flops 4296540160 | bytes 16777216 | tf_op jit(solution)/shard_map/dot_general | solution.py:87
  342.2 11.1 %convolution_convert_fusion = bf16[512,512]{1,0:T(8,128)(2,1)} fusion(bf16[512,8192]{0,1:T(8,128)(2,1)} %all-gather.2.cloned.1.call-done, bf16[512,8192]{1,0:T(8,128)(2,1)} %param.11), kind=kOutput, calls=%fused_computation.9 | convolution fusion | flops 4295229440 | bytes 17301504 | tf_op jit(solution)/shard_map/dot_general | solution.py:94
  (28 shorter events, 4.0 us)
Async XLA Ops:
  33.0 23.7 %all-to-all-start = ((bf16[64,16,512]{2,0,1:T(8,128)(2,1)}), bf16[64,16,512]{2,0,1:T(8,128)(2,1)S(1)}, u32[]{:S(2)}, u32[]{:S(2)}) async-start(bf16[64,16,512]{2,0,1:T(8,128)(2,1)} %copy.23), calls=%async_computation | async-start | bytes 2097152 | tf_op jit(solution)/shard_map/all_to_all | solution.py:48
  40.9 198.8 %reduce-scatter.2.cloned.1.call-start = ((), (), s32[]{:S(2)}) async-start(), calls=%async_computation.5 | async-start | bytes 2359296 | tf_op jit(solution)/shard_map/reduce_scatter | solution.py:79
  58.8 14.2 %collective-permute-start = (bf16[512,512]{1,0:T(8,128)(2,1)S(1)}, bf16[512,512]{1,0:T(8,128)(2,1)S(1)}, u32[]{:S(2)}, u32[]{:S(2)}) collective-permute-start(bf16[512,512]{1,0:T(8,128)(2,1)S(1)} %broadcast_select_fusion), channel_id=1, source_target_pairs={{0,16},{16,0},{1,17},{17,1},{2,18},{18,2},{3,19},{19,3},{4,20},{20... | collective-permute-start | bytes 1572872 | tf_op jit(solution)/shard_map/ppermute | solution.py:60
  76.9 24.4 %collective-permute-start.1 = (bf16[2,512,512]{2,1,0:T(8,128)(2,1)}, bf16[2,512,512]{2,1,0:T(8,128)(2,1)}, u32[]{:S(2)}, u32[]{:S(2)}) collective-permute-start(bf16[2,512,512]{2,1,0:T(8,128)(2,1)} %get-tuple-element.5), channel_id=1, source_target_pairs={{0,32},{32,64},{64,96},{96,0},{1,33},{33,65},{65,97},{97,1},{2,34}... | collective-permute-start | bytes 3145736 | tf_op jit(solution)/shard_map/ppermute | solution.py:67
  78.1 46.6 %collective-permute-start.2 = (bf16[2,512,512]{2,1,0:T(8,128)(2,1)}, bf16[2,512,512]{2,1,0:T(8,128)(2,1)S(1)}, u32[]{:S(2)}, u32[]{:S(2)}) collective-permute-start(bf16[2,512,512]{2,1,0:T(8,128)(2,1)} %get-tuple-element.5), channel_id=1, source_target_pairs={{0,64},{32,96},{64,0},{96,32},{1,65},{33,97},{65,1},{97,33},{2,66}... | collective-permute-start | bytes 3145736 | tf_op jit(solution)/shard_map/ppermute | solution.py:67
  80.6 45.2 %collective-permute-start.3 = (bf16[2,512,512]{2,1,0:T(8,128)(2,1)}, bf16[2,512,512]{2,1,0:T(8,128)(2,1)S(1)}, u32[]{:S(2)}, u32[]{:S(2)}) collective-permute-start(bf16[2,512,512]{2,1,0:T(8,128)(2,1)} %get-tuple-element.5), channel_id=1, source_target_pairs={{0,96},{32,0},{64,32},{96,64},{1,97},{33,1},{65,33},{97,65},{2,98}... | collective-permute-start | bytes 3145736 | tf_op jit(solution)/shard_map/ppermute | solution.py:67
  131.0 6.7 %collective-permute-start.4 = (bf16[512,8,256]{2,0,1:T(8,128)(2,1)}, bf16[512,8,256]{2,0,1:T(8,128)(2,1)S(1)}, u32[]{:S(2)}, u32[]{:S(2)}) collective-permute-start(bf16[512,8,256]{2,0,1:T(8,128)(2,1)} %fusion.5), channel_id=1, source_target_pairs={{0,1},{1,0},{2,3},{3,2},{4,5},{5,4},{6,7},{7,6},{8,9},{9,8},{10,11... | collective-permute-start | bytes 6291464 | tf_op jit(solution)/shard_map/ppermute | solution.py:29
  141.9 200.3 %all-gather.2.cloned.1.call-start = ((), (), s32[]{:S(2)}) async-start(), calls=%async_computation.6 | async-start | bytes 8912896 | tf_op jit(solution)/shard_map/all_gather | solution.py:95
  188.5 143.2 %all-to-all-start.3 = ((bf16[16,256,1024]{2,1,0:T(8,128)(2,1)}), bf16[16,256,1024]{2,1,0:T(8,128)(2,1)}, u32[]{:S(2)}, u32[]{:S(2)}) async-start(bf16[16,256,1024]{2,1,0:T(8,128)(2,1)} %broadcast_in_dim.45), calls=%async_computation.4 | async-start | bytes 16777216 | tf_op jit(solution)/shard_map/all_to_all | solution.py:53
  196.6 43.1 %copy-start = (f32[512,256]{1,0:T(8,128)S(1)}, f32[512,256]{1,0:T(8,128)}, u32[]{:S(2)}) copy-start(f32[512,256]{1,0:T(8,128)} %param.8) | copy-start | bytes 1572868
  196.6 135.2 %copy-start.1 = (f32[512,1024]{1,0:T(8,128)S(1)}, f32[512,1024]{1,0:T(8,128)}, u32[]{:S(2)}) copy-start(f32[512,1024]{1,0:T(8,128)} %param.9) | copy-start | bytes 6291460
Sparse Core Ops, SparseCore 0:
  142.0 97.5 reduce-scatter.1
Sparse Core Ops, SparseCore 1:
  148.9 126.6 all-gather.1

commit v5 on v3

--- a/solution.py
+++ b/solution.py
@@ -50,18 +50,22 @@
     grad_tile = jnp.take(received, slot_index(row_counts, tile_rows, capacity), axis=0)
     row_slice = lax.all_to_all(grad_tile, COL, split_axis=0, concat_axis=1, tiled=True)
     block_piece = lax.all_to_all(row_slice, ROW, split_axis=1, concat_axis=0, tiled=True)
-    row_block = lax.all_gather(block_piece, COL, axis=0, tiled=True)
     other_half = lax.ppermute(grad_tile, "yh", [(0, 1), (1, 0)])
     first = jnp.where(y_half == 0, grad_tile, other_half)
     second = jnp.where(y_half == 0, other_half, grad_tile)
     pair = jnp.stack([first, second])
+    moved = [
+        lax.ppermute(pair, "x", [(i, (i + s) % x_count) for i in range(x_count)])
+        for s in range(1, x_count)
+    ]
+    moved, block_piece = lax.optimization_barrier((moved, block_piece))
     panel_parts = jnp.zeros((row_count, tile_rows, tile_cols), grad_tile.dtype)
     panel_parts = lax.dynamic_update_slice_in_dim(panel_parts, pair, 2 * x_index, 0)
     for s in range(1, x_count):
-        moved = lax.ppermute(pair, "x", [(i, (i + s) % x_count) for i in range(x_count)])
         panel_parts = lax.dynamic_update_slice_in_dim(
-            panel_parts, moved, 2 * ((x_index - s) % x_count), 0
+            panel_parts, moved[s - 1], 2 * ((x_index - s) % x_count), 0
         )
+    row_block = lax.all_gather(block_piece, COL, axis=0, tiled=True)
     column_panel = panel_parts.reshape(HQ, tile_cols)
     panel_chunks = column_panel.reshape(chip_count, 2, chunk, tile_cols)
     keep_rows = lax.dynamic_index_in_dim(panel_chunks, core, 1, keepdims=False)

time: 300 us -> 298 us (level)
  blocking collectives: 29.6 us -> 15.6 us
  waiting for transfers between devices: 155 us -> 162 us
    reduce_scatter x1, waiting for transfers between devices: 4.81 us -> 53.5 us  [shards(): lax.psum_scatter(chip_sum.astype(jnp.bfloat16), 'chip', scatter_dimension...]
    ppermute x3, waiting for transfers between devices: 40.7 us -> 0.01 us  [shards(): lax.ppermute(pair, 'x', [(i, (i + s) % x_count) for i in range(x_count)])]
    all_gather x1, waiting for transfers between devices: 44.2 us -> 3.75 us  [shards(): lax.all_gather(left_mixed, COL, axis=1, tiled=True)]
    all_to_all x0 -> x1, waiting for transfers between devices: none -> 31.5 us  [shards(): lax.all_to_all(row_slice, ROW, split_axis=1, concat_axis=0, tiled=True)]
    all_to_all x1 -> x0, blocking collectives: 12.9 us -> none  [shards(): lax.all_to_all(row_slice, ROW, split_axis=1, concat_axis=0, tiled=True)]
    all_gather x1, waiting for transfers between devices: 35.5 us -> 42.9 us  [shards(): row_block = lax.all_gather(block_piece, COL, axis=0, tiled=True)]
    all_to_all x0 -> x1, starting transfers between devices: none -> 3.95 us  [shards(): lax.all_to_all(row_slice, ROW, split_axis=1, concat_axis=0, tiled=True)]
  transfers between devices with their start and end apart: 9 -> 10, of which waited for: 8 -> 7; matrix products, arithmetic and copies ran while one was open for 10% -> 9% of each run, Pallas kernels for 0% -> 0%
where the time goes in v5:
time: 298 us; the launch traced here: 297 us
  waiting for transfers between devices  162 us (54%)
  matrix products  37.3 us (13%)
  other arithmetic  27.5 us (9%)
  starting transfers between devices  20.2 us (7%)
  local copies, waits for them, and re-layouts  19.5 us (7%)
  between operations  15.7 us (5%)
  blocking collectives  15.6 us (5%)
    reduce_scatter x1, waiting for transfers between devices, shards(): lax.psum_scatter(chip_sum.astype(jnp.bfloat16), 'chip', scatter_dimension...  53.5 us
    all_gather x1, waiting for transfers between devices, shards(): row_block = lax.all_gather(block_piece, COL, axis=0, tiled=True)  42.9 us
    all_to_all x1, waiting for transfers between devices, shards(): lax.all_to_all(row_slice, ROW, split_axis=1, concat_axis=0, tiled=True)  31.5 us
    unnamed x1, other arithmetic  22.8 us
    all_to_all x1, blocking collectives, shards(): lax.all_to_all(grad_tile, COL, split_axis=0, concat_axis=1, tiled=True)  15.6 us
    all_to_all x1, waiting for transfers between devices, shards(): lax.all_to_all(held_rows, COL, split_axis=1, concat_axis=0, tiled=True)  14.1 us
    ppermute x1, waiting for transfers between devices, shards(): other_half = lax.ppermute(grad_tile, 'yh', [(0, 1), (1, 0)])  11.3 us
    dot_general x1, matrix products, shards(): lax.dot_general(lax.all_gather(left_mixed, COL, axis=1, tiled=True), righ...  11.1 us
  transfers between devices with their start and end apart: 10, of which 7 were waited for; matrix products, arithmetic and copies ran while one was open for 9% of the time, Pallas kernels for 0%

profile of v5, /device:TPU:1, one launch (start us, length us, event | category | flops | bytes accessed | tf_op | source)
XLA Modules:
  0.0 297.5 jit_solution(11638193783019487378)
XLA Ops:
  8.0 22.8 %reduce = bf16[524288]{0:T(1024)(128)(2,1)S(1)} reduce(bf16[1,1,524288]{2,1,0:T(2,128)(2,1)} %param.6, bf16[]{:T(256)} %constant.96), dimensions={0,1}, to_apply=%param.6.reduce_sub_computation | reduce | bytes 2097154 | tf_op args[0]
  31.5 1.5 copy.23
  33.0 7.8 %all-to-all-start = ((bf16[64,16,512]{2,0,1:T(8,128)(2,1)}), bf16[64,16,512]{2,0,1:T(8,128)(2,1)S(1)}, u32[]{:S(2)}, u32[]{:S(2)}) async-start(bf16[64,16,512]{2,0,1:T(8,128)(2,1)} %copy.23), calls=%async_computation | async-start | bytes 2097152 | tf_op jit(solution)/shard_map/all_to_all | solution.py:48
  41.7 0.7 subtract_bitcast_fusion
  42.6 14.1 %all-to-all-done = bf16[64,16,512]{2,0,1:T(8,128)(2,1)S(1)} async-done(((bf16[64,16,512]{2,0,1:T(8,128)(2,1)}), bf16[64,16,512]{2,0,1:T(8,128)(2,1)S(1)}, u32[]{:S(2)}, u32[]{:S(2)}) %all-to-all-start) | async-done | bytes 1048608 | tf_op jit(solution)/shard_map/all_to_all | solution.py:48
  56.7 2.0 gather_fusion
  58.8 2.7 collective-permute-start
  61.7 11.3 %collective-permute-done = bf16[512,512]{1,0:T(8,128)(2,1)S(1)} collective-permute-done((bf16[512,512]{1,0:T(8,128)(2,1)S(1)}, bf16[512,512]{1,0:T(8,128)(2,1)S(1)}, u32[]{:S(2)}, u32[]{:S(2)}) %collective-permute-start) | collective-permute-done | bytes 524320 | tf_op jit(solution)/shard_map/ppermute | solution.py:53
  73.1 2.3 broadcast_in_dim.33
  75.4 1.5 pad_maximum_fusion
  76.9 1.2 collective-permute-start.1
  78.2 2.5 collective-permute-start.2
  80.6 1.1 collective-permute-start.3
  81.9 15.6 %all_to_all.51 = bf16[16,32,512]{2,1,0:T(8,128)(2,1)S(1)} all-to-all(bf16[16,32,512]{2,1,0:T(8,128)(2,1)S(1)} %broadcast_select_fusion.1), channel_id=1, replica_groups=mesh['x'=4,'yh'=2,'chip'=8,'core'=2] {'chip','core'}, dimensions={0} | all-to-all | bytes 1048576 | tf_op jit(solution)/shard_map/all_to_all | solution.py:51
  98.0 1.1 copy.25
  99.1 3.9 %all-to-all-start.2 = ((bf16[32,8,1024]{2,0,1:T(8,128)(2,1)}), bf16[32,8,1024]{2,0,1:T(8,128)(2,1)S(1)}, u32[]{:S(2)}, u32[]{:S(2)}) async-start(bf16[32,8,1024]{2,0,1:T(8,128)(2,1)} %copy.25), calls=%async_computation.2 | async-start | bytes 1048576 | tf_op jit(solution)/shard_map/all_to_all | solution.py:52
  103.1 31.5 %all-to-all-done.2 = bf16[32,8,1024]{2,0,1:T(8,128)(2,1)S(1)} async-done(((bf16[32,8,1024]{2,0,1:T(8,128)(2,1)}), bf16[32,8,1024]{2,0,1:T(8,128)(2,1)S(1)}, u32[]{:S(2)}, u32[]{:S(2)}) %all-to-all-start.2) | async-done | bytes 524320 | tf_op jit(solution)/shard_map/all_to_all | solution.py:52
  134.6 1.2 constant_dynamic-update-slice_fusion.2
  135.8 2.3 constant_dynamic-update-slice_fusion.1
  138.1 2.3 constant_dynamic-update-slice_fusion
  140.4 4.2 %fusion.8 = bf16[512,8,256]{2,0,1:T(8,128)(2,1)} fusion(bf16[8,2,256,512]{3,2,1,0:T(8,128)(2,1)} %bitcast.13, s32[]{:T(128)S(6)} %select_n.98, bf16[512,512]{1,0:T(8,128)(2,1)S(1)} %broadcast_select_fusion), kind=kOutput, calls=%fused_computation.9 | convolution fusion | flops 1074790400 | bytes 4718596 | tf_op jit(solution)/shard_map/dot_general | solution.py:75
  144.6 0.8 collective-permute-start.4
  145.4 4.1 %collective-permute-done.4 = bf16[512,8,256]{2,0,1:T(8,128)(2,1)} collective-permute-done((bf16[512,8,256]{2,0,1:T(8,128)(2,1)}, bf16[512,8,256]{2,0,1:T(8,128)(2,1)}, u32[]{:S(2)}, u32[]{:S(2)}) %collective-permute-start.4) | collective-permute-done | bytes 2097184 | tf_op jit(solution)/shard_map/ppermute | solution.py:29
  149.5 4.8 %add_convert_fusion = bf16[512,8,256]{2,0,1:T(8,128)(2,1)} fusion(bf16[512,8,256]{2,0,1:T(8,128)(2,1)} %collective-permute-done.4, bf16[8,2,256,512]{3,2,1,0:T(8,128)(2,1)} %bitcast.13, s32[]{:T(128)S(6)} %select_n.97, bf16[512,512]{1,0:T(8,128)(2,1)S(1)} %broadcast_select_fusion), kind=kOutput, calls=%fused_computation.1 | convolution fusion | flops 1076887552 | bytes 6815748 | tf_op jit(solution)/shard_map/dot_general | solution.py:74
  154.4 6.6 %fusion.11 = bf16[512,512]{0,1:T(8,128)(2,1)} fusion(bf16[4096,512]{1,0:T(8,128)(2,1)} %bitcast.20, bf16[512,4096]{1,0:T(8,128)(2,1)} %param.10), kind=kOutput, calls=%fused_computation.12 | convolution fusion | flops 2147745792 | bytes 8912896 | tf_op jit(solution)/shard_map/dot_general | solution.py:89
  161.7 4.8 %copy.26 = bf16[8,16,32,512]{3,2,0,1:T(8,128)(2,1)} copy(bf16[8,16,32,512]{3,2,1,0:T(8,128)(2,1)} %bitcast.17) | data formatting | bytes 8388608 | tf_op jit(solution)/shard_map/reshape;reshape | solution.py:81
  166.4 53.5 %reduce-scatter.2.cloned.1.call-done = bf16[512,1,256]{2,0,1:T(8,128)(2,1)} async-done(((bf16[512,8,256]{2,0,1:T(8,128)(2,1)}), bf16[512,1,256]{2,0,1:T(8,128)(2,1)}) %reduce-scatter.2.cloned.1.call-update) | async-done | bytes 262160 | tf_op jit(solution)/shard_map/reduce_scatter | solution.py:77
  220.0 1.8 bitcast_add_fusion
  221.8 3.8 %all-gather.5.cloned.1.call-done = bf16[512,8192]{0,1:T(8,128)(2,1)} async-done(((bf16[512,512]{0,1:T(8,128)(2,1)}), bf16[512,8192]{0,1:T(8,128)(2,1)}) %all-gather.5.cloned.1.call-update) | async-done | bytes 8388624 | tf_op jit(solution)/shard_map/all_gather | solution.py:93
  225.6 11.1 %convolution_convert_fusion = bf16[512,512]{1,0:T(8,128)(2,1)} fusion(bf16[512,8192]{0,1:T(8,128)(2,1)} %all-gather.5.cloned.1.call-done, bf16[512,8192]{1,0:T(8,128)(2,1)} %param.11), kind=kOutput, calls=%fused_computation.10 | convolution fusion | flops 4295229440 | bytes 17301504 | tf_op jit(solution)/shard_map/dot_general | solution.py:92
  236.7 42.9 %all-gather.3.cloned.1.call-done = bf16[4096,1024]{1,0:T(8,128)(2,1)} async-done(((bf16[256,1024]{1,0:T(8,128)(2,1)}), bf16[4096,1024]{1,0:T(8,128)(2,1)}) %all-gather.3.cloned.1.call-update) | async-done | bytes 8388624 | tf_op jit(solution)/shard_map/all_gather | solution.py:68
  279.6 10.5 %multiply_add_fusion = f32[512,1024]{1,0:T(8,128)} fusion(f32[512,1024]{1,0:T(8,128)S(1)} %copy-done.2, bf16[4096,512]{1,0:T(8,128)(2,1)} %bitcast.50, bf16[4096,1024]{1,0:T(8,128)(2,1)} %all-gather.3.cloned.1.call-done), kind=kOutput, calls=%fused_computation.6 | convolution fusion | flops 4296540160 | bytes 16777216 | tf_op jit(solution)/shard_map/dot_general | solution.py:85
  (31 shorter events, 3.4 us)
Async XLA Ops:
  33.0 23.7 %all-to-all-start = ((bf16[64,16,512]{2,0,1:T(8,128)(2,1)}), bf16[64,16,512]{2,0,1:T(8,128)(2,1)S(1)}, u32[]{:S(2)}, u32[]{:S(2)}) async-start(bf16[64,16,512]{2,0,1:T(8,128)(2,1)} %copy.23), calls=%async_computation | async-start | bytes 2097152 | tf_op jit(solution)/shard_map/all_to_all | solution.py:48
  58.8 14.2 %collective-permute-start = (bf16[512,512]{1,0:T(8,128)(2,1)S(1)}, bf16[512,512]{1,0:T(8,128)(2,1)S(1)}, u32[]{:S(2)}, u32[]{:S(2)}) collective-permute-start(bf16[512,512]{1,0:T(8,128)(2,1)S(1)} %broadcast_select_fusion), channel_id=1, source_target_pairs={{0,16},{16,0},{1,17},{17,1},{2,18},{18,2},{3,19},{19,3},{4,20},{20... | collective-permute-start | bytes 1572872 | tf_op jit(solution)/shard_map/ppermute | solution.py:53
  76.9 57.7 %collective-permute-start.1 = (bf16[2,512,512]{2,1,0:T(8,128)(2,1)}, bf16[2,512,512]{2,1,0:T(8,128)(2,1)S(1)}, u32[]{:S(2)}, u32[]{:S(2)}) collective-permute-start(bf16[2,512,512]{2,1,0:T(8,128)(2,1)} %get-tuple-element.13), channel_id=1, source_target_pairs={{0,32},{32,64},{64,96},{96,0},{1,33},{33,65},{65,97},{97,1},{2,34}... | collective-permute-start | bytes 3145736 | tf_op jit(solution)/shard_map/ppermute | solution.py:58
  78.2 56.4 %collective-permute-start.2 = (bf16[2,512,512]{2,1,0:T(8,128)(2,1)}, bf16[2,512,512]{2,1,0:T(8,128)(2,1)}, u32[]{:S(2)}, u32[]{:S(2)}) collective-permute-start(bf16[2,512,512]{2,1,0:T(8,128)(2,1)} %get-tuple-element.13), channel_id=1, source_target_pairs={{0,64},{32,96},{64,0},{96,32},{1,65},{33,97},{65,1},{97,33},{2,66}... | collective-permute-start | bytes 3145736 | tf_op jit(solution)/shard_map/ppermute | solution.py:58
  80.6 54.0 %collective-permute-start.3 = (bf16[2,512,512]{2,1,0:T(8,128)(2,1)}, bf16[2,512,512]{2,1,0:T(8,128)(2,1)}, u32[]{:S(2)}, u32[]{:S(2)}) collective-permute-start(bf16[2,512,512]{2,1,0:T(8,128)(2,1)} %get-tuple-element.13), channel_id=1, source_target_pairs={{0,96},{32,0},{64,32},{96,64},{1,97},{33,1},{65,33},{97,65},{2,98}... | collective-permute-start | bytes 3145736 | tf_op jit(solution)/shard_map/ppermute | solution.py:58
  99.1 35.5 %all-to-all-start.2 = ((bf16[32,8,1024]{2,0,1:T(8,128)(2,1)}), bf16[32,8,1024]{2,0,1:T(8,128)(2,1)S(1)}, u32[]{:S(2)}, u32[]{:S(2)}) async-start(bf16[32,8,1024]{2,0,1:T(8,128)(2,1)} %copy.25), calls=%async_computation.2 | async-start | bytes 1048576 | tf_op jit(solution)/shard_map/all_to_all | solution.py:52
  103.0 117.0 %reduce-scatter.2.cloned.1.call-start = ((), (), s32[]{:S(2)}) async-start(), calls=%async_computation.4 | async-start | bytes 2359296 | tf_op jit(solution)/shard_map/reduce_scatter | solution.py:77
  134.6 10.0 %copy-start = (bf16[32,8,1024]{2,0,1:T(8,128)(2,1)}, bf16[32,8,1024]{2,0,1:T(8,128)(2,1)S(1)}, u32[]{:S(2)}) copy-start(bf16[32,8,1024]{2,0,1:T(8,128)(2,1)S(1)} %all-to-all-done.2) | copy-start | bytes 1572868
  144.6 4.9 %collective-permute-start.4 = (bf16[512,8,256]{2,0,1:T(8,128)(2,1)}, bf16[512,8,256]{2,0,1:T(8,128)(2,1)}, u32[]{:S(2)}, u32[]{:S(2)}) collective-permute-start(bf16[512,8,256]{2,0,1:T(8,128)(2,1)} %fusion.8), channel_id=1, source_target_pairs={{0,1},{1,0},{2,3},{3,2},{4,5},{5,4},{6,7},{7,6},{8,9},{9,8},{10,11... | collective-permute-start | bytes 6291464 | tf_op jit(solution)/shard_map/ppermute | solution.py:29
  154.3 71.2 %all-gather.5.cloned.1.call-start = ((), (), s32[]{:S(2)}) async-start(), calls=%async_computation.6 | async-start | bytes 8912896 | tf_op jit(solution)/shard_map/all_gather | solution.py:93
  161.1 118.5 %all-gather.3.cloned.1.call-start = ((), (), s32[]{:S(2)}) async-start(), calls=%async_computation.5 | async-start | bytes 8912896 | tf_op jit(solution)/shard_map/all_gather | solution.py:68
  161.6 58.3 %copy-start.1 = (f32[512,256]{1,0:T(8,128)S(1)}, f32[512,256]{1,0:T(8,128)}, u32[]{:S(2)}) copy-start(f32[512,256]{1,0:T(8,128)} %param.8) | copy-start | bytes 1572868
  221.8 57.8 %copy-start.2 = (f32[512,1024]{1,0:T(8,128)S(1)}, f32[512,1024]{1,0:T(8,128)}, u32[]{:S(2)}) copy-start(f32[512,1024]{1,0:T(8,128)} %param.9) | copy-start | bytes 6291460
Sparse Core Ops, SparseCore 0:
  154.5 65.4 reduce-scatter.1
Sparse Core Ops, SparseCore 1:
  161.1 64.4 all-gather.4
  227.1 52.4 all-gather.2

commit v6 on v5

--- a/solution.py
+++ b/solution.py
@@ -58,14 +58,14 @@
         lax.ppermute(pair, "x", [(i, (i + s) % x_count) for i in range(x_count)])
         for s in range(1, x_count)
     ]
-    moved, block_piece = lax.optimization_barrier((moved, block_piece))
+    row_block = lax.all_gather(block_piece, COL, axis=0, tiled=True)
+    moved, row_block = lax.optimization_barrier((moved, row_block))
     panel_parts = jnp.zeros((row_count, tile_rows, tile_cols), grad_tile.dtype)
     panel_parts = lax.dynamic_update_slice_in_dim(panel_parts, pair, 2 * x_index, 0)
     for s in range(1, x_count):
         panel_parts = lax.dynamic_update_slice_in_dim(
             panel_parts, moved[s - 1], 2 * ((x_index - s) % x_count), 0
         )
-    row_block = lax.all_gather(block_piece, COL, axis=0, tiled=True)
     column_panel = panel_parts.reshape(HQ, tile_cols)
     panel_chunks = column_panel.reshape(chip_count, 2, chunk, tile_cols)
     keep_rows = lax.dynamic_index_in_dim(panel_chunks, core, 1, keepdims=False)

time: 298 us -> 288 us (0.966)
  blocking collectives: 15.6 us -> 29 us
  waiting for transfers between devices: 162 us -> 153 us
  starting transfers between devices: 20.2 us -> 14.1 us
  local copies, waits for them, and re-layouts: 19.5 us -> 14.1 us
    all_gather x1, waiting for transfers between devices: 3.75 us -> 57 us  [shards(): lax.all_gather(left_mixed, COL, axis=1, tiled=True)]
    ppermute x3, waiting for transfers between devices: 0.01 us -> 45.3 us  [shards(): lax.ppermute(pair, 'x', [(i, (i + s) % x_count) for i in range(x_count)])]
    all_gather x1, waiting for transfers between devices: 42.9 us -> 0.01 us  [shards(): row_block = lax.all_gather(block_piece, COL, axis=0, tiled=True)]
    reduce_scatter x1, waiting for transfers between devices: 53.5 us -> 21.2 us  [shards(): lax.psum_scatter(chip_sum.astype(jnp.bfloat16), 'chip', scatter_dimension...]
    all_to_all x1 -> x0, waiting for transfers between devices: 31.5 us -> none  [shards(): lax.all_to_all(row_slice, ROW, split_axis=1, concat_axis=0, tiled=True)]
    all_to_all x0 -> x1, blocking collectives: none -> 15.8 us  [shards(): lax.all_to_all(row_slice, ROW, split_axis=1, concat_axis=0, tiled=True)]
    all_to_all x1 -> x0, starting transfers between devices: 3.95 us -> none  [shards(): lax.all_to_all(row_slice, ROW, split_axis=1, concat_axis=0, tiled=True)]
  transfers between devices with their start and end apart: 10 -> 9, of which waited for: 7 -> 8; matrix products, arithmetic and copies ran while one was open for 9% -> 9% of each run, Pallas kernels for 0% -> 0%
where the time goes in v6:
time: 288 us
  waiting for transfers between devices  153 us (53%)
  matrix products  35.7 us (12%)
  blocking collectives  29 us (10%)
  other arithmetic  27.5 us (10%)
  local copies, waits for them, and re-layouts  14.1 us (5%)
  starting transfers between devices  14.1 us (5%)
  between operations  13.9 us (5%)
    all_gather x1, waiting for transfers between devices, shards(): lax.all_gather(left_mixed, COL, axis=1, tiled=True)  57 us
    ppermute x3, waiting for transfers between devices, shards(): lax.ppermute(pair, 'x', [(i, (i + s) % x_count) for i in range(x_count)])  45.3 us
    unnamed x1, other arithmetic  22.8 us
    reduce_scatter x1, waiting for transfers between devices, shards(): lax.psum_scatter(chip_sum.astype(jnp.bfloat16), 'chip', scatter_dimension...  21.2 us
    all_to_all x1, blocking collectives, shards(): lax.all_to_all(row_slice, ROW, split_axis=1, concat_axis=0, tiled=True)  15.8 us
    all_to_all x1, waiting for transfers between devices, shards(): lax.all_to_all(held_rows, COL, split_axis=1, concat_axis=0, tiled=True)  13.9 us
    all_to_all x1, blocking collectives, shards(): lax.all_to_all(grad_tile, COL, split_axis=0, concat_axis=1, tiled=True)  13.2 us
    ppermute x1, waiting for transfers between devices, shards(): other_half = lax.ppermute(grad_tile, 'yh', [(0, 1), (1, 0)])  11.9 us
  transfers between devices with their start and end apart: 9, of which 8 were waited for; matrix products, arithmetic and copies ran while one was open for 9% of the time, Pallas kernels for 0%

profile of v6, /device:TPU:1, one launch (start us, length us, event | category | flops | bytes accessed | tf_op | source)
XLA Modules:
  0.0 287.7 jit_solution(14847457144527146430)
XLA Ops:
  7.2 22.8 %reduce = bf16[524288]{0:T(1024)(128)(2,1)S(1)} reduce(bf16[1,1,524288]{2,1,0:T(2,128)(2,1)} %param.6, bf16[]{:T(256)} %constant.96), dimensions={0,1}, to_apply=%param.6.reduce_sub_computation | reduce | bytes 2097154 | tf_op args[0]
  30.0 0.7 all_to_all.38
  30.6 1.5 copy.23
  32.2 7.8 %all-to-all-start = ((bf16[64,16,512]{2,0,1:T(8,128)(2,1)}), bf16[64,16,512]{2,0,1:T(8,128)(2,1)S(1)}, u32[]{:S(2)}, u32[]{:S(2)}) async-start(bf16[64,16,512]{2,0,1:T(8,128)(2,1)} %copy.23), calls=%async_computation | async-start | bytes 2097152 | tf_op jit(solution)/shard_map/all_to_all | solution.py:48
  40.1 0.7 constant_dynamic-slice_fusion
  41.0 0.7 subtract_bitcast_fusion
  42.0 13.9 %all-to-all-done = bf16[64,16,512]{2,0,1:T(8,128)(2,1)S(1)} async-done(((bf16[64,16,512]{2,0,1:T(8,128)(2,1)}), bf16[64,16,512]{2,0,1:T(8,128)(2,1)S(1)}, u32[]{:S(2)}, u32[]{:S(2)}) %all-to-all-start) | async-done | bytes 1048608 | tf_op jit(solution)/shard_map/all_to_all | solution.py:48
  55.9 2.0 gather_fusion
  58.0 13.2 %all_to_all.51 = bf16[16,32,512]{2,1,0:T(8,128)(2,1)S(1)} all-to-all(bf16[16,32,512]{2,1,0:T(8,128)(2,1)S(1)} %broadcast_select_fusion.1), channel_id=1, replica_groups=mesh['x'=4,'yh'=2,'chip'=8,'core'=2] {'chip','core'}, dimensions={0} | all-to-all | bytes 1048576 | tf_op jit(solution)/shard_map/all_to_all | solution.py:51
  72.0 15.8 %all_to_all.52 = bf16[32,8,1024]{2,0,1:T(8,128)(2,1)} all-to-all(bf16[32,8,1024]{2,0,1:T(8,128)(2,1)S(1)} %copy.25), channel_id=1, replica_groups=mesh['x'=4,'yh'=2,'chip'=8,'core'=2] {'x','yh'}, dimensions={1} | all-to-all | bytes 1048576 | tf_op jit(solution)/shard_map/all_to_all | solution.py:52
  88.0 1.3 collective-permute-start
  89.3 11.9 %collective-permute-done = bf16[512,512]{1,0:T(8,128)(2,1)S(1)} collective-permute-done((bf16[512,512]{1,0:T(8,128)(2,1)S(1)}, bf16[512,512]{1,0:T(8,128)(2,1)S(1)}, u32[]{:S(2)}, u32[]{:S(2)}) %collective-permute-start) | collective-permute-done | bytes 524320 | tf_op jit(solution)/shard_map/ppermute | solution.py:53
  101.3 2.3 broadcast_in_dim.33
  103.6 1.5 pad_maximum_fusion
  105.7 2.1 collective-permute-start.3
  107.8 14.0 %collective-permute-done.1 = bf16[2,512,512]{2,1,0:T(8,128)(2,1)S(1)} collective-permute-done((bf16[2,512,512]{2,1,0:T(8,128)(2,1)}, bf16[2,512,512]{2,1,0:T(8,128)(2,1)S(1)}, u32[]{:S(2)}, u32[]{:S(2)}) %collective-permute-start.1) | collective-permute-done | bytes 1048608 | tf_op jit(solution)/shard_map/ppermute | solution.py:58
  121.8 21.1 %collective-permute-done.2 = bf16[2,512,512]{2,1,0:T(8,128)(2,1)S(1)} collective-permute-done((bf16[2,512,512]{2,1,0:T(8,128)(2,1)}, bf16[2,512,512]{2,1,0:T(8,128)(2,1)S(1)}, u32[]{:S(2)}, u32[]{:S(2)}) %collective-permute-start.2) | collective-permute-done | bytes 1048608 | tf_op jit(solution)/shard_map/ppermute | solution.py:58
  143.0 10.2 %collective-permute-done.3 = bf16[2,512,512]{2,1,0:T(8,128)(2,1)S(1)} collective-permute-done((bf16[2,512,512]{2,1,0:T(8,128)(2,1)}, bf16[2,512,512]{2,1,0:T(8,128)(2,1)S(1)}, u32[]{:S(2)}, u32[]{:S(2)}) %collective-permute-start.3) | collective-permute-done | bytes 1048608 | tf_op jit(solution)/shard_map/ppermute | solution.py:58
  153.1 1.1 constant_dynamic-update-slice_fusion.2
  154.2 1.0 constant_dynamic-update-slice_fusion.1
  155.2 1.1 constant_dynamic-update-slice_fusion
  156.3 4.2 %fusion.8 = bf16[512,8,256]{2,0,1:T(8,128)(2,1)} fusion(bf16[8,2,256,512]{3,2,1,0:T(8,128)(2,1)} %bitcast.13, s32[]{:T(128)S(6)} %select_n.98, bf16[512,512]{1,0:T(8,128)(2,1)S(1)} %copy-done.2), kind=kOutput, calls=%fused_computation.9 | convolution fusion | flops 1074790400 | bytes 4718596 | tf_op jit(solution)/shard_map/dot_general | solution.py:75
  160.6 2.1 collective-permute-start.4
  162.7 4.0 %collective-permute-done.4 = bf16[512,8,256]{2,0,1:T(8,128)(2,1)S(1)} collective-permute-done((bf16[512,8,256]{2,0,1:T(8,128)(2,1)}, bf16[512,8,256]{2,0,1:T(8,128)(2,1)S(1)}, u32[]{:S(2)}, u32[]{:S(2)}) %collective-permute-start.4) | collective-permute-done | bytes 2097184 | tf_op jit(solution)/shard_map/ppermute | solution.py:29
  166.7 4.2 %add_convert_fusion = bf16[512,8,256]{2,0,1:T(8,128)(2,1)} fusion(bf16[512,8,256]{2,0,1:T(8,128)(2,1)S(1)} %collective-permute-done.4, bf16[8,2,256,512]{3,2,1,0:T(8,128)(2,1)} %bitcast.13, s32[]{:T(128)S(6)} %select_n.97, bf16[512,512]{1,0:T(8,128)(2,1)S(1)} %copy-done.3), kind=kOutput, calls=%fused_computation.1 | convolution fusion | flops 1076887552 | bytes 6815748 | tf_op jit(solution)/shard_map/dot_general | solution.py:74
  171.0 6.6 %fusion.11 = bf16[512,512]{0,1:T(8,128)(2,1)} fusion(bf16[4096,512]{1,0:T(8,128)(2,1)} %bitcast.20, bf16[512,4096]{1,0:T(8,128)(2,1)} %param.10), kind=kOutput, calls=%fused_computation.12 | convolution fusion | flops 2147745792 | bytes 8912896 | tf_op jit(solution)/shard_map/dot_general | solution.py:89
  177.6 2.8 copy.26
  180.5 9.5 %multiply_add_fusion = f32[512,1024]{1,0:T(8,128)} fusion(f32[512,1024]{1,0:T(8,128)S(1)} %copy-done.4, bf16[4096,512]{1,0:T(8,128)(2,1)S(1)} %bitcast.50, bf16[4096,1024]{1,0:T(8,128)(2,1)} %all-gather.3.cloned.1.call-done), kind=kOutput, calls=%fused_computation.6 | convolution fusion | flops 4296540160 | bytes 16777216 | tf_op jit(solution)/shard_map/dot_general | solution.py:85
  189.9 21.2 %reduce-scatter.2.cloned.1.call-done = bf16[512,1,256]{2,0,1:T(8,128)(2,1)} async-done(((bf16[512,8,256]{2,0,1:T(8,128)(2,1)}), bf16[512,1,256]{2,0,1:T(8,128)(2,1)}) %reduce-scatter.2.cloned.1.call-update) | async-done | bytes 262160 | tf_op jit(solution)/shard_map/reduce_scatter | solution.py:77
  211.2 1.8 bitcast_add_fusion
  213.0 57.0 %all-gather.5.cloned.1.call-done = bf16[512,8192]{0,1:T(8,128)(2,1)} async-done(((bf16[512,512]{0,1:T(8,128)(2,1)}), bf16[512,8192]{0,1:T(8,128)(2,1)}) %all-gather.5.cloned.1.call-update) | async-done | bytes 8388624 | tf_op jit(solution)/shard_map/all_gather | solution.py:93
  270.0 11.1 %convolution_convert_fusion = bf16[512,512]{1,0:T(8,128)(2,1)} fusion(bf16[512,8192]{0,1:T(8,128)(2,1)} %all-gather.5.cloned.1.call-done, bf16[512,8192]{1,0:T(8,128)(2,1)} %param.11), kind=kOutput, calls=%fused_computation.10 | convolution fusion | flops 4295229440 | bytes 17301504 | tf_op jit(solution)/shard_map/dot_general | solution.py:92
  (34 shorter events, 2.4 us)
Async XLA Ops:
  32.2 23.7 %all-to-all-start = ((bf16[64,16,512]{2,0,1:T(8,128)(2,1)}), bf16[64,16,512]{2,0,1:T(8,128)(2,1)S(1)}, u32[]{:S(2)}, u32[]{:S(2)}) async-start(bf16[64,16,512]{2,0,1:T(8,128)(2,1)} %copy.23), calls=%async_computation | async-start | bytes 2097152 | tf_op jit(solution)/shard_map/all_to_all | solution.py:48
  40.0 113.1 %all-gather.3.cloned.1.call-start = ((), (), s32[]{:S(2)}) async-start(), calls=%async_computation.4 | async-start | bytes 8912896 | tf_op jit(solution)/shard_map/all_gather | solution.py:61
  87.7 123.4 %reduce-scatter.2.cloned.1.call-start = ((), (), s32[]{:S(2)}) async-start(), calls=%async_computation.5 | async-start | bytes 2359296 | tf_op jit(solution)/shard_map/reduce_scatter | solution.py:77
  87.9 17.2 %copy-start.1 = (bf16[512,512]{1,0:T(8,128)(2,1)}, bf16[512,512]{1,0:T(8,128)(2,1)S(1)}, u32[]{:S(2)}) copy-start(bf16[512,512]{1,0:T(8,128)(2,1)S(1)} %broadcast_select_fusion) | copy-start | bytes 1572868
  88.0 13.2 %collective-permute-start = (bf16[512,512]{1,0:T(8,128)(2,1)S(1)}, bf16[512,512]{1,0:T(8,128)(2,1)S(1)}, u32[]{:S(2)}, u32[]{:S(2)}) collective-permute-start(bf16[512,512]{1,0:T(8,128)(2,1)S(1)} %broadcast_select_fusion), channel_id=1, source_target_pairs={{0,16},{16,0},{1,17},{17,1},{2,18},{18,2},{3,19},{19,3},{4,20},{20... | collective-permute-start | bytes 1572872 | tf_op jit(solution)/shard_map/ppermute | solution.py:53
  105.1 16.7 %collective-permute-start.1 = (bf16[2,512,512]{2,1,0:T(8,128)(2,1)}, bf16[2,512,512]{2,1,0:T(8,128)(2,1)S(1)}, u32[]{:S(2)}, u32[]{:S(2)}) collective-permute-start(bf16[2,512,512]{2,1,0:T(8,128)(2,1)} %get-tuple-element.13), channel_id=1, source_target_pairs={{0,32},{32,64},{64,96},{96,0},{1,33},{33,65},{65,97},{97,1},{2,34}... | collective-permute-start | bytes 3145736 | tf_op jit(solution)/shard_map/ppermute | solution.py:58
  105.1 37.8 %collective-permute-start.2 = (bf16[2,512,512]{2,1,0:T(8,128)(2,1)}, bf16[2,512,512]{2,1,0:T(8,128)(2,1)S(1)}, u32[]{:S(2)}, u32[]{:S(2)}) collective-permute-start(bf16[2,512,512]{2,1,0:T(8,128)(2,1)} %get-tuple-element.13), channel_id=1, source_target_pairs={{0,64},{32,96},{64,0},{96,32},{1,65},{33,97},{65,1},{97,33},{2,66}... | collective-permute-start | bytes 3145736 | tf_op jit(solution)/shard_map/ppermute | solution.py:58
  105.7 47.4 %collective-permute-start.3 = (bf16[2,512,512]{2,1,0:T(8,128)(2,1)}, bf16[2,512,512]{2,1,0:T(8,128)(2,1)S(1)}, u32[]{:S(2)}, u32[]{:S(2)}) collective-permute-start(bf16[2,512,512]{2,1,0:T(8,128)(2,1)} %get-tuple-element.13), channel_id=1, source_target_pairs={{0,96},{32,0},{64,32},{96,64},{1,97},{33,1},{65,33},{97,65},{2,98}... | collective-permute-start | bytes 3145736 | tf_op jit(solution)/shard_map/ppermute | solution.py:58
  153.1 3.2 %copy-start.2 = (bf16[512,512]{1,0:T(8,128)(2,1)S(1)}, bf16[512,512]{1,0:T(8,128)(2,1)}, u32[]{:S(2)}) copy-start(bf16[512,512]{1,0:T(8,128)(2,1)} %copy-done.1) | copy-start | bytes 1572868
  155.2 11.4 %copy-start.3 = (bf16[512,512]{1,0:T(8,128)(2,1)S(1)}, bf16[512,512]{1,0:T(8,128)(2,1)}, u32[]{:S(2)}) copy-start(bf16[512,512]{1,0:T(8,128)(2,1)} %copy-done.1) | copy-start | bytes 1572868
  160.6 6.1 %collective-permute-start.4 = (bf16[512,8,256]{2,0,1:T(8,128)(2,1)}, bf16[512,8,256]{2,0,1:T(8,128)(2,1)S(1)}, u32[]{:S(2)}, u32[]{:S(2)}) collective-permute-start(bf16[512,8,256]{2,0,1:T(8,128)(2,1)} %fusion.8), channel_id=1, source_target_pairs={{0,1},{1,0},{2,3},{3,2},{4,5},{5,4},{6,7},{7,6},{8,9},{9,8},{10,11... | collective-permute-start | bytes 6291464 | tf_op jit(solution)/shard_map/ppermute | solution.py:29
  170.9 99.1 %all-gather.5.cloned.1.call-start = ((), (), s32[]{:S(2)}) async-start(), calls=%async_computation.6 | async-start | bytes 8912896 | tf_op jit(solution)/shard_map/all_gather | solution.py:93
  177.6 2.9 copy-start.4
  180.5 30.7 %copy-start = (f32[512,256]{1,0:T(8,128)S(1)}, f32[512,256]{1,0:T(8,128)}, u32[]{:S(2)}) copy-start(f32[512,256]{1,0:T(8,128)} %param.8) | copy-start | bytes 1572868
Sparse Core Ops, SparseCore 0:
  87.8 55.5 all-gather.2
  171.0 40.1 reduce-scatter.1
  213.5 56.5 all-gather.4

commit v7 on v6

--- a/solution.py
+++ b/solution.py
@@ -67,16 +67,21 @@
             panel_parts, moved[s - 1], 2 * ((x_index - s) % x_count), 0
         )
     column_panel = panel_parts.reshape(HQ, tile_cols)
-    panel_chunks = column_panel.reshape(chip_count, 2, chunk, tile_cols)
-    keep_rows = lax.dynamic_index_in_dim(panel_chunks, core, 1, keepdims=False)
-    send_rows = lax.dynamic_index_in_dim(panel_chunks, 1 - core, 1, keepdims=False)
-    contract = (((1,), (2,)), ((), ()))
-    keep = lax.dot_general(grad_tile, keep_rows, contract, preferred_element_type=jnp.float32)
-    send = lax.dot_general(grad_tile, send_rows, contract, preferred_element_type=jnp.float32)
-    chip_sum = keep + partner(send.astype(jnp.bfloat16)).astype(jnp.float32)
-    left_sum = lax.psum_scatter(
-        chip_sum.astype(jnp.bfloat16), "chip", scatter_dimension=1, tiled=True
-    ).reshape(tile_rows, chunk).astype(jnp.float32)
+    col_index = lax.axis_index(COL)
+    sub = jnp.arange(chunk, dtype=jnp.int32)
+    sub_index = (
+        ((col_index % 2) * (col_count // 2) + sub // slice_rows) * (row_count * slice_rows)
+        + (col_index // 2) * slice_rows
+        + sub % slice_rows
+    )
+    sub_rows = jnp.take(row_block, sub_index, axis=0)
+    left_part = lax.dot_general(
+        row_block, sub_rows, (((1,), (1,)), ((), ())), preferred_element_type=jnp.float32
+    ).astype(jnp.bfloat16)
+    left_part = (
+        left_part.reshape(col_count, row_count, slice_rows, chunk).transpose(1, 0, 2, 3).reshape(HQ, chunk)
+    )
+    left_sum = lax.psum_scatter(left_part, ROW, scatter_dimension=0, tiled=True).astype(jnp.float32)
     panel_reordered = (
         column_panel.reshape(row_count, col_count, slice_rows, tile_cols)
         .transpose(1, 0, 2, 3)

time: 288 us -> 319 us (1.11)
  waiting for transfers between devices: 153 us -> 182 us
  local copies, waits for them, and re-layouts: 14.1 us -> 22.5 us
  matrix products: 35.7 us -> 31.9 us
    reduce_scatter x1, waiting for transfers between devices: 21.2 us -> 57.3 us  [shards(): lax.psum_scatter(left_part, ROW, scatter_dimension=0, tiled=True)]
    gather x0 -> x1, local copies, waits for them, and re-layouts: none -> 6.81 us  [shards(): sub_rows = jnp.take(row_block, sub_index, axis=0)]
    transpose x0 -> x2, local copies, waits for them, and re-layouts: none -> 4.36 us  [the longest x1 2.81 us: shards(): panel_reordered = column_panel.reshape(row_count, col_count, slice_rows,...]
    ppermute x1 -> x0, waiting for transfers between devices: 4 us -> none  [partner(): return lax.ppermute(block, 'core', [(0, 1), (1, 0)])]
    all_gather x1, waiting for transfers between devices: 57 us -> 53.5 us  [shards(): lax.all_gather(left_mixed, COL, axis=1, tiled=True)]
    dot_general x2 -> x1, matrix products: 8.44 us -> 5.88 us  [shards(): lax.dot_general(row_block, sub_rows, (((1,), (1,)), ((), ())), preferred_...]
  transfers between devices with their start and end apart: 9 -> 8, of which waited for: 8 -> 7; matrix products, arithmetic and copies ran while one was open for 9% -> 9% of each run, Pallas kernels for 0% -> 0%
where the time goes in v7:
time: 319 us
  waiting for transfers between devices  182 us (57%)
  matrix products  31.9 us (10%)
  blocking collectives  29 us (9%)
  other arithmetic  27.6 us (9%)
  local copies, waits for them, and re-layouts  22.5 us (7%)
  between operations  14 us (4%)
  starting transfers between devices  12 us (4%)
    reduce_scatter x1, waiting for transfers between devices, shards(): lax.psum_scatter(left_part, ROW, scatter_dimension=0, tiled=True)  57.3 us
    all_gather x1, waiting for transfers between devices, shards(): lax.all_gather(left_mixed, COL, axis=1, tiled=True)  53.5 us
    ppermute x3, waiting for transfers between devices, shards(): lax.ppermute(pair, 'x', [(i, (i + s) % x_count) for i in range(x_count)])  45.3 us
    unnamed x1, other arithmetic  22.8 us
    all_to_all x1, blocking collectives, shards(): lax.all_to_all(row_slice, ROW, split_axis=1, concat_axis=0, tiled=True)  15.8 us
    all_to_all x1, waiting for transfers between devices, shards(): lax.all_to_all(held_rows, COL, split_axis=1, concat_axis=0, tiled=True)  13.9 us
    all_to_all x1, blocking collectives, shards(): lax.all_to_all(grad_tile, COL, split_axis=0, concat_axis=1, tiled=True)  13.2 us
    ppermute x1, waiting for transfers between devices, shards(): other_half = lax.ppermute(grad_tile, 'yh', [(0, 1), (1, 0)])  11.9 us
  transfers between devices with their start and end apart: 8, of which 7 were waited for; matrix products, arithmetic and copies ran while one was open for 9% of the time, Pallas kernels for 0%

profile of v7, /device:TPU:1, one launch (start us, length us, event | category | flops | bytes accessed | tf_op | source)
XLA Modules:
  0.0 318.7 jit_solution(15484728986991232005)
XLA Ops:
  7.2 22.8 %reduce = bf16[524288]{0:T(1024)(128)(2,1)S(1)} reduce(bf16[1,1,524288]{2,1,0:T(2,128)(2,1)} %param.6, bf16[]{:T(256)} %constant.158), dimensions={0,1}, to_apply=%param.6.reduce_sub_computation | reduce | bytes 2097154 | tf_op args[0]
  30.0 0.7 all_to_all.38
  30.6 1.5 copy.26
  32.2 7.8 %all-to-all-start = ((bf16[64,16,512]{2,0,1:T(8,128)(2,1)}), bf16[64,16,512]{2,0,1:T(8,128)(2,1)S(1)}, u32[]{:S(2)}, u32[]{:S(2)}) async-start(bf16[64,16,512]{2,0,1:T(8,128)(2,1)} %copy.26), calls=%async_computation | async-start | bytes 2097152 | tf_op jit(solution)/shard_map/all_to_all | solution.py:48
  40.1 0.7 constant_dynamic-slice_fusion
  41.0 0.7 subtract_bitcast_fusion
  42.0 13.9 %all-to-all-done = bf16[64,16,512]{2,0,1:T(8,128)(2,1)S(1)} async-done(((bf16[64,16,512]{2,0,1:T(8,128)(2,1)}), bf16[64,16,512]{2,0,1:T(8,128)(2,1)S(1)}, u32[]{:S(2)}, u32[]{:S(2)}) %all-to-all-start) | async-done | bytes 1048608 | tf_op jit(solution)/shard_map/all_to_all | solution.py:48
  55.9 2.0 gather_fusion
  58.0 13.2 %all_to_all.51 = bf16[16,32,512]{2,1,0:T(8,128)(2,1)S(1)} all-to-all(bf16[16,32,512]{2,1,0:T(8,128)(2,1)S(1)} %broadcast_select_fusion.1), channel_id=1, replica_groups=mesh['x'=4,'yh'=2,'chip'=8,'core'=2] {'chip','core'}, dimensions={0} | all-to-all | bytes 1048576 | tf_op jit(solution)/shard_map/all_to_all | solution.py:51
  72.0 15.8 %all_to_all.52 = bf16[32,8,1024]{2,0,1:T(8,128)(2,1)} all-to-all(bf16[32,8,1024]{2,0,1:T(8,128)(2,1)S(1)} %copy.28), channel_id=1, replica_groups=mesh['x'=4,'yh'=2,'chip'=8,'core'=2] {'x','yh'}, dimensions={1} | all-to-all | bytes 1048576 | tf_op jit(solution)/shard_map/all_to_all | solution.py:52
  87.9 1.3 collective-permute-start
  89.3 11.9 %collective-permute-done = bf16[512,512]{1,0:T(8,128)(2,1)S(1)} collective-permute-done((bf16[512,512]{1,0:T(8,128)(2,1)S(1)}, bf16[512,512]{1,0:T(8,128)(2,1)S(1)}, u32[]{:S(2)}, u32[]{:S(2)}) %collective-permute-start) | collective-permute-done | bytes 524320 | tf_op jit(solution)/shard_map/ppermute | solution.py:53
  101.3 2.3 broadcast_in_dim.47
  103.6 1.5 constant_dynamic-update-slice_fusion.3
  105.1 0.5 collective-permute-start.2
  105.7 2.1 collective-permute-start.3
  107.8 14.0 %collective-permute-done.1 = bf16[2,512,512]{2,1,0:T(8,128)(2,1)S(1)} collective-permute-done((bf16[2,512,512]{2,1,0:T(8,128)(2,1)}, bf16[2,512,512]{2,1,0:T(8,128)(2,1)S(1)}, u32[]{:S(2)}, u32[]{:S(2)}) %collective-permute-start.1) | collective-permute-done | bytes 1048608 | tf_op jit(solution)/shard_map/ppermute | solution.py:58
  121.8 21.1 %collective-permute-done.2 = bf16[2,512,512]{2,1,0:T(8,128)(2,1)S(1)} collective-permute-done((bf16[2,512,512]{2,1,0:T(8,128)(2,1)}, bf16[2,512,512]{2,1,0:T(8,128)(2,1)S(1)}, u32[]{:S(2)}, u32[]{:S(2)}) %collective-permute-start.2) | collective-permute-done | bytes 1048608 | tf_op jit(solution)/shard_map/ppermute | solution.py:58
  142.9 10.2 %collective-permute-done.3 = bf16[2,512,512]{2,1,0:T(8,128)(2,1)S(1)} collective-permute-done((bf16[2,512,512]{2,1,0:T(8,128)(2,1)}, bf16[2,512,512]{2,1,0:T(8,128)(2,1)S(1)}, u32[]{:S(2)}, u32[]{:S(2)}) %collective-permute-start.3) | collective-permute-done | bytes 1048608 | tf_op jit(solution)/shard_map/ppermute | solution.py:58
  153.1 6.8 %gather_fusion.1 = bf16[256,1024]{1,0:T(8,128)(2,1)} fusion(bf16[4096,1024]{1,0:T(8,128)(2,1)} %all-gather.3.cloned.1.call-done, s32[1024]{0:T(1024)S(1)} %pad_clamp_fusion), kind=kCustom, calls=%fused_computation.1 | custom fusion | bytes 1049600 | tf_op jit(solution)/shard_map/jit(_take)/gather | solution.py:77
  159.9 5.9 %convolution_convert_fusion = bf16[4096,256]{1,0:T(8,128)(2,1)S(1)} fusion(bf16[4096,1024]{1,0:T(8,128)(2,1)} %all-gather.3.cloned.1.call-done, bf16[256,1024]{1,0:T(8,128)(2,1)} %gather_fusion.1, pred[256]{0:T(512)(128)(4,1)S(1)} %compare_and_fusion.1), kind=kOutput, calls=%fused_computation.2 | convolution fusion | flops 2148794368 | bytes 11010304 | tf_op jit(solution)/shard_map/dot_general | solution.py:78
  165.8 1.6 copy.29
  167.5 1.1 constant_dynamic-update-slice_fusion.2
  168.6 1.1 constant_dynamic-update-slice_fusion.1
  169.6 1.1 constant_dynamic-update-slice_fusion
  170.8 5.4 %fusion = bf16[512,512]{0,1:T(8,128)(2,1)} fusion(bf16[4096,512]{1,0:T(8,128)(2,1)} %bitcast.19, bf16[512,4096]{1,0:T(8,128)(2,1)S(1)} %copy-done.1), kind=kOutput, calls=%fused_computation.6 | convolution fusion | flops 2147745792 | bytes 8912896 | tf_op jit(solution)/shard_map/dot_general | solution.py:94
  176.2 2.8 copy.30
  179.1 9.5 %multiply_add_fusion = f32[512,1024]{1,0:T(8,128)} fusion(f32[512,1024]{1,0:T(8,128)S(1)} %copy-done.2, bf16[4096,512]{1,0:T(8,128)(2,1)S(1)} %bitcast.39, bf16[4096,1024]{1,0:T(8,128)(2,1)} %all-gather.3.cloned.1.call-done), kind=kOutput, calls=%fused_computation.3 | convolution fusion | flops 4296540160 | bytes 16777216 | tf_op jit(solution)/shard_map/dot_general | solution.py:90
  188.5 57.3 %reduce-scatter.2.cloned.1.call-done = bf16[512,256]{1,0:T(8,128)(2,1)} async-done(((bf16[4096,256]{1,0:T(8,128)(2,1)}), bf16[512,256]{1,0:T(8,128)(2,1)}) %reduce-scatter.2.cloned.1.call-update) | async-done | bytes 262160 | tf_op jit(solution)/shard_map/reduce_scatter | solution.py:84
  245.8 1.8 multiply_add_fusion.1
  247.6 53.5 %all-gather.5.cloned.1.call-done = bf16[512,8192]{0,1:T(8,128)(2,1)} async-done(((bf16[512,512]{0,1:T(8,128)(2,1)}), bf16[512,8192]{0,1:T(8,128)(2,1)}) %all-gather.5.cloned.1.call-update) | async-done | bytes 8388624 | tf_op jit(solution)/shard_map/all_gather | solution.py:98
  301.1 11.1 %convolution_convert_fusion.1 = bf16[512,512]{1,0:T(8,128)(2,1)} fusion(bf16[512,8192]{0,1:T(8,128)(2,1)} %all-gather.5.cloned.1.call-done, bf16[512,8192]{1,0:T(8,128)(2,1)} %param.11), kind=kOutput, calls=%fused_computation.4 | convolution fusion | flops 4295229440 | bytes 17301504 | tf_op jit(solution)/shard_map/dot_general | solution.py:97
  (32 shorter events, 1.9 us)
Async XLA Ops:
  32.2 23.7 %all-to-all-start = ((bf16[64,16,512]{2,0,1:T(8,128)(2,1)}), bf16[64,16,512]{2,0,1:T(8,128)(2,1)S(1)}, u32[]{:S(2)}, u32[]{:S(2)}) async-start(bf16[64,16,512]{2,0,1:T(8,128)(2,1)} %copy.26), calls=%async_computation | async-start | bytes 2097152 | tf_op jit(solution)/shard_map/all_to_all | solution.py:48
  40.0 113.1 %all-gather.3.cloned.1.call-start = ((), (), s32[]{:S(2)}) async-start(), calls=%async_computation.4 | async-start | bytes 8912896 | tf_op jit(solution)/shard_map/all_gather | solution.py:61
  87.7 158.0 %reduce-scatter.2.cloned.1.call-start = ((), (), s32[]{:S(2)}) async-start(), calls=%async_computation.5 | async-start | bytes 2359296 | tf_op jit(solution)/shard_map/reduce_scatter | solution.py:84
  87.9 13.2 %collective-permute-start = (bf16[512,512]{1,0:T(8,128)(2,1)S(1)}, bf16[512,512]{1,0:T(8,128)(2,1)S(1)}, u32[]{:S(2)}, u32[]{:S(2)}) collective-permute-start(bf16[512,512]{1,0:T(8,128)(2,1)S(1)} %broadcast_select_fusion), channel_id=1, source_target_pairs={{0,16},{16,0},{1,17},{17,1},{2,18},{18,2},{3,19},{19,3},{4,20},{20... | collective-permute-start | bytes 1572872 | tf_op jit(solution)/shard_map/ppermute | solution.py:53
  105.1 16.7 %collective-permute-start.1 = (bf16[2,512,512]{2,1,0:T(8,128)(2,1)}, bf16[2,512,512]{2,1,0:T(8,128)(2,1)S(1)}, u32[]{:S(2)}, u32[]{:S(2)}) collective-permute-start(bf16[2,512,512]{2,1,0:T(8,128)(2,1)} %get-tuple-element.14), channel_id=1, source_target_pairs={{0,32},{32,64},{64,96},{96,0},{1,33},{33,65},{65,97},{97,1},{2,34}... | collective-permute-start | bytes 3145736 | tf_op jit(solution)/shard_map/ppermute | solution.py:58
  105.1 37.8 %collective-permute-start.2 = (bf16[2,512,512]{2,1,0:T(8,128)(2,1)}, bf16[2,512,512]{2,1,0:T(8,128)(2,1)S(1)}, u32[]{:S(2)}, u32[]{:S(2)}) collective-permute-start(bf16[2,512,512]{2,1,0:T(8,128)(2,1)} %get-tuple-element.14), channel_id=1, source_target_pairs={{0,64},{32,96},{64,0},{96,32},{1,65},{33,97},{65,1},{97,33},{2,66}... | collective-permute-start | bytes 3145736 | tf_op jit(solution)/shard_map/ppermute | solution.py:58
  105.7 47.4 %collective-permute-start.3 = (bf16[2,512,512]{2,1,0:T(8,128)(2,1)}, bf16[2,512,512]{2,1,0:T(8,128)(2,1)S(1)}, u32[]{:S(2)}, u32[]{:S(2)}) collective-permute-start(bf16[2,512,512]{2,1,0:T(8,128)(2,1)} %get-tuple-element.14), channel_id=1, source_target_pairs={{0,96},{32,0},{64,32},{96,64},{1,97},{33,1},{65,33},{97,65},{2,98}... | collective-permute-start | bytes 3145736 | tf_op jit(solution)/shard_map/ppermute | solution.py:58
  167.4 133.7 %all-gather.5.cloned.1.call-start = ((), (), s32[]{:S(2)}) async-start(), calls=%async_computation.6 | async-start | bytes 8912896 | tf_op jit(solution)/shard_map/all_gather | solution.py:98
  167.5 3.3 %copy-start.1 = (bf16[512,4096]{1,0:T(8,128)(2,1)S(1)}, bf16[512,4096]{1,0:T(8,128)(2,1)}, u32[]{:S(2)}) copy-start(bf16[512,4096]{1,0:T(8,128)(2,1)} %param.10) | copy-start | bytes 12582916
  176.2 2.9 copy-start.2
  179.1 66.7 %copy-start = (f32[512,256]{1,0:T(8,128)S(1)}, f32[512,256]{1,0:T(8,128)}, u32[]{:S(2)}) copy-start(f32[512,256]{1,0:T(8,128)} %param.8) | copy-start | bytes 1572868
Sparse Core Ops, SparseCore 0:
  87.8 55.5 all-gather.2
  167.5 78.2 reduce-scatter.1
  248.2 52.8 all-gather.4

commit v8 on v6

--- a/solution.py
+++ b/solution.py
@@ -74,9 +74,16 @@
     keep = lax.dot_general(grad_tile, keep_rows, contract, preferred_element_type=jnp.float32)
     send = lax.dot_general(grad_tile, send_rows, contract, preferred_element_type=jnp.float32)
     chip_sum = keep + partner(send.astype(jnp.bfloat16)).astype(jnp.float32)
-    left_sum = lax.psum_scatter(
-        chip_sum.astype(jnp.bfloat16), "chip", scatter_dimension=1, tiled=True
-    ).reshape(tile_rows, chunk).astype(jnp.float32)
+    chip_index = lax.axis_index("chip")
+    outgoing = chip_sum.astype(jnp.bfloat16).transpose(1, 0, 2)
+    incoming = [
+        lax.ppermute(
+            lax.dynamic_index_in_dim(outgoing, (chip_index + s) % chip_count, 0, keepdims=False),
+            "chip",
+            [(i, (i + s) % chip_count) for i in range(chip_count)],
+        )
+        for s in range(1, chip_count)
+    ]
     panel_reordered = (
         column_panel.reshape(row_count, col_count, slice_rows, tile_cols)
         .transpose(1, 0, 2, 3)
@@ -89,8 +96,13 @@
     left_mixed = jnp.dot(left_root, column_panel, preferred_element_type=jnp.float32).astype(
         jnp.bfloat16
     )
+    mixed_rows = lax.all_gather(left_mixed, COL, axis=1, tiled=True)
+    incoming, mixed_rows = lax.optimization_barrier((incoming, mixed_rows))
+    left_sum = lax.dynamic_index_in_dim(chip_sum, chip_index, 1, keepdims=False)
+    for part in incoming:
+        left_sum = left_sum + part.astype(jnp.float32)
     update_sum = lax.dot_general(
-        lax.all_gather(left_mixed, COL, axis=1, tiled=True),
+        mixed_rows,
         right_root,
         (((1,), (1,)), ((), ())),
         preferred_element_type=jnp.float32,

time: 288 us -> 266 us (0.924)
  waiting for transfers between devices: 153 us -> 112 us
  starting transfers between devices: 14.1 us -> 30.9 us
    all_gather x1, waiting for transfers between devices: 57 us -> 20.4 us  [shards(): mixed_rows = lax.all_gather(left_mixed, COL, axis=1, tiled=True)]
    reduce_scatter x1 -> x0, waiting for transfers between devices: 21.2 us -> none  [shards(): lax.psum_scatter(chip_sum.astype(jnp.bfloat16), 'chip', scatter_dimension...]
    ppermute x0 -> x7, waiting for transfers between devices: none -> 16.8 us  [shards(): lax.ppermute(lax.dynamic_index_in_dim(outgoing, (chip_index + s) % chip_c...]
    ppermute x0 -> x7, starting transfers between devices: none -> 16.8 us  [shards(): lax.ppermute(lax.dynamic_index_in_dim(outgoing, (chip_index + s) % chip_c...]
  transfers between devices with their start and end apart: 9 -> 15, of which waited for: 8 -> 10; matrix products, arithmetic and copies ran while one was open for 9% -> 11% of each run, Pallas kernels for 0% -> 0%
where the time goes in v8:
time: 266 us
  waiting for transfers between devices  112 us (42%)
  matrix products  34.9 us (13%)
  starting transfers between devices  30.9 us (12%)
  blocking collectives  29 us (11%)
  other arithmetic  27.9 us (10%)
  local copies, waits for them, and re-layouts  16.4 us (6%)
  between operations  14.2 us (5%)
    ppermute x3, waiting for transfers between devices, shards(): lax.ppermute(pair, 'x', [(i, (i + s) % x_count) for i in range(x_count)])  45.3 us
    unnamed x1, other arithmetic  22.8 us
    all_gather x1, waiting for transfers between devices, shards(): mixed_rows = lax.all_gather(left_mixed, COL, axis=1, tiled=True)  20.4 us
    ppermute x7, waiting for transfers between devices, shards(): lax.ppermute(lax.dynamic_index_in_dim(outgoing, (chip_index + s) % chip_c...  16.8 us
    ppermute x7, starting transfers between devices, shards(): lax.ppermute(lax.dynamic_index_in_dim(outgoing, (chip_index + s) % chip_c...  16.8 us
    all_to_all x1, blocking collectives, shards(): lax.all_to_all(row_slice, ROW, split_axis=1, concat_axis=0, tiled=True)  15.8 us
    all_to_all x1, waiting for transfers between devices, shards(): lax.all_to_all(held_rows, COL, split_axis=1, concat_axis=0, tiled=True)  13.9 us
    all_to_all x1, blocking collectives, shards(): lax.all_to_all(grad_tile, COL, split_axis=0, concat_axis=1, tiled=True)  13.2 us
  transfers between devices with their start and end apart: 15, of which 10 were waited for; matrix products, arithmetic and copies ran while one was open for 11% of the time, Pallas kernels for 0%

profile of v8, /device:TPU:1, one launch (start us, length us, event | category | flops | bytes accessed | tf_op | source)
XLA Modules:
  0.0 265.5 jit_solution(16899076636767929168)
XLA Ops:
  7.2 22.8 %reduce = bf16[524288]{0:T(1024)(128)(2,1)S(1)} reduce(bf16[1,1,524288]{2,1,0:T(2,128)(2,1)} %param.6, bf16[]{:T(256)} %constant.157), dimensions={0,1}, to_apply=%param.6.reduce_sub_computation | reduce | bytes 2097154 | tf_op args[0]
  30.6 1.5 copy.23
  32.2 7.8 %all-to-all-start = ((bf16[64,16,512]{2,0,1:T(8,128)(2,1)}), bf16[64,16,512]{2,0,1:T(8,128)(2,1)S(1)}, u32[]{:S(2)}, u32[]{:S(2)}) async-start(bf16[64,16,512]{2,0,1:T(8,128)(2,1)} %copy.23), calls=%async_computation | async-start | bytes 2097152 | tf_op jit(solution)/shard_map/all_to_all | solution.py:48
  42.0 13.9 %all-to-all-done = bf16[64,16,512]{2,0,1:T(8,128)(2,1)S(1)} async-done(((bf16[64,16,512]{2,0,1:T(8,128)(2,1)}), bf16[64,16,512]{2,0,1:T(8,128)(2,1)S(1)}, u32[]{:S(2)}, u32[]{:S(2)}) %all-to-all-start) | async-done | bytes 1048608 | tf_op jit(solution)/shard_map/all_to_all | solution.py:48
  55.9 2.0 gather_fusion
  58.0 13.2 %all_to_all.51 = bf16[16,32,512]{2,1,0:T(8,128)(2,1)S(1)} all-to-all(bf16[16,32,512]{2,1,0:T(8,128)(2,1)S(1)} %broadcast_select_fusion.1), channel_id=1, replica_groups=mesh['x'=4,'yh'=2,'chip'=8,'core'=2] {'chip','core'}, dimensions={0} | all-to-all | bytes 1048576 | tf_op jit(solution)/shard_map/all_to_all | solution.py:51
  72.0 15.8 %all_to_all.52 = bf16[32,8,1024]{2,0,1:T(8,128)(2,1)} all-to-all(bf16[32,8,1024]{2,0,1:T(8,128)(2,1)S(1)} %copy.25), channel_id=1, replica_groups=mesh['x'=4,'yh'=2,'chip'=8,'core'=2] {'x','yh'}, dimensions={1} | all-to-all | bytes 1048576 | tf_op jit(solution)/shard_map/all_to_all | solution.py:52
  87.9 1.3 collective-permute-start
  89.3 11.9 %collective-permute-done = bf16[512,512]{1,0:T(8,128)(2,1)S(1)} collective-permute-done((bf16[512,512]{1,0:T(8,128)(2,1)S(1)}, bf16[512,512]{1,0:T(8,128)(2,1)S(1)}, u32[]{:S(2)}, u32[]{:S(2)}) %collective-permute-start) | collective-permute-done | bytes 524320 | tf_op jit(solution)/shard_map/ppermute | solution.py:53
  101.3 2.3 broadcast_in_dim.33
  103.7 1.5 pad_maximum_fusion
  105.8 2.1 collective-permute-start.3
  107.9 13.9 %collective-permute-done.1 = bf16[2,512,512]{2,1,0:T(8,128)(2,1)S(1)} collective-permute-done((bf16[2,512,512]{2,1,0:T(8,128)(2,1)}, bf16[2,512,512]{2,1,0:T(8,128)(2,1)S(1)}, u32[]{:S(2)}, u32[]{:S(2)}) %collective-permute-start.1) | collective-permute-done | bytes 1048608 | tf_op jit(solution)/shard_map/ppermute | solution.py:58
  121.8 21.3 %collective-permute-done.2 = bf16[2,512,512]{2,1,0:T(8,128)(2,1)S(1)} collective-permute-done((bf16[2,512,512]{2,1,0:T(8,128)(2,1)}, bf16[2,512,512]{2,1,0:T(8,128)(2,1)S(1)}, u32[]{:S(2)}, u32[]{:S(2)}) %collective-permute-start.2) | collective-permute-done | bytes 1048608 | tf_op jit(solution)/shard_map/ppermute | solution.py:58
  143.1 10.1 %collective-permute-done.3 = bf16[2,512,512]{2,1,0:T(8,128)(2,1)} collective-permute-done((bf16[2,512,512]{2,1,0:T(8,128)(2,1)}, bf16[2,512,512]{2,1,0:T(8,128)(2,1)}, u32[]{:S(2)}, u32[]{:S(2)}) %collective-permute-start.3) | collective-permute-done | bytes 1048608 | tf_op jit(solution)/shard_map/ppermute | solution.py:58
  155.4 2.3 constant_dynamic-update-slice_fusion
  157.7 5.4 %fusion.11 = bf16[512,512]{0,1:T(8,128)(2,1)} fusion(bf16[4096,512]{1,0:T(8,128)(2,1)} %bitcast.24, bf16[512,4096]{1,0:T(8,128)(2,1)S(1)} %copy-done.1), kind=kOutput, calls=%fused_computation.12 | convolution fusion | flops 2147745792 | bytes 8912896 | tf_op jit(solution)/shard_map/dot_general | solution.py:96
  163.1 4.2 %fusion.8 = bf16[512,8,256]{2,0,1:T(8,128)(2,1)} fusion(bf16[8,2,256,512]{3,2,1,0:T(8,128)(2,1)} %bitcast.13, s32[]{:T(128)S(6)} %select_n.152, bf16[512,512]{1,0:T(8,128)(2,1)S(1)} %broadcast_select_fusion), kind=kOutput, calls=%fused_computation.9 | convolution fusion | flops 1074790400 | bytes 4718596 | tf_op jit(solution)/shard_map/dot_general | solution.py:75
  167.3 2.2 collective-permute-start.4
  169.5 4.0 %collective-permute-done.4 = bf16[512,8,256]{2,0,1:T(8,128)(2,1)S(1)} collective-permute-done((bf16[512,8,256]{2,0,1:T(8,128)(2,1)}, bf16[512,8,256]{2,0,1:T(8,128)(2,1)S(1)}, u32[]{:S(2)}, u32[]{:S(2)}) %collective-permute-start.4) | collective-permute-done | bytes 2097184 | tf_op jit(solution)/shard_map/ppermute | solution.py:29
  173.5 4.8 %fusion.24 = (bf16[512,8,256]{2,0,1:T(8,128)(2,1)S(1)}, f32[512,8,256]{2,0,1:T(8,128)}) fusion(bf16[512,8,256]{2,0,1:T(8,128)(2,1)S(1)} %collective-permute-done.4, bf16[8,2,256,512]{3,2,1,0:T(8,128)(2,1)} %bitcast.13, s32[]{:T(128)S(6)} %select_n.151, bf16[512,512]{1,0:T(8,128)(2,1)S(1)} %broadcast_select_fusion), kind=kOutput, calls=%fused_computation.54 | convolution fusion | flops 1076887552 | bytes 11010052 | tf_op jit(solution)/shard_map/dot_general | solution.py:74
  179.2 1.3 collective-permute-start.10
  181.5 2.9 %copy.26 = bf16[8,16,32,512]{3,2,0,1:T(8,128)(2,1)S(1)} copy(bf16[8,16,32,512]{3,2,1,0:T(8,128)(2,1)} %bitcast.26) | data formatting | bytes 8388608 | tf_op jit(solution)/shard_map/reshape;reshape | solution.py:88
  184.8 3.0 %collective-permute-start.6 = (bf16[512,256]{1,0:T(8,128)(2,1)S(1)}, bf16[512,256]{1,0:T(8,128)(2,1)S(1)}, u32[]{:S(2)}, u32[]{:S(2)}) collective-permute-start(bf16[512,256]{1,0:T(8,128)(2,1)S(1)} %get-tuple-element.34), channel_id=1, source_target_pairs={{0,4},{2,6},{4,8},{6,10},{8,12},{10,14},{12,0},{14,2},{1,5},{3,7},... | collective-permute-start | bytes 786440 | tf_op jit(solution)/shard_map/ppermute | solution.py:80
  187.8 3.6 %collective-permute-start.7 = (bf16[512,256]{1,0:T(8,128)(2,1)S(1)}, bf16[512,256]{1,0:T(8,128)(2,1)S(1)}, u32[]{:S(2)}, u32[]{:S(2)}) collective-permute-start(bf16[512,256]{1,0:T(8,128)(2,1)S(1)} %get-tuple-element.33), channel_id=1, source_target_pairs={{0,6},{2,8},{4,10},{6,12},{8,14},{10,0},{12,2},{14,4},{1,7},{3,9},... | collective-permute-start | bytes 786440 | tf_op jit(solution)/shard_map/ppermute | solution.py:80
  191.5 12.3 %collective-permute-done.10 = bf16[512,256]{1,0:T(8,128)(2,1)S(1)} collective-permute-done((bf16[512,256]{1,0:T(8,128)(2,1)S(1)}, bf16[512,256]{1,0:T(8,128)(2,1)S(1)}, u32[]{:S(2)}, u32[]{:S(2)}) %collective-permute-start.10) | collective-permute-done | bytes 262176 | tf_op jit(solution)/shard_map/ppermute | solution.py:80
  205.3 6.7 %collective-permute-start.9 = (bf16[512,256]{1,0:T(8,128)(2,1)S(1)}, bf16[512,256]{1,0:T(8,128)(2,1)S(1)}, u32[]{:S(2)}, u32[]{:S(2)}) collective-permute-start(bf16[512,256]{1,0:T(8,128)(2,1)S(1)} %get-tuple-element.31), channel_id=1, source_target_pairs={{0,10},{2,12},{4,14},{6,0},{8,2},{10,4},{12,6},{14,8},{1,11},{3,13... | collective-permute-start | bytes 786440 | tf_op jit(solution)/shard_map/ppermute | solution.py:80
  212.1 9.3 %multiply_add_fusion = f32[512,1024]{1,0:T(8,128)} fusion(f32[512,1024]{1,0:T(8,128)S(1)} %copy-done.2, bf16[4096,512]{1,0:T(8,128)(2,1)S(1)} %bitcast.84, bf16[4096,1024]{1,0:T(8,128)(2,1)} %all-gather.3.cloned.1.call-done), kind=kOutput, calls=%fused_computation.6 | convolution fusion | flops 4296540160 | bytes 16777216 | tf_op jit(solution)/shard_map/dot_general | solution.py:92
  221.4 3.7 %collective-permute-done.9 = bf16[512,256]{1,0:T(8,128)(2,1)S(1)} collective-permute-done((bf16[512,256]{1,0:T(8,128)(2,1)S(1)}, bf16[512,256]{1,0:T(8,128)(2,1)S(1)}, u32[]{:S(2)}, u32[]{:S(2)}) %collective-permute-start.9) | collective-permute-done | bytes 262176 | tf_op jit(solution)/shard_map/ppermute | solution.py:80
  225.0 20.4 %all-gather.5.cloned.1.call-done = bf16[512,8192]{0,1:T(8,128)(2,1)} async-done(((bf16[512,512]{0,1:T(8,128)(2,1)}), bf16[512,8192]{0,1:T(8,128)(2,1)}) %all-gather.5.cloned.1.call-update) | async-done | bytes 8388624 | tf_op jit(solution)/shard_map/all_gather | solution.py:99
  245.4 11.1 %convolution_convert_fusion = bf16[512,512]{1,0:T(8,128)(2,1)} fusion(bf16[512,8192]{0,1:T(8,128)(2,1)} %all-gather.5.cloned.1.call-done, bf16[512,8192]{1,0:T(8,128)(2,1)} %param.11), kind=kOutput, calls=%fused_computation.10 | convolution fusion | flops 4295229440 | bytes 17301504 | tf_op jit(solution)/shard_map/dot_general | solution.py:104
  256.5 2.1 fusion.19
  (42 shorter events, 10.6 us)
Async XLA Ops:
  32.2 23.7 %all-to-all-start = ((bf16[64,16,512]{2,0,1:T(8,128)(2,1)}), bf16[64,16,512]{2,0,1:T(8,128)(2,1)S(1)}, u32[]{:S(2)}, u32[]{:S(2)}) async-start(bf16[64,16,512]{2,0,1:T(8,128)(2,1)} %copy.23), calls=%async_computation | async-start | bytes 2097152 | tf_op jit(solution)/shard_map/all_to_all | solution.py:48
  40.0 113.2 %all-gather.3.cloned.1.call-start = ((), (), s32[]{:S(2)}) async-start(), calls=%async_computation.3 | async-start | bytes 8912896 | tf_op jit(solution)/shard_map/all_gather | solution.py:61
  87.7 157.7 %all-gather.5.cloned.1.call-start = ((), (), s32[]{:S(2)}) async-start(), calls=%async_computation.4 | async-start | bytes 8912896 | tf_op jit(solution)/shard_map/all_gather | solution.py:99
  87.9 13.2 %collective-permute-start = (bf16[512,512]{1,0:T(8,128)(2,1)S(1)}, bf16[512,512]{1,0:T(8,128)(2,1)S(1)}, u32[]{:S(2)}, u32[]{:S(2)}) collective-permute-start(bf16[512,512]{1,0:T(8,128)(2,1)S(1)} %broadcast_select_fusion), channel_id=1, source_target_pairs={{0,16},{16,0},{1,17},{17,1},{2,18},{18,2},{3,19},{19,3},{4,20},{20... | collective-permute-start | bytes 1572872 | tf_op jit(solution)/shard_map/ppermute | solution.py:53
  105.2 16.6 %collective-permute-start.1 = (bf16[2,512,512]{2,1,0:T(8,128)(2,1)}, bf16[2,512,512]{2,1,0:T(8,128)(2,1)S(1)}, u32[]{:S(2)}, u32[]{:S(2)}) collective-permute-start(bf16[2,512,512]{2,1,0:T(8,128)(2,1)} %get-tuple-element.36), channel_id=1, source_target_pairs={{0,32},{32,64},{64,96},{96,0},{1,33},{33,65},{65,97},{97,1},{2,34}... | collective-permute-start | bytes 3145736 | tf_op jit(solution)/shard_map/ppermute | solution.py:58
  105.2 37.9 %collective-permute-start.2 = (bf16[2,512,512]{2,1,0:T(8,128)(2,1)}, bf16[2,512,512]{2,1,0:T(8,128)(2,1)S(1)}, u32[]{:S(2)}, u32[]{:S(2)}) collective-permute-start(bf16[2,512,512]{2,1,0:T(8,128)(2,1)} %get-tuple-element.36), channel_id=1, source_target_pairs={{0,64},{32,96},{64,0},{96,32},{1,65},{33,97},{65,1},{97,33},{2,66}... | collective-permute-start | bytes 3145736 | tf_op jit(solution)/shard_map/ppermute | solution.py:58
  105.8 47.4 %collective-permute-start.3 = (bf16[2,512,512]{2,1,0:T(8,128)(2,1)}, bf16[2,512,512]{2,1,0:T(8,128)(2,1)}, u32[]{:S(2)}, u32[]{:S(2)}) collective-permute-start(bf16[2,512,512]{2,1,0:T(8,128)(2,1)} %get-tuple-element.36), channel_id=1, source_target_pairs={{0,96},{32,0},{64,32},{96,64},{1,97},{33,1},{65,33},{97,65},{2,98}... | collective-permute-start | bytes 3145736 | tf_op jit(solution)/shard_map/ppermute | solution.py:58
  153.2 4.5 %copy-start.1 = (bf16[512,4096]{1,0:T(8,128)(2,1)S(1)}, bf16[512,4096]{1,0:T(8,128)(2,1)}, u32[]{:S(2)}) copy-start(bf16[512,4096]{1,0:T(8,128)(2,1)} %param.10) | copy-start | bytes 12582916
  167.3 6.2 %collective-permute-start.4 = (bf16[512,8,256]{2,0,1:T(8,128)(2,1)}, bf16[512,8,256]{2,0,1:T(8,128)(2,1)S(1)}, u32[]{:S(2)}, u32[]{:S(2)}) collective-permute-start(bf16[512,8,256]{2,0,1:T(8,128)(2,1)} %fusion.8), channel_id=1, source_target_pairs={{0,1},{1,0},{2,3},{3,2},{4,5},{5,4},{6,7},{7,6},{8,9},{9,8},{10,11... | collective-permute-start | bytes 6291464 | tf_op jit(solution)/shard_map/ppermute | solution.py:29
  179.2 24.6 %collective-permute-start.10 = (bf16[512,256]{1,0:T(8,128)(2,1)S(1)}, bf16[512,256]{1,0:T(8,128)(2,1)S(1)}, u32[]{:S(2)}, u32[]{:S(2)}) collective-permute-start(bf16[512,256]{1,0:T(8,128)(2,1)S(1)} %get-tuple-element.30), channel_id=1, source_target_pairs={{0,12},{2,14},{4,0},{6,2},{8,4},{10,6},{12,8},{14,10},{1,13},{3,15... | collective-permute-start | bytes 786440 | tf_op jit(solution)/shard_map/ppermute | solution.py:80
  180.5 24.9 %collective-permute-start.11 = (bf16[512,256]{1,0:T(8,128)(2,1)S(1)}, bf16[512,256]{1,0:T(8,128)(2,1)S(1)}, u32[]{:S(2)}, u32[]{:S(2)}) collective-permute-start(bf16[512,256]{1,0:T(8,128)(2,1)S(1)} %get-tuple-element.29), channel_id=1, source_target_pairs={{0,14},{2,0},{4,2},{6,4},{8,6},{10,8},{12,10},{14,12},{1,15},{3,1}... | collective-permute-start | bytes 786440 | tf_op jit(solution)/shard_map/ppermute | solution.py:80
  181.5 30.6 %copy-start.2 = (f32[512,1024]{1,0:T(8,128)S(1)}, f32[512,1024]{1,0:T(8,128)}, u32[]{:S(2)}) copy-start(f32[512,1024]{1,0:T(8,128)} %param.9) | copy-start | bytes 6291460
  184.4 36.9 %collective-permute-start.5 = (bf16[512,256]{1,0:T(8,128)(2,1)}, bf16[512,256]{1,0:T(8,128)(2,1)S(1)}, u32[]{:S(2)}, u32[]{:S(2)}) collective-permute-start(bf16[512,256]{1,0:T(8,128)(2,1)} %get-tuple-element.35), channel_id=1, source_target_pairs={{0,2},{2,4},{4,6},{6,8},{8,10},{10,12},{12,14},{14,0},{1,3},{3,5},... | collective-permute-start | bytes 786440 | tf_op jit(solution)/shard_map/ppermute | solution.py:80
  184.8 36.5 %collective-permute-start.6 = (bf16[512,256]{1,0:T(8,128)(2,1)S(1)}, bf16[512,256]{1,0:T(8,128)(2,1)S(1)}, u32[]{:S(2)}, u32[]{:S(2)}) collective-permute-start(bf16[512,256]{1,0:T(8,128)(2,1)S(1)} %get-tuple-element.34), channel_id=1, source_target_pairs={{0,4},{2,6},{4,8},{6,10},{8,12},{10,14},{12,0},{14,2},{1,5},{3,7},... | collective-permute-start | bytes 786440 | tf_op jit(solution)/shard_map/ppermute | solution.py:80
  187.8 33.5 %collective-permute-start.7 = (bf16[512,256]{1,0:T(8,128)(2,1)S(1)}, bf16[512,256]{1,0:T(8,128)(2,1)S(1)}, u32[]{:S(2)}, u32[]{:S(2)}) collective-permute-start(bf16[512,256]{1,0:T(8,128)(2,1)S(1)} %get-tuple-element.33), channel_id=1, source_target_pairs={{0,6},{2,8},{4,10},{6,12},{8,14},{10,0},{12,2},{14,4},{1,7},{3,9},... | collective-permute-start | bytes 786440 | tf_op jit(solution)/shard_map/ppermute | solution.py:80
  203.7 17.6 %collective-permute-start.8 = (bf16[512,256]{1,0:T(8,128)(2,1)S(1)}, bf16[512,256]{1,0:T(8,128)(2,1)S(1)}, u32[]{:S(2)}, u32[]{:S(2)}) collective-permute-start(bf16[512,256]{1,0:T(8,128)(2,1)S(1)} %get-tuple-element.32), channel_id=1, source_target_pairs={{0,8},{2,10},{4,12},{6,14},{8,0},{10,2},{12,4},{14,6},{1,9},{3,11}... | collective-permute-start | bytes 786440 | tf_op jit(solution)/shard_map/ppermute | solution.py:80
  205.3 19.7 %collective-permute-start.9 = (bf16[512,256]{1,0:T(8,128)(2,1)S(1)}, bf16[512,256]{1,0:T(8,128)(2,1)S(1)}, u32[]{:S(2)}, u32[]{:S(2)}) collective-permute-start(bf16[512,256]{1,0:T(8,128)(2,1)S(1)} %get-tuple-element.31), channel_id=1, source_target_pairs={{0,10},{2,12},{4,14},{6,0},{8,2},{10,4},{12,6},{14,8},{1,11},{3,13... | collective-permute-start | bytes 786440 | tf_op jit(solution)/shard_map/ppermute | solution.py:80
  221.3 35.2 %copy-start = (f32[512,256]{1,0:T(8,128)S(1)}, f32[512,256]{1,0:T(8,128)}, u32[]{:S(2)}) copy-start(f32[512,256]{1,0:T(8,128)} %param.8) | copy-start | bytes 1572868
Sparse Core Ops, SparseCore 0:
  87.8 55.5 all-gather.2
  163.2 82.1 all-gather.4

commit v9 on v8

--- a/solution.py
+++ b/solution.py
@@ -96,17 +96,21 @@
     left_mixed = jnp.dot(left_root, column_panel, preferred_element_type=jnp.float32).astype(
         jnp.bfloat16
     )
-    mixed_rows = lax.all_gather(left_mixed, COL, axis=1, tiled=True)
-    incoming, mixed_rows = lax.optimization_barrier((incoming, mixed_rows))
+    own_mixed = lax.all_gather(left_mixed, "chip", axis=1, tiled=True)
+    incoming, own_mixed = lax.optimization_barrier((incoming, own_mixed))
+    other_mixed = partner(own_mixed)
     left_sum = lax.dynamic_index_in_dim(chip_sum, chip_index, 1, keepdims=False)
     for part in incoming:
         left_sum = left_sum + part.astype(jnp.float32)
+    root_blocks = right_root.reshape(tile_cols, chip_count, 2, tile_cols)
+    own_root = lax.dynamic_index_in_dim(root_blocks, core, 2, keepdims=False).reshape(tile_cols, DIN // 2)
+    other_root = lax.dynamic_index_in_dim(root_blocks, 1 - core, 2, keepdims=False).reshape(
+        tile_cols, DIN // 2
+    )
+    contract_cols = (((1,), (1,)), ((), ()))
     update_sum = lax.dot_general(
-        mixed_rows,
-        right_root,
-        (((1,), (1,)), ((), ())),
-        preferred_element_type=jnp.float32,
-    )
+        own_mixed, own_root, contract_cols, preferred_element_type=jnp.float32
+    ) + lax.dot_general(other_mixed, other_root, contract_cols, preferred_element_type=jnp.float32)
     left_new = stat_decay * left_stat + left_sum * (1.0 / math.sqrt(DIN))
     return (left_new, right_new, update_sum.astype(jnp.bfloat16))
 

time: 266 us -> 291 us (1.094)
  waiting for transfers between devices: 112 us -> 128 us
  local copies, waits for them, and re-layouts: 16.4 us -> 31.4 us
  matrix products: 34.9 us -> 31.6 us
  starting transfers between devices: 30.9 us -> 27.7 us
    ppermute x7, waiting for transfers between devices: 16.8 us -> 42.8 us  [shards(): lax.ppermute(lax.dynamic_index_in_dim(outgoing, (chip_index + s) % chip_c...]
    unnamed x6 -> x9, local copies, waits for them, and re-layouts: 0.01 us -> 11.6 us
    all_gather x1, waiting for transfers between devices: 20.4 us -> 9.47 us  [shards(): own_mixed = lax.all_gather(left_mixed, 'chip', axis=1, tiled=True)]
    dynamic_slice x0 -> x1, local copies, waits for them, and re-layouts: none -> 4.32 us  [shards(): lax.dynamic_index_in_dim(root_blocks, core, 2, keepdims=False)]
    dot_general x1 -> x2, matrix products: 11.1 us -> 7.85 us  [the longest x1 4.68 us: shards(): lax.dot_general(other_mixed, other_root, contract_cols, preferred_element...]
  transfers between devices with their start and end apart: 15 -> 16, of which waited for: 10 -> 10; matrix products, arithmetic and copies ran while one was open for 11% -> 16% of each run, Pallas kernels for 0% -> 0%
where the time goes in v9:
time: 291 us; the launch traced here: 290 us
  waiting for transfers between devices  128 us (44%)
  matrix products  31.6 us (11%)
  local copies, waits for them, and re-layouts  31.4 us (11%)
  blocking collectives  29 us (10%)
  other arithmetic  27.9 us (10%)
  starting transfers between devices  27.7 us (10%)
  between operations  14.2 us (5%)
    ppermute x3, waiting for transfers between devices, shards(): lax.ppermute(pair, 'x', [(i, (i + s) % x_count) for i in range(x_count)])  46.4 us
    ppermute x7, waiting for transfers between devices, shards(): lax.ppermute(lax.dynamic_index_in_dim(outgoing, (chip_index + s) % chip_c...  42.8 us
    unnamed x1, other arithmetic  22.8 us
    all_to_all x1, blocking collectives, shards(): lax.all_to_all(row_slice, ROW, split_axis=1, concat_axis=0, tiled=True)  15.8 us
    ppermute x7, starting transfers between devices, shards(): lax.ppermute(lax.dynamic_index_in_dim(outgoing, (chip_index + s) % chip_c...  13.9 us
    all_to_all x1, waiting for transfers between devices, shards(): lax.all_to_all(held_rows, COL, split_axis=1, concat_axis=0, tiled=True)  13.9 us
    all_to_all x1, blocking collectives, shards(): lax.all_to_all(grad_tile, COL, split_axis=0, concat_axis=1, tiled=True)  13.2 us
    ppermute x1, waiting for transfers between devices, shards(): other_half = lax.ppermute(grad_tile, 'yh', [(0, 1), (1, 0)])  11.9 us
  transfers between devices with their start and end apart: 16, of which 10 were waited for; matrix products, arithmetic and copies ran while one was open for 16% of the time, Pallas kernels for 0%

profile of v9, /device:TPU:1, one launch (start us, length us, event | category | flops | bytes accessed | tf_op | source)
XLA Modules:
  0.0 290.3 jit_solution(16561264956926045576)
XLA Ops:
  7.2 22.8 %reduce = bf16[524288]{0:T(1024)(128)(2,1)S(1)} reduce(bf16[1,1,524288]{2,1,0:T(2,128)(2,1)} %param.6, bf16[]{:T(256)} %constant.163), dimensions={0,1}, to_apply=%param.6.reduce_sub_computation | reduce | bytes 2097154 | tf_op args[0]
  32.2 7.8 %all-to-all-start = ((bf16[64,16,512]{2,0,1:T(8,128)(2,1)}), bf16[64,16,512]{2,0,1:T(8,128)(2,1)S(1)}, u32[]{:S(2)}, u32[]{:S(2)}) async-start(bf16[64,16,512]{2,0,1:T(8,128)(2,1)} %copy.25), calls=%async_computation | async-start | bytes 2097152 | tf_op jit(solution)/shard_map/all_to_all | solution.py:48
  42.0 13.9 %all-to-all-done = bf16[64,16,512]{2,0,1:T(8,128)(2,1)S(1)} async-done(((bf16[64,16,512]{2,0,1:T(8,128)(2,1)}), bf16[64,16,512]{2,0,1:T(8,128)(2,1)S(1)}, u32[]{:S(2)}, u32[]{:S(2)}) %all-to-all-start) | async-done | bytes 1048608 | tf_op jit(solution)/shard_map/all_to_all | solution.py:48
  55.9 2.0 gather_fusion
  58.0 13.2 %all_to_all.51 = bf16[16,32,512]{2,1,0:T(8,128)(2,1)S(1)} all-to-all(bf16[16,32,512]{2,1,0:T(8,128)(2,1)S(1)} %broadcast_select_fusion.1), channel_id=1, replica_groups=mesh['x'=4,'yh'=2,'chip'=8,'core'=2] {'chip','core'}, dimensions={0} | all-to-all | bytes 1048576 | tf_op jit(solution)/shard_map/all_to_all | solution.py:51
  72.0 15.8 %all_to_all.52 = bf16[32,8,1024]{2,0,1:T(8,128)(2,1)} all-to-all(bf16[32,8,1024]{2,0,1:T(8,128)(2,1)S(1)} %copy.27), channel_id=1, replica_groups=mesh['x'=4,'yh'=2,'chip'=8,'core'=2] {'x','yh'}, dimensions={1} | all-to-all | bytes 1048576 | tf_op jit(solution)/shard_map/all_to_all | solution.py:52
  89.3 11.9 %collective-permute-done = bf16[512,512]{1,0:T(8,128)(2,1)S(1)} collective-permute-done((bf16[512,512]{1,0:T(8,128)(2,1)S(1)}, bf16[512,512]{1,0:T(8,128)(2,1)S(1)}, u32[]{:S(2)}, u32[]{:S(2)}) %collective-permute-start) | collective-permute-done | bytes 524320 | tf_op jit(solution)/shard_map/ppermute | solution.py:53
  101.3 2.3 broadcast_in_dim.33
  105.5 2.7 collective-permute-start.3
  108.2 13.4 %collective-permute-done.2 = bf16[2,512,512]{2,1,0:T(8,128)(2,1)S(1)} collective-permute-done((bf16[2,512,512]{2,1,0:T(8,128)(2,1)}, bf16[2,512,512]{2,1,0:T(8,128)(2,1)S(1)}, u32[]{:S(2)}, u32[]{:S(2)}) %collective-permute-start.2) | collective-permute-done | bytes 1048608 | tf_op jit(solution)/shard_map/ppermute | solution.py:58
  121.6 33.0 %collective-permute-done.1 = bf16[2,512,512]{2,1,0:T(8,128)(2,1)} collective-permute-done((bf16[2,512,512]{2,1,0:T(8,128)(2,1)}, bf16[2,512,512]{2,1,0:T(8,128)(2,1)}, u32[]{:S(2)}, u32[]{:S(2)}) %collective-permute-start.1) | collective-permute-done | bytes 1048608 | tf_op jit(solution)/shard_map/ppermute | solution.py:58
  154.6 2.4 constant_dynamic-update-slice_fusion.2
  159.1 5.4 %fusion.12 = bf16[512,512]{0,1:T(8,128)(2,1)} fusion(bf16[4096,512]{1,0:T(8,128)(2,1)} %bitcast.24, bf16[512,4096]{1,0:T(8,128)(2,1)S(1)} %copy-done.2), kind=kOutput, calls=%fused_computation.13 | convolution fusion | flops 2147745792 | bytes 8912896 | tf_op jit(solution)/shard_map/dot_general | solution.py:96
  164.5 4.2 %fusion.8 = bf16[512,8,256]{2,0,1:T(8,128)(2,1)} fusion(bf16[8,2,256,512]{3,2,1,0:T(8,128)(2,1)} %bitcast.13, s32[]{:T(128)S(6)} %select_n.155, bf16[512,512]{1,0:T(8,128)(2,1)S(1)} %broadcast_select_fusion), kind=kOutput, calls=%fused_computation.9 | convolution fusion | flops 1074790400 | bytes 4718596 | tf_op jit(solution)/shard_map/dot_general | solution.py:75
  169.2 4.0 %collective-permute-done.4 = bf16[512,8,256]{2,0,1:T(8,128)(2,1)S(1)} collective-permute-done((bf16[512,8,256]{2,0,1:T(8,128)(2,1)}, bf16[512,8,256]{2,0,1:T(8,128)(2,1)S(1)}, u32[]{:S(2)}, u32[]{:S(2)}) %collective-permute-start.4) | collective-permute-done | bytes 2097184 | tf_op jit(solution)/shard_map/ppermute | solution.py:29
  173.2 4.9 %fusion.25 = (bf16[512,8,256]{2,0,1:T(8,128)(2,1)S(1)}, f32[512,8,256]{2,0,1:T(8,128)}) fusion(bf16[512,8,256]{2,0,1:T(8,128)(2,1)S(1)} %collective-permute-done.4, bf16[8,2,256,512]{3,2,1,0:T(8,128)(2,1)} %bitcast.13, s32[]{:T(128)S(6)} %select_n.154, bf16[512,512]{1,0:T(8,128)(2,1)S(1)} %broadcast_select_fusion), kind=kOutput, calls=%fused_computation.57 | convolution fusion | flops 1076887552 | bytes 11010052 | tf_op jit(solution)/shard_map/dot_general | solution.py:74
  178.2 2.2 collective-permute-start.11
  180.4 3.5 %collective-permute-start.9 = (bf16[512,256]{1,0:T(8,128)(2,1)S(1)}, bf16[512,256]{1,0:T(8,128)(2,1)S(1)}, u32[]{:S(2)}, u32[]{:S(2)}) collective-permute-start(bf16[512,256]{1,0:T(8,128)(2,1)S(1)} %get-tuple-element.33), channel_id=1, source_target_pairs={{0,10},{2,12},{4,14},{6,0},{8,2},{10,4},{12,6},{14,8},{1,11},{3,13... | collective-permute-start | bytes 786440 | tf_op jit(solution)/shard_map/ppermute | solution.py:80
  184.0 2.3 collective-permute-start.7
  186.3 12.2 %collective-permute-done.11 = bf16[512,256]{1,0:T(8,128)(2,1)S(1)} collective-permute-done((bf16[512,256]{1,0:T(8,128)(2,1)S(1)}, bf16[512,256]{1,0:T(8,128)(2,1)S(1)}, u32[]{:S(2)}, u32[]{:S(2)}) %collective-permute-start.11) | collective-permute-done | bytes 262176 | tf_op jit(solution)/shard_map/ppermute | solution.py:80
  198.5 9.4 %collective-permute-done.10 = bf16[512,256]{1,0:T(8,128)(2,1)S(1)} collective-permute-done((bf16[512,256]{1,0:T(8,128)(2,1)S(1)}, bf16[512,256]{1,0:T(8,128)(2,1)S(1)}, u32[]{:S(2)}, u32[]{:S(2)}) %collective-permute-start.10) | collective-permute-done | bytes 262176 | tf_op jit(solution)/shard_map/ppermute | solution.py:80
  207.9 5.9 %collective-permute-start.5 = (bf16[512,256]{1,0:T(8,128)(2,1)S(1)}, bf16[512,256]{1,0:T(8,128)(2,1)S(1)}, u32[]{:S(2)}, u32[]{:S(2)}) collective-permute-start(bf16[512,256]{1,0:T(8,128)(2,1)S(1)} %get-tuple-element.37), channel_id=1, source_target_pairs={{0,2},{2,4},{4,6},{6,8},{8,10},{10,12},{12,14},{14,0},{1,3},{3,5},... | collective-permute-start | bytes 786440 | tf_op jit(solution)/shard_map/ppermute | solution.py:80
  213.8 5.4 %collective-permute-done.9 = bf16[512,256]{1,0:T(8,128)(2,1)S(1)} collective-permute-done((bf16[512,256]{1,0:T(8,128)(2,1)S(1)}, bf16[512,256]{1,0:T(8,128)(2,1)S(1)}, u32[]{:S(2)}, u32[]{:S(2)}) %collective-permute-start.9) | collective-permute-done | bytes 262176 | tf_op jit(solution)/shard_map/ppermute | solution.py:80
  219.2 15.8 %collective-permute-done.8 = bf16[512,256]{1,0:T(8,128)(2,1)S(1)} collective-permute-done((bf16[512,256]{1,0:T(8,128)(2,1)S(1)}, bf16[512,256]{1,0:T(8,128)(2,1)S(1)}, u32[]{:S(2)}, u32[]{:S(2)}) %collective-permute-start.8) | collective-permute-done | bytes 262176 | tf_op jit(solution)/shard_map/ppermute | solution.py:80
  235.0 9.5 %all-gather.5.cloned.1.call-done = bf16[512,4096]{0,1:T(8,128)(2,1)} async-done(((bf16[512,512]{0,1:T(8,128)(2,1)}), bf16[512,4096]{0,1:T(8,128)(2,1)}) %all-gather.5.cloned.1.call-update) | async-done | bytes 4194320 | tf_op jit(solution)/shard_map/all_gather | solution.py:99
  245.4 11.5 %copy.29 = bf16[512,8192]{0,1:T(8,128)(2,1)} copy(bf16[512,8192]{1,0:T(8,128)(2,1)} %param.11) | data formatting | bytes 16777216 | tf_op args[5]
  257.0 4.3 %constant_dynamic-slice_fusion.1 = (bf16[512,8,1,512]{0,3,2,1:T(8,128)(2,1)S(1)}, bf16[512,8,1,512]{0,3,2,1:T(8,128)(2,1)S(1)}) fusion(bf16[512,8,2,512]{0,3,2,1:T(8,128)(2,1)} %bitcast.88, s32[]{:T(128)S(6)} %select_n.154, s32[]{:T(128)S(6)} %select_n.155), kind=kLoop, calls=%fused_computation.45 | loop fusion | bytes 16777224 | tf_op jit(solution)/shard_map/jit(dynamic_index_in_dim)/dynamic_slice | solution.py:106
  261.3 2.8 copy.28
  264.2 9.3 %multiply_add_fusion = f32[512,1024]{1,0:T(8,128)} fusion(f32[512,1024]{1,0:T(8,128)S(1)} %copy-done.3, bf16[4096,512]{1,0:T(8,128)(2,1)S(1)} %bitcast.92, bf16[4096,1024]{1,0:T(8,128)(2,1)} %all-gather.3.cloned.1.call-done), kind=kOutput, calls=%fused_computation.6 | convolution fusion | flops 4296540160 | bytes 16777216 | tf_op jit(solution)/shard_map/dot_general | solution.py:92
  273.4 2.1 fusion.20
  275.6 4.7 %fusion.26 = f32[512,512]{1,0:T(8,128)S(1)} fusion(bf16[512,4096]{0,1:T(8,128)(2,1)} %collective-permute-done.12, bf16[512,4096]{0,1:T(8,128)(2,1)S(1)} %bitcast.89), kind=kOutput, calls=%fused_computation.58 | convolution fusion | flops 2147483648 | bytes 9437184 | tf_op jit(solution)/shard_map/dot_general | solution.py:113
  280.3 3.2 %fusion.11 = bf16[512,512]{1,0:T(8,128)(2,1)} fusion(f32[512,512]{1,0:T(8,128)S(1)} %fusion.26, bf16[512,4096]{0,1:T(8,128)(2,1)S(1)} %copy-done, bf16[512,4096]{0,1:T(8,128)(2,1)S(1)} %bitcast.87), kind=kOutput, calls=%fused_computation.11 | convolution fusion | flops 2148007936 | bytes 9961472 | tf_op jit(solution)/shard_map/dot_general | solution.py:111
  (49 shorter events, 12.4 us)
Async XLA Ops:
  32.2 23.7 %all-to-all-start = ((bf16[64,16,512]{2,0,1:T(8,128)(2,1)}), bf16[64,16,512]{2,0,1:T(8,128)(2,1)S(1)}, u32[]{:S(2)}, u32[]{:S(2)}) async-start(bf16[64,16,512]{2,0,1:T(8,128)(2,1)} %copy.25), calls=%async_computation | async-start | bytes 2097152 | tf_op jit(solution)/shard_map/all_to_all | solution.py:48
  40.0 114.6 %all-gather.3.cloned.1.call-start = ((), (), s32[]{:S(2)}) async-start(), calls=%async_computation.3 | async-start | bytes 8912896 | tf_op jit(solution)/shard_map/all_gather | solution.py:61
  87.7 156.7 %all-gather.5.cloned.1.call-start = ((), (), s32[]{:S(2)}) async-start(), calls=%async_computation.4 | async-start | bytes 4718592 | tf_op jit(solution)/shard_map/all_gather | solution.py:99
  87.9 13.2 %collective-permute-start = (bf16[512,512]{1,0:T(8,128)(2,1)S(1)}, bf16[512,512]{1,0:T(8,128)(2,1)S(1)}, u32[]{:S(2)}, u32[]{:S(2)}) collective-permute-start(bf16[512,512]{1,0:T(8,128)(2,1)S(1)} %broadcast_select_fusion), channel_id=1, source_target_pairs={{0,16},{16,0},{1,17},{17,1},{2,18},{18,2},{3,19},{19,3},{4,20},{20... | collective-permute-start | bytes 1572872 | tf_op jit(solution)/shard_map/ppermute | solution.py:53
  105.2 16.4 %collective-permute-start.2 = (bf16[2,512,512]{2,1,0:T(8,128)(2,1)}, bf16[2,512,512]{2,1,0:T(8,128)(2,1)S(1)}, u32[]{:S(2)}, u32[]{:S(2)}) collective-permute-start(bf16[2,512,512]{2,1,0:T(8,128)(2,1)} %get-tuple-element.38), channel_id=1, source_target_pairs={{0,64},{32,96},{64,0},{96,32},{1,65},{33,97},{65,1},{97,33},{2,66}... | collective-permute-start | bytes 3145736 | tf_op jit(solution)/shard_map/ppermute | solution.py:58
  105.5 49.0 %collective-permute-start.1 = (bf16[2,512,512]{2,1,0:T(8,128)(2,1)}, bf16[2,512,512]{2,1,0:T(8,128)(2,1)}, u32[]{:S(2)}, u32[]{:S(2)}) collective-permute-start(bf16[2,512,512]{2,1,0:T(8,128)(2,1)} %get-tuple-element.38), channel_id=1, source_target_pairs={{0,32},{32,64},{64,96},{96,0},{1,33},{33,65},{65,97},{97,1},{2,34}... | collective-permute-start | bytes 3145736 | tf_op jit(solution)/shard_map/ppermute | solution.py:58
  105.5 49.0 %collective-permute-start.3 = (bf16[2,512,512]{2,1,0:T(8,128)(2,1)}, bf16[2,512,512]{2,1,0:T(8,128)(2,1)S(1)}, u32[]{:S(2)}, u32[]{:S(2)}) collective-permute-start(bf16[2,512,512]{2,1,0:T(8,128)(2,1)} %get-tuple-element.38), channel_id=1, source_target_pairs={{0,96},{32,0},{64,32},{96,64},{1,97},{33,1},{65,33},{97,65},{2,98}... | collective-permute-start | bytes 3145736 | tf_op jit(solution)/shard_map/ppermute | solution.py:58
  154.6 4.5 %copy-start.2 = (bf16[512,4096]{1,0:T(8,128)(2,1)S(1)}, bf16[512,4096]{1,0:T(8,128)(2,1)}, u32[]{:S(2)}) copy-start(bf16[512,4096]{1,0:T(8,128)(2,1)} %param.10) | copy-start | bytes 12582916
  168.8 4.5 %collective-permute-start.4 = (bf16[512,8,256]{2,0,1:T(8,128)(2,1)}, bf16[512,8,256]{2,0,1:T(8,128)(2,1)S(1)}, u32[]{:S(2)}, u32[]{:S(2)}) collective-permute-start(bf16[512,8,256]{2,0,1:T(8,128)(2,1)} %fusion.8), channel_id=1, source_target_pairs={{0,1},{1,0},{2,3},{3,2},{4,5},{5,4},{6,7},{7,6},{8,9},{9,8},{10,11... | collective-permute-start | bytes 6291464 | tf_op jit(solution)/shard_map/ppermute | solution.py:29
  178.2 20.2 %collective-permute-start.11 = (bf16[512,256]{1,0:T(8,128)(2,1)S(1)}, bf16[512,256]{1,0:T(8,128)(2,1)S(1)}, u32[]{:S(2)}, u32[]{:S(2)}) collective-permute-start(bf16[512,256]{1,0:T(8,128)(2,1)S(1)} %get-tuple-element.31), channel_id=1, source_target_pairs={{0,14},{2,0},{4,2},{6,4},{8,6},{10,8},{12,10},{14,12},{1,15},{3,1}... | collective-permute-start | bytes 786440 | tf_op jit(solution)/shard_map/ppermute | solution.py:80
  180.4 27.4 %collective-permute-start.10 = (bf16[512,256]{1,0:T(8,128)(2,1)S(1)}, bf16[512,256]{1,0:T(8,128)(2,1)S(1)}, u32[]{:S(2)}, u32[]{:S(2)}) collective-permute-start(bf16[512,256]{1,0:T(8,128)(2,1)S(1)} %get-tuple-element.32), channel_id=1, source_target_pairs={{0,12},{2,14},{4,0},{6,2},{8,4},{10,6},{12,8},{14,10},{1,13},{3,15... | collective-permute-start | bytes 786440 | tf_op jit(solution)/shard_map/ppermute | solution.py:80
  180.4 38.8 %collective-permute-start.9 = (bf16[512,256]{1,0:T(8,128)(2,1)S(1)}, bf16[512,256]{1,0:T(8,128)(2,1)S(1)}, u32[]{:S(2)}, u32[]{:S(2)}) collective-permute-start(bf16[512,256]{1,0:T(8,128)(2,1)S(1)} %get-tuple-element.33), channel_id=1, source_target_pairs={{0,10},{2,12},{4,14},{6,0},{8,2},{10,4},{12,6},{14,8},{1,11},{3,13... | collective-permute-start | bytes 786440 | tf_op jit(solution)/shard_map/ppermute | solution.py:80
  184.0 51.0 %collective-permute-start.8 = (bf16[512,256]{1,0:T(8,128)(2,1)S(1)}, bf16[512,256]{1,0:T(8,128)(2,1)S(1)}, u32[]{:S(2)}, u32[]{:S(2)}) collective-permute-start(bf16[512,256]{1,0:T(8,128)(2,1)S(1)} %get-tuple-element.34), channel_id=1, source_target_pairs={{0,8},{2,10},{4,12},{6,14},{8,0},{10,2},{12,4},{14,6},{1,9},{3,11}... | collective-permute-start | bytes 786440 | tf_op jit(solution)/shard_map/ppermute | solution.py:80
  184.0 51.0 %collective-permute-start.7 = (bf16[512,256]{1,0:T(8,128)(2,1)S(1)}, bf16[512,256]{1,0:T(8,128)(2,1)S(1)}, u32[]{:S(2)}, u32[]{:S(2)}) collective-permute-start(bf16[512,256]{1,0:T(8,128)(2,1)S(1)} %get-tuple-element.35), channel_id=1, source_target_pairs={{0,6},{2,8},{4,10},{6,12},{8,14},{10,0},{12,2},{14,4},{1,7},{3,9},... | collective-permute-start | bytes 786440 | tf_op jit(solution)/shard_map/ppermute | solution.py:80
  198.5 36.5 %collective-permute-start.6 = (bf16[512,256]{1,0:T(8,128)(2,1)S(1)}, bf16[512,256]{1,0:T(8,128)(2,1)S(1)}, u32[]{:S(2)}, u32[]{:S(2)}) collective-permute-start(bf16[512,256]{1,0:T(8,128)(2,1)S(1)} %get-tuple-element.36), channel_id=1, source_target_pairs={{0,4},{2,6},{4,8},{6,10},{8,12},{10,14},{12,0},{14,2},{1,5},{3,7},... | collective-permute-start | bytes 786440 | tf_op jit(solution)/shard_map/ppermute | solution.py:80
  207.9 27.1 %collective-permute-start.5 = (bf16[512,256]{1,0:T(8,128)(2,1)S(1)}, bf16[512,256]{1,0:T(8,128)(2,1)S(1)}, u32[]{:S(2)}, u32[]{:S(2)}) collective-permute-start(bf16[512,256]{1,0:T(8,128)(2,1)S(1)} %get-tuple-element.37), channel_id=1, source_target_pairs={{0,2},{2,4},{4,6},{6,8},{8,10},{10,12},{12,14},{14,0},{1,3},{3,5},... | collective-permute-start | bytes 786440 | tf_op jit(solution)/shard_map/ppermute | solution.py:80
  244.4 31.1 %collective-permute-start.12 = (bf16[512,4096]{0,1:T(8,128)(2,1)}, bf16[512,4096]{0,1:T(8,128)(2,1)}, u32[]{:S(2)}, u32[]{:S(2)}) collective-permute-start(bf16[512,4096]{0,1:T(8,128)(2,1)} %all-gather.5.cloned.1.call-done), channel_id=1, source_target_pairs={{0,1},{1,0},{2,3},{3,2},{4,5},{5,4},{6,7},{7,6},{8,9},{9,8},{10,11... | collective-permute-start | bytes 12582920 | tf_op jit(solution)/shard_map/ppermute | solution.py:29
  261.3 2.9 copy-start.3
  264.2 9.3 %copy-start.1 = (f32[512,256]{1,0:T(8,128)S(1)}, f32[512,256]{1,0:T(8,128)}, u32[]{:S(2)}) copy-start(f32[512,256]{1,0:T(8,128)} %param.8) | copy-start | bytes 1572868
  275.6 4.7 %copy-start = (bf16[512,4096]{0,1:T(8,128)(2,1)S(1)}, bf16[512,4096]{0,1:T(8,128)(2,1)}, u32[]{:S(2)}) copy-start(bf16[512,4096]{0,1:T(8,128)(2,1)} %all-gather.5.cloned.1.call-done) | copy-start | bytes 12582916
Sparse Core Ops, SparseCore 0:
  87.8 55.5 all-gather.2
  164.7 79.7 all-gather.4

commit v10 on v7

--- a/solution.py
+++ b/solution.py
@@ -77,11 +77,18 @@
     sub_rows = jnp.take(row_block, sub_index, axis=0)
     left_part = lax.dot_general(
         row_block, sub_rows, (((1,), (1,)), ((), ())), preferred_element_type=jnp.float32
-    ).astype(jnp.bfloat16)
-    left_part = (
-        left_part.reshape(col_count, row_count, slice_rows, chunk).transpose(1, 0, 2, 3).reshape(HQ, chunk)
     )
-    left_sum = lax.psum_scatter(left_part, ROW, scatter_dimension=0, tiled=True).astype(jnp.float32)
+    left_part = left_part.reshape(col_count, row_count, slice_rows, chunk).transpose(1, 0, 2, 3)
+    left_part = left_part.reshape(row_count, tile_rows, chunk)
+    outgoing = left_part.astype(jnp.bfloat16)
+    incoming = [
+        lax.ppermute(
+            lax.dynamic_index_in_dim(outgoing, (row_index + s) % row_count, 0, keepdims=False),
+            ROW,
+            [(i, (i + s) % row_count) for i in range(row_count)],
+        )
+        for s in range(1, row_count)
+    ]
     panel_reordered = (
         column_panel.reshape(row_count, col_count, slice_rows, tile_cols)
         .transpose(1, 0, 2, 3)
@@ -94,8 +101,13 @@
     left_mixed = jnp.dot(left_root, column_panel, preferred_element_type=jnp.float32).astype(
         jnp.bfloat16
     )
+    mixed_rows = lax.all_gather(left_mixed, COL, axis=1, tiled=True)
+    incoming, mixed_rows = lax.optimization_barrier((incoming, mixed_rows))
+    left_sum = lax.dynamic_index_in_dim(left_part, row_index, 0, keepdims=False)
+    for part in incoming:
+        left_sum = left_sum + part.astype(jnp.float32)
     update_sum = lax.dot_general(
-        lax.all_gather(left_mixed, COL, axis=1, tiled=True),
+        mixed_rows,
         right_root,
         (((1,), (1,)), ((), ())),
         preferred_element_type=jnp.float32,

time: 319 us -> 262 us (0.82)
  waiting for transfers between devices: 182 us -> 111 us
  starting transfers between devices: 12 us -> 28 us
  matrix products: 31.9 us -> 28.2 us
    reduce_scatter x1 -> x0, waiting for transfers between devices: 57.3 us -> none  [shards(): lax.psum_scatter(left_part, ROW, scatter_dimension=0, tiled=True)]
    all_gather x1, waiting for transfers between devices: 53.5 us -> 24.1 us  [shards(): mixed_rows = lax.all_gather(left_mixed, COL, axis=1, tiled=True)]
    ppermute x0 -> x7, starting transfers between devices: none -> 16.1 us  [shards(): lax.ppermute(lax.dynamic_index_in_dim(outgoing, (row_index + s) % row_cou...]
    ppermute x0 -> x7, waiting for transfers between devices: none -> 15.8 us  [shards(): lax.ppermute(lax.dynamic_index_in_dim(outgoing, (row_index + s) % row_cou...]
    dot_general x1, matrix products: 9.46 us -> 5.83 us  [shards(): lax.dot_general(panel_reordered, row_block, (((0,), (0,)), ((), ())), pre...]
    unnamed x1 -> x2, other arithmetic: 22.8 us -> 22.8 us
  transfers between devices with their start and end apart: 8 -> 14, of which waited for: 7 -> 9; matrix products, arithmetic and copies ran while one was open for 9% -> 11% of each run, Pallas kernels for 0% -> 0%
where the time goes in v10:
time: 262 us; the launch traced here: 261 us
  waiting for transfers between devices  111 us (42%)
  blocking collectives  29 us (11%)
  other arithmetic  28.4 us (11%)
  matrix products  28.2 us (11%)
  starting transfers between devices  28 us (11%)
  local copies, waits for them, and re-layouts  22.4 us (9%)
  between operations  14.4 us (5%)
    ppermute x3, waiting for transfers between devices, shards(): lax.ppermute(pair, 'x', [(i, (i + s) % x_count) for i in range(x_count)])  45.3 us
    all_gather x1, waiting for transfers between devices, shards(): mixed_rows = lax.all_gather(left_mixed, COL, axis=1, tiled=True)  24.1 us
    unnamed x2, other arithmetic  22.8 us
    ppermute x7, starting transfers between devices, shards(): lax.ppermute(lax.dynamic_index_in_dim(outgoing, (row_index + s) % row_cou...  16.1 us
    ppermute x7, waiting for transfers between devices, shards(): lax.ppermute(lax.dynamic_index_in_dim(outgoing, (row_index + s) % row_cou...  15.8 us
    all_to_all x1, blocking collectives, shards(): lax.all_to_all(row_slice, ROW, split_axis=1, concat_axis=0, tiled=True)  15.8 us
    all_to_all x1, waiting for transfers between devices, shards(): lax.all_to_all(held_rows, COL, split_axis=1, concat_axis=0, tiled=True)  13.9 us
    all_to_all x1, blocking collectives, shards(): lax.all_to_all(grad_tile, COL, split_axis=0, concat_axis=1, tiled=True)  13.2 us
  transfers between devices with their start and end apart: 14, of which 9 were waited for; matrix products, arithmetic and copies ran while one was open for 11% of the time, Pallas kernels for 0%

profile of v10, /device:TPU:1, one launch (start us, length us, event | category | flops | bytes accessed | tf_op | source)
XLA Modules:
  0.0 261.3 jit_solution(17659053970784793307)
XLA Ops:
  7.2 22.8 %reduce = bf16[524288]{0:T(1024)(128)(2,1)S(1)} reduce(bf16[1,1,524288]{2,1,0:T(2,128)(2,1)} %param.6, bf16[]{:T(256)} %constant.214), dimensions={0,1}, to_apply=%param.6.reduce_sub_computation | reduce | bytes 2097154 | tf_op args[0]
  30.6 1.5 copy.25
  32.2 7.8 %all-to-all-start = ((bf16[64,16,512]{2,0,1:T(8,128)(2,1)}), bf16[64,16,512]{2,0,1:T(8,128)(2,1)S(1)}, u32[]{:S(2)}, u32[]{:S(2)}) async-start(bf16[64,16,512]{2,0,1:T(8,128)(2,1)} %copy.25), calls=%async_computation | async-start | bytes 2097152 | tf_op jit(solution)/shard_map/all_to_all | solution.py:48
  42.0 13.9 %all-to-all-done = bf16[64,16,512]{2,0,1:T(8,128)(2,1)S(1)} async-done(((bf16[64,16,512]{2,0,1:T(8,128)(2,1)}), bf16[64,16,512]{2,0,1:T(8,128)(2,1)S(1)}, u32[]{:S(2)}, u32[]{:S(2)}) %all-to-all-start) | async-done | bytes 1048608 | tf_op jit(solution)/shard_map/all_to_all | solution.py:48
  55.9 2.0 gather_fusion
  58.0 13.2 %all_to_all.51 = bf16[16,32,512]{2,1,0:T(8,128)(2,1)S(1)} all-to-all(bf16[16,32,512]{2,1,0:T(8,128)(2,1)S(1)} %broadcast_select_fusion.1), channel_id=1, replica_groups=mesh['x'=4,'yh'=2,'chip'=8,'core'=2] {'chip','core'}, dimensions={0} | all-to-all | bytes 1048576 | tf_op jit(solution)/shard_map/all_to_all | solution.py:51
  72.0 15.8 %all_to_all.52 = bf16[32,8,1024]{2,0,1:T(8,128)(2,1)} all-to-all(bf16[32,8,1024]{2,0,1:T(8,128)(2,1)S(1)} %copy.27), channel_id=1, replica_groups=mesh['x'=4,'yh'=2,'chip'=8,'core'=2] {'x','yh'}, dimensions={1} | all-to-all | bytes 1048576 | tf_op jit(solution)/shard_map/all_to_all | solution.py:52
  87.9 1.3 collective-permute-start
  89.3 11.9 %collective-permute-done = bf16[512,512]{1,0:T(8,128)(2,1)S(1)} collective-permute-done((bf16[512,512]{1,0:T(8,128)(2,1)S(1)}, bf16[512,512]{1,0:T(8,128)(2,1)S(1)}, u32[]{:S(2)}, u32[]{:S(2)}) %collective-permute-start) | collective-permute-done | bytes 524320 | tf_op jit(solution)/shard_map/ppermute | solution.py:53
  101.3 2.3 broadcast_in_dim.47
  103.7 1.5 constant_dynamic-update-slice_fusion.3
  105.8 2.1 collective-permute-start.3
  107.8 13.9 %collective-permute-done.1 = bf16[2,512,512]{2,1,0:T(8,128)(2,1)S(1)} collective-permute-done((bf16[2,512,512]{2,1,0:T(8,128)(2,1)}, bf16[2,512,512]{2,1,0:T(8,128)(2,1)S(1)}, u32[]{:S(2)}, u32[]{:S(2)}) %collective-permute-start.1) | collective-permute-done | bytes 1048608 | tf_op jit(solution)/shard_map/ppermute | solution.py:58
  121.7 21.4 %collective-permute-done.2 = bf16[2,512,512]{2,1,0:T(8,128)(2,1)S(1)} collective-permute-done((bf16[2,512,512]{2,1,0:T(8,128)(2,1)}, bf16[2,512,512]{2,1,0:T(8,128)(2,1)S(1)}, u32[]{:S(2)}, u32[]{:S(2)}) %collective-permute-start.2) | collective-permute-done | bytes 1048608 | tf_op jit(solution)/shard_map/ppermute | solution.py:58
  143.1 10.1 %collective-permute-done.3 = bf16[2,512,512]{2,1,0:T(8,128)(2,1)S(1)} collective-permute-done((bf16[2,512,512]{2,1,0:T(8,128)(2,1)}, bf16[2,512,512]{2,1,0:T(8,128)(2,1)S(1)}, u32[]{:S(2)}, u32[]{:S(2)}) %collective-permute-start.3) | collective-permute-done | bytes 1048608 | tf_op jit(solution)/shard_map/ppermute | solution.py:58
  153.1 1.1 constant_dynamic-update-slice_fusion.2
  156.4 5.4 %fusion = bf16[512,512]{0,1:T(8,128)(2,1)} fusion(bf16[4096,512]{1,0:T(8,128)(2,1)} %bitcast.25, bf16[512,4096]{1,0:T(8,128)(2,1)S(1)} %copy-done.2), kind=kOutput, calls=%fused_computation.5 | convolution fusion | flops 2147745792 | bytes 8912896 | tf_op jit(solution)/shard_map/dot_general | solution.py:101
  162.0 6.0 %gather_fusion.1 = bf16[256,1024]{1,0:T(8,128)(2,1)S(1)} fusion(bf16[4096,1024]{1,0:T(8,128)(2,1)} %all-gather.3.cloned.1.call-done, s32[1024]{0:T(1024)S(1)} %pad_clamp_fusion), kind=kCustom, calls=%fused_computation.1 | custom fusion | bytes 1049600 | tf_op jit(solution)/shard_map/jit(_take)/gather | solution.py:77
  168.0 5.8 %fusion.9 = f32[4096,256]{1,0:T(8,128)S(1)} fusion(bf16[4096,1024]{1,0:T(8,128)(2,1)} %all-gather.3.cloned.1.call-done, bf16[256,1024]{1,0:T(8,128)(2,1)S(1)} %gather_fusion.1, pred[256]{0:T(512)(128)(4,1)S(1)} %compare_and_fusion.1), kind=kOutput, calls=%fused_computation.16 | convolution fusion | flops 2147745792 | bytes 13107456 | tf_op jit(solution)/shard_map/dot_general | solution.py:78
  175.0 1.5 copy-done
  176.5 6.1 %collective-permute-start.10 = (bf16[512,256]{1,0:T(8,128)(2,1)S(1)}, bf16[512,256]{1,0:T(8,128)(2,1)S(1)}, u32[]{:S(2)}, u32[]{:S(2)}) collective-permute-start(bf16[512,256]{1,0:T(8,128)(2,1)S(1)} %get-tuple-element.29), channel_id=1, source_target_pairs={{0,112},{16,0},{32,16},{48,32},{64,48},{80,64},{96,80},{112,96},{1... | collective-permute-start | bytes 786440 | tf_op jit(solution)/shard_map/ppermute | solution.py:85
  182.6 2.9 %copy.29 = bf16[16,8,32,512]{3,2,1,0:T(8,128)(2,1)S(1)} copy(bf16[16,8,32,512]{3,2,0,1:T(8,128)(2,1)} %bitcast.28) | data formatting | bytes 8388608 | tf_op jit(solution)/shard_map/transpose | solution.py:94
  185.6 2.3 collective-permute-start.6
  187.9 4.0 %collective-permute-start.7 = (bf16[512,256]{1,0:T(8,128)(2,1)S(1)}, bf16[512,256]{1,0:T(8,128)(2,1)S(1)}, u32[]{:S(2)}, u32[]{:S(2)}) collective-permute-start(bf16[512,256]{1,0:T(8,128)(2,1)S(1)} %get-tuple-element.32), channel_id=1, source_target_pairs={{0,64},{16,80},{32,96},{48,112},{64,0},{80,16},{96,32},{112,48},{1... | collective-permute-start | bytes 786440 | tf_op jit(solution)/shard_map/ppermute | solution.py:85
  191.9 5.1 %collective-permute-done.10 = bf16[512,256]{1,0:T(8,128)(2,1)S(1)} collective-permute-done((bf16[512,256]{1,0:T(8,128)(2,1)S(1)}, bf16[512,256]{1,0:T(8,128)(2,1)S(1)}, u32[]{:S(2)}, u32[]{:S(2)}) %collective-permute-start.10) | collective-permute-done | bytes 262176 | tf_op jit(solution)/shard_map/ppermute | solution.py:85
  197.0 5.6 %collective-permute-done.4 = bf16[512,256]{1,0:T(8,128)(2,1)S(1)} collective-permute-done((bf16[512,256]{1,0:T(8,128)(2,1)S(1)}, bf16[512,256]{1,0:T(8,128)(2,1)S(1)}, u32[]{:S(2)}, u32[]{:S(2)}) %collective-permute-start.4) | collective-permute-done | bytes 262176 | tf_op jit(solution)/shard_map/ppermute | solution.py:85
  202.6 3.6 %collective-permute-start.9 = (bf16[512,256]{1,0:T(8,128)(2,1)S(1)}, bf16[512,256]{1,0:T(8,128)(2,1)S(1)}, u32[]{:S(2)}, u32[]{:S(2)}) collective-permute-start(bf16[512,256]{1,0:T(8,128)(2,1)S(1)} %get-tuple-element.30), channel_id=1, source_target_pairs={{0,96},{16,112},{32,0},{48,16},{64,32},{80,48},{96,64},{112,80},{1... | collective-permute-start | bytes 786440 | tf_op jit(solution)/shard_map/ppermute | solution.py:85
  206.3 5.8 %multiply_add_fusion = f32[512,1024]{1,0:T(8,128)} fusion(f32[512,1024]{1,0:T(8,128)S(1)} %copy-done.3, bf16[4096,512]{1,0:T(8,128)(2,1)S(1)} %bitcast.72, bf16[4096,1024]{1,0:T(8,128)(2,1)S(1)} %bitcast.75), kind=kOutput, calls=%fused_computation.2 | convolution fusion | flops 4296540160 | bytes 16777216 | tf_op jit(solution)/shard_map/dot_general | solution.py:97
  212.1 5.0 %collective-permute-done.9 = bf16[512,256]{1,0:T(8,128)(2,1)S(1)} collective-permute-done((bf16[512,256]{1,0:T(8,128)(2,1)S(1)}, bf16[512,256]{1,0:T(8,128)(2,1)S(1)}, u32[]{:S(2)}, u32[]{:S(2)}) %collective-permute-start.9) | collective-permute-done | bytes 262176 | tf_op jit(solution)/shard_map/ppermute | solution.py:85
  217.2 24.1 %all-gather.5.cloned.1.call-done = bf16[512,8192]{0,1:T(8,128)(2,1)} async-done(((bf16[512,512]{0,1:T(8,128)(2,1)}), bf16[512,8192]{0,1:T(8,128)(2,1)}) %all-gather.5.cloned.1.call-update) | async-done | bytes 8388624 | tf_op jit(solution)/shard_map/all_gather | solution.py:104
  241.2 11.1 %convolution_convert_fusion = bf16[512,512]{1,0:T(8,128)(2,1)} fusion(bf16[512,8192]{0,1:T(8,128)(2,1)} %all-gather.5.cloned.1.call-done, bf16[512,8192]{1,0:T(8,128)(2,1)} %param.11), kind=kOutput, calls=%fused_computation.3 | convolution fusion | flops 4295229440 | bytes 17301504 | tf_op jit(solution)/shard_map/dot_general | solution.py:109
  252.3 2.1 fusion.8
  (52 shorter events, 7.8 us)
Async XLA Ops:
  32.2 23.7 %all-to-all-start = ((bf16[64,16,512]{2,0,1:T(8,128)(2,1)}), bf16[64,16,512]{2,0,1:T(8,128)(2,1)S(1)}, u32[]{:S(2)}, u32[]{:S(2)}) async-start(bf16[64,16,512]{2,0,1:T(8,128)(2,1)} %copy.25), calls=%async_computation | async-start | bytes 2097152 | tf_op jit(solution)/shard_map/all_to_all | solution.py:48
  40.0 113.1 %all-gather.3.cloned.1.call-start = ((), (), s32[]{:S(2)}) async-start(), calls=%async_computation.3 | async-start | bytes 8912896 | tf_op jit(solution)/shard_map/all_gather | solution.py:61
  87.7 153.5 %all-gather.5.cloned.1.call-start = ((), (), s32[]{:S(2)}) async-start(), calls=%async_computation.4 | async-start | bytes 8912896 | tf_op jit(solution)/shard_map/all_gather | solution.py:104
  87.9 13.2 %collective-permute-start = (bf16[512,512]{1,0:T(8,128)(2,1)S(1)}, bf16[512,512]{1,0:T(8,128)(2,1)S(1)}, u32[]{:S(2)}, u32[]{:S(2)}) collective-permute-start(bf16[512,512]{1,0:T(8,128)(2,1)S(1)} %broadcast_select_fusion), channel_id=1, source_target_pairs={{0,16},{16,0},{1,17},{17,1},{2,18},{18,2},{3,19},{19,3},{4,20},{20... | collective-permute-start | bytes 1572872 | tf_op jit(solution)/shard_map/ppermute | solution.py:53
  105.1 16.6 %collective-permute-start.1 = (bf16[2,512,512]{2,1,0:T(8,128)(2,1)}, bf16[2,512,512]{2,1,0:T(8,128)(2,1)S(1)}, u32[]{:S(2)}, u32[]{:S(2)}) collective-permute-start(bf16[2,512,512]{2,1,0:T(8,128)(2,1)} %get-tuple-element.37), channel_id=1, source_target_pairs={{0,32},{32,64},{64,96},{96,0},{1,33},{33,65},{65,97},{97,1},{2,34}... | collective-permute-start | bytes 3145736 | tf_op jit(solution)/shard_map/ppermute | solution.py:58
  105.2 37.9 %collective-permute-start.2 = (bf16[2,512,512]{2,1,0:T(8,128)(2,1)}, bf16[2,512,512]{2,1,0:T(8,128)(2,1)S(1)}, u32[]{:S(2)}, u32[]{:S(2)}) collective-permute-start(bf16[2,512,512]{2,1,0:T(8,128)(2,1)} %get-tuple-element.37), channel_id=1, source_target_pairs={{0,64},{32,96},{64,0},{96,32},{1,65},{33,97},{65,1},{97,33},{2,66}... | collective-permute-start | bytes 3145736 | tf_op jit(solution)/shard_map/ppermute | solution.py:58
  105.8 47.4 %collective-permute-start.3 = (bf16[2,512,512]{2,1,0:T(8,128)(2,1)}, bf16[2,512,512]{2,1,0:T(8,128)(2,1)S(1)}, u32[]{:S(2)}, u32[]{:S(2)}) collective-permute-start(bf16[2,512,512]{2,1,0:T(8,128)(2,1)} %get-tuple-element.37), channel_id=1, source_target_pairs={{0,96},{32,0},{64,32},{96,64},{1,97},{33,1},{65,33},{97,65},{2,98}... | collective-permute-start | bytes 3145736 | tf_op jit(solution)/shard_map/ppermute | solution.py:58
  153.1 3.2 %copy-start.2 = (bf16[512,4096]{1,0:T(8,128)(2,1)S(1)}, bf16[512,4096]{1,0:T(8,128)(2,1)}, u32[]{:S(2)}) copy-start(bf16[512,4096]{1,0:T(8,128)(2,1)} %param.10) | copy-start | bytes 12582916
  174.4 2.2 copy-start
  174.4 31.9 %slice-start = ((s8[8388608]{0:T(1024)(128)(4,1)}), s8[4194304]{0:T(1024)(128)(4,1)S(1)}, s32[]{:S(2)}) async-start(s8[8388608]{0:T(1024)(128)(4,1)} %bitcast.74), calls=%async_computation.5 | async-start | bytes 8388608
  174.9 31.4 %slice-start.1 = ((s8[8388608]{0:T(1024)(128)(4,1)}), s8[4194304]{0:T(1024)(128)(4,1)S(1)}, s32[]{:S(2)}) async-start(s8[8388608]{0:T(1024)(128)(4,1)} %bitcast.74), calls=%async_computation.6 | async-start | bytes 8388608
  176.5 20.4 %collective-permute-start.10 = (bf16[512,256]{1,0:T(8,128)(2,1)S(1)}, bf16[512,256]{1,0:T(8,128)(2,1)S(1)}, u32[]{:S(2)}, u32[]{:S(2)}) collective-permute-start(bf16[512,256]{1,0:T(8,128)(2,1)S(1)} %get-tuple-element.29), channel_id=1, source_target_pairs={{0,112},{16,0},{32,16},{48,32},{64,48},{80,64},{96,80},{112,96},{1... | collective-permute-start | bytes 786440 | tf_op jit(solution)/shard_map/ppermute | solution.py:85
  182.6 20.0 %collective-permute-start.4 = (bf16[512,256]{1,0:T(8,128)(2,1)S(1)}, bf16[512,256]{1,0:T(8,128)(2,1)S(1)}, u32[]{:S(2)}, u32[]{:S(2)}) collective-permute-start(bf16[512,256]{1,0:T(8,128)(2,1)S(1)} %get-tuple-element.35), channel_id=1, source_target_pairs={{0,16},{16,32},{32,48},{48,64},{64,80},{80,96},{96,112},{112,0},{1... | collective-permute-start | bytes 786440 | tf_op jit(solution)/shard_map/ppermute | solution.py:85
  182.6 23.6 %copy-start.3 = (f32[512,1024]{1,0:T(8,128)S(1)}, f32[512,1024]{1,0:T(8,128)}, u32[]{:S(2)}) copy-start(f32[512,1024]{1,0:T(8,128)} %param.9) | copy-start | bytes 6291460
  185.5 26.6 %collective-permute-start.5 = (bf16[512,256]{1,0:T(8,128)(2,1)S(1)}, bf16[512,256]{1,0:T(8,128)(2,1)S(1)}, u32[]{:S(2)}, u32[]{:S(2)}) collective-permute-start(bf16[512,256]{1,0:T(8,128)(2,1)S(1)} %get-tuple-element.34), channel_id=1, source_target_pairs={{0,32},{16,48},{32,64},{48,80},{64,96},{80,112},{96,0},{112,16},{1... | collective-permute-start | bytes 786440 | tf_op jit(solution)/shard_map/ppermute | solution.py:85
  185.6 26.5 %collective-permute-start.6 = (bf16[512,256]{1,0:T(8,128)(2,1)S(1)}, bf16[512,256]{1,0:T(8,128)(2,1)S(1)}, u32[]{:S(2)}, u32[]{:S(2)}) collective-permute-start(bf16[512,256]{1,0:T(8,128)(2,1)S(1)} %get-tuple-element.33), channel_id=1, source_target_pairs={{0,48},{16,64},{32,80},{48,96},{64,112},{80,0},{96,16},{112,32},{1... | collective-permute-start | bytes 786440 | tf_op jit(solution)/shard_map/ppermute | solution.py:85
  187.9 24.2 %collective-permute-start.7 = (bf16[512,256]{1,0:T(8,128)(2,1)S(1)}, bf16[512,256]{1,0:T(8,128)(2,1)S(1)}, u32[]{:S(2)}, u32[]{:S(2)}) collective-permute-start(bf16[512,256]{1,0:T(8,128)(2,1)S(1)} %get-tuple-element.32), channel_id=1, source_target_pairs={{0,64},{16,80},{32,96},{48,112},{64,0},{80,16},{96,32},{112,48},{1... | collective-permute-start | bytes 786440 | tf_op jit(solution)/shard_map/ppermute | solution.py:85
  197.0 15.1 %collective-permute-start.8 = (bf16[512,256]{1,0:T(8,128)(2,1)S(1)}, bf16[512,256]{1,0:T(8,128)(2,1)S(1)}, u32[]{:S(2)}, u32[]{:S(2)}) collective-permute-start(bf16[512,256]{1,0:T(8,128)(2,1)S(1)} %get-tuple-element.31), channel_id=1, source_target_pairs={{0,80},{16,96},{32,112},{48,0},{64,16},{80,32},{96,48},{112,64},{1... | collective-permute-start | bytes 786440 | tf_op jit(solution)/shard_map/ppermute | solution.py:85
  202.6 14.5 %collective-permute-start.9 = (bf16[512,256]{1,0:T(8,128)(2,1)S(1)}, bf16[512,256]{1,0:T(8,128)(2,1)S(1)}, u32[]{:S(2)}, u32[]{:S(2)}) collective-permute-start(bf16[512,256]{1,0:T(8,128)(2,1)S(1)} %get-tuple-element.30), channel_id=1, source_target_pairs={{0,96},{16,112},{32,0},{48,16},{64,32},{80,48},{96,64},{112,80},{1... | collective-permute-start | bytes 786440 | tf_op jit(solution)/shard_map/ppermute | solution.py:85
  212.1 40.2 %copy-start.1 = (f32[512,256]{1,0:T(8,128)S(1)}, f32[512,256]{1,0:T(8,128)}, u32[]{:S(2)}) copy-start(f32[512,256]{1,0:T(8,128)} %param.8) | copy-start | bytes 1572868
Sparse Core Ops, SparseCore 0:
  87.8 55.5 all-gather.2
  161.9 79.2 all-gather.4

commit v11 on v7

--- a/solution.py
+++ b/solution.py
@@ -77,11 +77,10 @@
     sub_rows = jnp.take(row_block, sub_index, axis=0)
     left_part = lax.dot_general(
         row_block, sub_rows, (((1,), (1,)), ((), ())), preferred_element_type=jnp.float32
-    ).astype(jnp.bfloat16)
-    left_part = (
-        left_part.reshape(col_count, row_count, slice_rows, chunk).transpose(1, 0, 2, 3).reshape(HQ, chunk)
     )
-    left_sum = lax.psum_scatter(left_part, ROW, scatter_dimension=0, tiled=True).astype(jnp.float32)
+    left_part = left_part.reshape(col_count, row_count, slice_rows, chunk).transpose(1, 0, 2, 3)
+    left_part = left_part.reshape(row_count, tile_rows, chunk)
+    incoming = lax.all_to_all(left_part.astype(jnp.bfloat16), ROW, 0, 0, tiled=True)
     panel_reordered = (
         column_panel.reshape(row_count, col_count, slice_rows, tile_cols)
         .transpose(1, 0, 2, 3)
@@ -94,8 +93,15 @@
     left_mixed = jnp.dot(left_root, column_panel, preferred_element_type=jnp.float32).astype(
         jnp.bfloat16
     )
+    mixed_rows = lax.all_gather(left_mixed, COL, axis=1, tiled=True)
+    incoming, mixed_rows = lax.optimization_barrier((incoming, mixed_rows))
+    own_part = lax.dynamic_index_in_dim(left_part, row_index, 0, keepdims=False)
+    others = jnp.arange(row_count, dtype=jnp.int32)[:, None, None] != row_index
+    left_sum = own_part + jnp.sum(
+        jnp.where(others, incoming.astype(jnp.float32), 0.0), axis=0
+    )
     update_sum = lax.dot_general(
-        lax.all_gather(left_mixed, COL, axis=1, tiled=True),
+        mixed_rows,
         right_root,
         (((1,), (1,)), ((), ())),
         preferred_element_type=jnp.float32,

time: 319 us -> 262 us (0.82)
  waiting for transfers between devices: 182 us -> 115 us
  starting transfers between devices: 12 us -> 19.4 us
    reduce_scatter x1 -> x0, waiting for transfers between devices: 57.3 us -> none  [shards(): lax.psum_scatter(left_part, ROW, scatter_dimension=0, tiled=True)]
    all_gather x1, waiting for transfers between devices: 53.5 us -> 23.7 us  [shards(): mixed_rows = lax.all_gather(left_mixed, COL, axis=1, tiled=True)]
    all_to_all x0 -> x1, waiting for transfers between devices: none -> 19.7 us  [shards(): lax.all_to_all(left_part.astype(jnp.bfloat16), ROW, 0, 0, tiled=True)]
    all_to_all x0 -> x1, starting transfers between devices: none -> 7.42 us  [shards(): lax.all_to_all(left_part.astype(jnp.bfloat16), ROW, 0, 0, tiled=True)]
  transfers between devices with their start and end apart: 8 -> 8, of which waited for: 7 -> 7; matrix products, arithmetic and copies ran while one was open for 9% -> 12% of each run, Pallas kernels for 0% -> 0%
where the time goes in v11:
time: 262 us
  waiting for transfers between devices  115 us (44%)
  matrix products  31.7 us (12%)
  other arithmetic  30.1 us (11%)
  blocking collectives  29 us (11%)
  local copies, waits for them, and re-layouts  22.8 us (9%)
  starting transfers between devices  19.4 us (7%)
  between operations  14.2 us (5%)
    ppermute x3, waiting for transfers between devices, shards(): lax.ppermute(pair, 'x', [(i, (i + s) % x_count) for i in range(x_count)])  45.3 us
    all_gather x1, waiting for transfers between devices, shards(): mixed_rows = lax.all_gather(left_mixed, COL, axis=1, tiled=True)  23.7 us
    unnamed x1, other arithmetic  22.8 us
    all_to_all x1, waiting for transfers between devices, shards(): lax.all_to_all(left_part.astype(jnp.bfloat16), ROW, 0, 0, tiled=True)  19.7 us
    all_to_all x1, blocking collectives, shards(): lax.all_to_all(row_slice, ROW, split_axis=1, concat_axis=0, tiled=True)  15.8 us
    all_to_all x1, waiting for transfers between devices, shards(): lax.all_to_all(held_rows, COL, split_axis=1, concat_axis=0, tiled=True)  13.9 us
    all_to_all x1, blocking collectives, shards(): lax.all_to_all(grad_tile, COL, split_axis=0, concat_axis=1, tiled=True)  13.2 us
    ppermute x1, waiting for transfers between devices, shards(): other_half = lax.ppermute(grad_tile, 'yh', [(0, 1), (1, 0)])  11.9 us
  transfers between devices with their start and end apart: 8, of which 7 were waited for; matrix products, arithmetic and copies ran while one was open for 12% of the time, Pallas kernels for 0%

profile of v11, /device:TPU:1, one launch (start us, length us, event | category | flops | bytes accessed | tf_op | source)
XLA Modules:
  0.0 261.7 jit_solution(2449368434572296919)
XLA Ops:
  7.2 22.8 %reduce = bf16[524288]{0:T(1024)(128)(2,1)S(1)} reduce(bf16[1,1,524288]{2,1,0:T(2,128)(2,1)} %param.6, bf16[]{:T(256)} %constant.164), dimensions={0,1}, to_apply=%param.6.reduce_sub_computation | reduce | bytes 2097154 | tf_op args[0]
  30.6 1.5 copy.25
  32.2 7.8 %all-to-all-start = ((bf16[64,16,512]{2,0,1:T(8,128)(2,1)}), bf16[64,16,512]{2,0,1:T(8,128)(2,1)S(1)}, u32[]{:S(2)}, u32[]{:S(2)}) async-start(bf16[64,16,512]{2,0,1:T(8,128)(2,1)} %copy.25), calls=%async_computation | async-start | bytes 2097152 | tf_op jit(solution)/shard_map/all_to_all | solution.py:48
  40.1 0.7 constant_dynamic-slice_fusion
  41.0 0.7 subtract_bitcast_fusion
  42.0 13.9 %all-to-all-done = bf16[64,16,512]{2,0,1:T(8,128)(2,1)S(1)} async-done(((bf16[64,16,512]{2,0,1:T(8,128)(2,1)}), bf16[64,16,512]{2,0,1:T(8,128)(2,1)S(1)}, u32[]{:S(2)}, u32[]{:S(2)}) %all-to-all-start) | async-done | bytes 1048608 | tf_op jit(solution)/shard_map/all_to_all | solution.py:48
  55.9 2.0 gather_fusion
  58.0 13.2 %all_to_all.56 = bf16[16,32,512]{2,1,0:T(8,128)(2,1)S(1)} all-to-all(bf16[16,32,512]{2,1,0:T(8,128)(2,1)S(1)} %broadcast_select_fusion.1), channel_id=1, replica_groups=mesh['x'=4,'yh'=2,'chip'=8,'core'=2] {'chip','core'}, dimensions={0} | all-to-all | bytes 1048576 | tf_op jit(solution)/shard_map/all_to_all | solution.py:51
  72.0 15.8 %all_to_all.57 = bf16[32,8,1024]{2,0,1:T(8,128)(2,1)} all-to-all(bf16[32,8,1024]{2,0,1:T(8,128)(2,1)S(1)} %copy.27), channel_id=1, replica_groups=mesh['x'=4,'yh'=2,'chip'=8,'core'=2] {'x','yh'}, dimensions={1} | all-to-all | bytes 1048576 | tf_op jit(solution)/shard_map/all_to_all | solution.py:52
  87.9 1.3 collective-permute-start
  89.3 11.9 %collective-permute-done = bf16[512,512]{1,0:T(8,128)(2,1)S(1)} collective-permute-done((bf16[512,512]{1,0:T(8,128)(2,1)S(1)}, bf16[512,512]{1,0:T(8,128)(2,1)S(1)}, u32[]{:S(2)}, u32[]{:S(2)}) %collective-permute-start) | collective-permute-done | bytes 524320 | tf_op jit(solution)/shard_map/ppermute | solution.py:53
  101.3 2.3 broadcast_in_dim.61
  103.6 1.5 constant_dynamic-update-slice_fusion.3
  105.7 2.1 collective-permute-start.3
  107.8 14.0 %collective-permute-done.1 = bf16[2,512,512]{2,1,0:T(8,128)(2,1)S(1)} collective-permute-done((bf16[2,512,512]{2,1,0:T(8,128)(2,1)}, bf16[2,512,512]{2,1,0:T(8,128)(2,1)S(1)}, u32[]{:S(2)}, u32[]{:S(2)}) %collective-permute-start.1) | collective-permute-done | bytes 1048608 | tf_op jit(solution)/shard_map/ppermute | solution.py:58
  121.8 21.2 %collective-permute-done.2 = bf16[2,512,512]{2,1,0:T(8,128)(2,1)S(1)} collective-permute-done((bf16[2,512,512]{2,1,0:T(8,128)(2,1)}, bf16[2,512,512]{2,1,0:T(8,128)(2,1)S(1)}, u32[]{:S(2)}, u32[]{:S(2)}) %collective-permute-start.2) | collective-permute-done | bytes 1048608 | tf_op jit(solution)/shard_map/ppermute | solution.py:58
  143.0 10.1 %collective-permute-done.3 = bf16[2,512,512]{2,1,0:T(8,128)(2,1)S(1)} collective-permute-done((bf16[2,512,512]{2,1,0:T(8,128)(2,1)}, bf16[2,512,512]{2,1,0:T(8,128)(2,1)S(1)}, u32[]{:S(2)}, u32[]{:S(2)}) %collective-permute-start.3) | collective-permute-done | bytes 1048608 | tf_op jit(solution)/shard_map/ppermute | solution.py:58
  153.1 1.1 constant_dynamic-update-slice_fusion.2
  154.2 1.1 constant_dynamic-update-slice_fusion.1
  155.3 1.1 constant_dynamic-update-slice_fusion
  156.3 5.4 %fusion = bf16[512,512]{0,1:T(8,128)(2,1)} fusion(bf16[4096,512]{1,0:T(8,128)(2,1)} %bitcast.18, bf16[512,4096]{1,0:T(8,128)(2,1)S(1)} %copy-done.2), kind=kOutput, calls=%fused_computation.6 | convolution fusion | flops 2147745792 | bytes 8912896 | tf_op jit(solution)/shard_map/dot_general | solution.py:93
  161.9 6.0 %gather_fusion.1 = bf16[256,1024]{1,0:T(8,128)(2,1)S(1)} fusion(bf16[4096,1024]{1,0:T(8,128)(2,1)} %all-gather.3.cloned.1.call-done, s32[1024]{0:T(1024)S(1)} %pad_clamp_fusion), kind=kCustom, calls=%fused_computation.1 | custom fusion | bytes 1049600 | tf_op jit(solution)/shard_map/jit(_take)/gather | solution.py:77
  167.9 5.8 %fusion.3 = f32[4096,256]{1,0:T(8,128)S(1)} fusion(bf16[4096,1024]{1,0:T(8,128)(2,1)} %all-gather.3.cloned.1.call-done, bf16[256,1024]{1,0:T(8,128)(2,1)S(1)} %gather_fusion.1, pred[256]{0:T(512)(128)(4,1)S(1)} %compare_and_fusion.1), kind=kOutput, calls=%fused_computation.11 | convolution fusion | flops 2147745792 | bytes 13107456 | tf_op jit(solution)/shard_map/dot_general | solution.py:78
  174.3 1.9 copy-done
  176.3 1.8 bitcast_convert_fusion
  178.1 7.4 %all-to-all-start.3 = ((bf16[8,512,256]{2,1,0:T(8,128)(2,1)}), bf16[8,512,256]{2,1,0:T(8,128)(2,1)S(1)}, u32[]{:S(2)}, u32[]{:S(2)}) async-start(bf16[8,512,256]{2,1,0:T(8,128)(2,1)} %bitcast_convert_fusion), calls=%async_computation.3 | async-start | bytes 4194304 | tf_op jit(solution)/shard_map/all_to_all | solution.py:83
  185.6 2.9 %copy.29 = bf16[16,8,32,512]{3,2,1,0:T(8,128)(2,1)S(1)} copy(bf16[16,8,32,512]{3,2,0,1:T(8,128)(2,1)} %bitcast.21) | data formatting | bytes 8388608 | tf_op jit(solution)/shard_map/transpose | solution.py:86
  188.5 9.3 %multiply_add_fusion = f32[512,1024]{1,0:T(8,128)} fusion(f32[512,1024]{1,0:T(8,128)S(1)} %copy-done.3, bf16[4096,512]{1,0:T(8,128)(2,1)S(1)} %bitcast.47, bf16[4096,1024]{1,0:T(8,128)(2,1)} %all-gather.3.cloned.1.call-done), kind=kOutput, calls=%fused_computation.3 | convolution fusion | flops 4296540160 | bytes 16777216 | tf_op jit(solution)/shard_map/dot_general | solution.py:89
  197.7 19.7 %all-to-all-done.3 = bf16[8,512,256]{2,1,0:T(8,128)(2,1)S(1)} async-done(((bf16[8,512,256]{2,1,0:T(8,128)(2,1)}), bf16[8,512,256]{2,1,0:T(8,128)(2,1)S(1)}, u32[]{:S(2)}, u32[]{:S(2)}) %all-to-all-start.3) | async-done | bytes 2097184 | tf_op jit(solution)/shard_map/all_to_all | solution.py:83
  217.5 23.7 %all-gather.5.cloned.1.call-done = bf16[512,8192]{0,1:T(8,128)(2,1)} async-done(((bf16[512,512]{0,1:T(8,128)(2,1)}), bf16[512,8192]{0,1:T(8,128)(2,1)}) %all-gather.5.cloned.1.call-update) | async-done | bytes 8388624 | tf_op jit(solution)/shard_map/all_gather | solution.py:96
  241.7 11.2 %convolution_convert_fusion = bf16[512,512]{1,0:T(8,128)(2,1)} fusion(bf16[512,8192]{0,1:T(8,128)(2,1)} %all-gather.5.cloned.1.call-done, bf16[512,8192]{1,0:T(8,128)(2,1)} %param.11), kind=kOutput, calls=%fused_computation.4 | convolution fusion | flops 4295229440 | bytes 17301504 | tf_op jit(solution)/shard_map/dot_general | solution.py:103
  252.9 2.0 fusion.2
  (36 shorter events, 4.2 us)
Async XLA Ops:
  32.2 23.7 %all-to-all-start = ((bf16[64,16,512]{2,0,1:T(8,128)(2,1)}), bf16[64,16,512]{2,0,1:T(8,128)(2,1)S(1)}, u32[]{:S(2)}, u32[]{:S(2)}) async-start(bf16[64,16,512]{2,0,1:T(8,128)(2,1)} %copy.25), calls=%async_computation | async-start | bytes 2097152 | tf_op jit(solution)/shard_map/all_to_all | solution.py:48
  40.0 113.1 %all-gather.3.cloned.1.call-start = ((), (), s32[]{:S(2)}) async-start(), calls=%async_computation.4 | async-start | bytes 8912896 | tf_op jit(solution)/shard_map/all_gather | solution.py:61
  87.7 153.5 %all-gather.5.cloned.1.call-start = ((), (), s32[]{:S(2)}) async-start(), calls=%async_computation.5 | async-start | bytes 8912896 | tf_op jit(solution)/shard_map/all_gather | solution.py:96
  87.9 13.2 %collective-permute-start = (bf16[512,512]{1,0:T(8,128)(2,1)S(1)}, bf16[512,512]{1,0:T(8,128)(2,1)S(1)}, u32[]{:S(2)}, u32[]{:S(2)}) collective-permute-start(bf16[512,512]{1,0:T(8,128)(2,1)S(1)} %broadcast_select_fusion), channel_id=1, source_target_pairs={{0,16},{16,0},{1,17},{17,1},{2,18},{18,2},{3,19},{19,3},{4,20},{20... | collective-permute-start | bytes 1572872 | tf_op jit(solution)/shard_map/ppermute | solution.py:53
  105.1 16.7 %collective-permute-start.1 = (bf16[2,512,512]{2,1,0:T(8,128)(2,1)}, bf16[2,512,512]{2,1,0:T(8,128)(2,1)S(1)}, u32[]{:S(2)}, u32[]{:S(2)}) collective-permute-start(bf16[2,512,512]{2,1,0:T(8,128)(2,1)} %get-tuple-element.18), channel_id=1, source_target_pairs={{0,32},{32,64},{64,96},{96,0},{1,33},{33,65},{65,97},{97,1},{2,34}... | collective-permute-start | bytes 3145736 | tf_op jit(solution)/shard_map/ppermute | solution.py:58
  105.1 37.9 %collective-permute-start.2 = (bf16[2,512,512]{2,1,0:T(8,128)(2,1)}, bf16[2,512,512]{2,1,0:T(8,128)(2,1)S(1)}, u32[]{:S(2)}, u32[]{:S(2)}) collective-permute-start(bf16[2,512,512]{2,1,0:T(8,128)(2,1)} %get-tuple-element.18), channel_id=1, source_target_pairs={{0,64},{32,96},{64,0},{96,32},{1,65},{33,97},{65,1},{97,33},{2,66}... | collective-permute-start | bytes 3145736 | tf_op jit(solution)/shard_map/ppermute | solution.py:58
  105.7 47.4 %collective-permute-start.3 = (bf16[2,512,512]{2,1,0:T(8,128)(2,1)}, bf16[2,512,512]{2,1,0:T(8,128)(2,1)S(1)}, u32[]{:S(2)}, u32[]{:S(2)}) collective-permute-start(bf16[2,512,512]{2,1,0:T(8,128)(2,1)} %get-tuple-element.18), channel_id=1, source_target_pairs={{0,96},{32,0},{64,32},{96,64},{1,97},{33,1},{65,33},{97,65},{2,98}... | collective-permute-start | bytes 3145736 | tf_op jit(solution)/shard_map/ppermute | solution.py:58
  153.1 3.2 %copy-start.2 = (bf16[512,4096]{1,0:T(8,128)(2,1)S(1)}, bf16[512,4096]{1,0:T(8,128)(2,1)}, u32[]{:S(2)}) copy-start(bf16[512,4096]{1,0:T(8,128)(2,1)} %param.10) | copy-start | bytes 12582916
  174.3 1.9 copy-start
  178.1 39.4 %all-to-all-start.3 = ((bf16[8,512,256]{2,1,0:T(8,128)(2,1)}), bf16[8,512,256]{2,1,0:T(8,128)(2,1)S(1)}, u32[]{:S(2)}, u32[]{:S(2)}) async-start(bf16[8,512,256]{2,1,0:T(8,128)(2,1)} %bitcast_convert_fusion), calls=%async_computation.3 | async-start | bytes 4194304 | tf_op jit(solution)/shard_map/all_to_all | solution.py:83
  185.5 2.9 %copy-start.3 = (f32[512,1024]{1,0:T(8,128)S(1)}, f32[512,1024]{1,0:T(8,128)}, u32[]{:S(2)}) copy-start(f32[512,1024]{1,0:T(8,128)} %param.9) | copy-start | bytes 6291460
  241.7 11.2 %copy-start.1 = (f32[512,256]{1,0:T(8,128)S(1)}, f32[512,256]{1,0:T(8,128)}, u32[]{:S(2)}) copy-start(f32[512,256]{1,0:T(8,128)} %param.8) | copy-start | bytes 1572868
Sparse Core Ops, SparseCore 0:
  87.8 55.5 all-gather.2
  161.9 79.2 all-gather.4

commit v12 on v10

--- a/solution.py
+++ b/solution.py
@@ -51,6 +51,7 @@
     row_slice = lax.all_to_all(grad_tile, COL, split_axis=0, concat_axis=1, tiled=True)
     block_piece = lax.all_to_all(row_slice, ROW, split_axis=1, concat_axis=0, tiled=True)
     other_half = lax.ppermute(grad_tile, "yh", [(0, 1), (1, 0)])
+    other_half, block_piece = lax.optimization_barrier((other_half, block_piece))
     first = jnp.where(y_half == 0, grad_tile, other_half)
     second = jnp.where(y_half == 0, other_half, grad_tile)
     pair = jnp.stack([first, second])

time: 262 us -> 249 us (0.950)
  blocking collectives: 29 us -> 0 us
  starting transfers between devices: 28 us -> 44.4 us
  waiting for transfers between devices: 111 us -> 108 us
    all_to_all x2 -> x0, blocking collectives: 29 us -> none  [the longest x1 15.8 us: shards(): lax.all_to_all(row_slice, ROW, split_axis=1, concat_axis=0, tiled=True)]
    all_to_all x0 -> x2, waiting for transfers between devices: none -> 13.1 us  [the longest x1 7.32 us: shards(): lax.all_to_all(grad_tile, COL, split_axis=0, concat_axis=1, tiled=True)]
    all_to_all x0 -> x2, starting transfers between devices: none -> 10.3 us  [the longest x1 6.06 us: shards(): lax.all_to_all(row_slice, ROW, split_axis=1, concat_axis=0, tiled=True)]
    ppermute x1, waiting for transfers between devices: 11.9 us -> 2.77 us  [shards(): other_half = lax.ppermute(grad_tile, 'yh', [(0, 1), (1, 0)])]
    ppermute x7, waiting for transfers between devices: 15.8 us -> 11.5 us  [shards(): lax.ppermute(lax.dynamic_index_in_dim(outgoing, (row_index + s) % row_cou...]
    ppermute x7, starting transfers between devices: 16.1 us -> 20.3 us  [shards(): lax.ppermute(lax.dynamic_index_in_dim(outgoing, (row_index + s) % row_cou...]
    all_gather x1, waiting for transfers between devices: 24.1 us -> 21.4 us  [shards(): mixed_rows = lax.all_gather(left_mixed, COL, axis=1, tiled=True)]
  transfers between devices with their start and end apart: 14 -> 16, of which waited for: 9 -> 10; matrix products, arithmetic and copies ran while one was open for 11% -> 12% of each run, Pallas kernels for 0% -> 0%
where the time goes in v12:
time: 249 us; the launch traced here: 248 us
  waiting for transfers between devices  108 us (43%)
  starting transfers between devices  44.4 us (18%)
  other arithmetic  29.2 us (12%)
  matrix products  28.2 us (11%)
  local copies, waits for them, and re-layouts  23.9 us (10%)
  between operations  14.4 us (6%)
    ppermute x3, waiting for transfers between devices, shards(): lax.ppermute(pair, 'x', [(i, (i + s) % x_count) for i in range(x_count)])  45.4 us
    unnamed x2, other arithmetic  22.8 us
    all_gather x1, waiting for transfers between devices, shards(): mixed_rows = lax.all_gather(left_mixed, COL, axis=1, tiled=True)  21.4 us
    ppermute x7, starting transfers between devices, shards(): lax.ppermute(lax.dynamic_index_in_dim(outgoing, (row_index + s) % row_cou...  20.3 us
    all_to_all x1, waiting for transfers between devices, shards(): lax.all_to_all(held_rows, COL, split_axis=1, concat_axis=0, tiled=True)  13.9 us
    ppermute x7, waiting for transfers between devices, shards(): lax.ppermute(lax.dynamic_index_in_dim(outgoing, (row_index + s) % row_cou...  11.5 us
    dot_general x1, matrix products, shards(): lax.dot_general(mixed_rows, right_root, (((1,), (1,)), ((), ())), preferr...  11.1 us
    all_to_all x1, starting transfers between devices, shards(): lax.all_to_all(held_rows, COL, split_axis=1, concat_axis=0, tiled=True)  7.84 us
  transfers between devices with their start and end apart: 16, of which 10 were waited for; matrix products, arithmetic and copies ran while one was open for 12% of the time, Pallas kernels for 0%

profile of v12, /device:TPU:1, one launch (start us, length us, event | category | flops | bytes accessed | tf_op | source)
XLA Modules:
  0.0 248.4 jit_solution(1788222238391534180)
XLA Ops:
  7.2 22.8 %reduce = bf16[524288]{0:T(1024)(128)(2,1)S(1)} reduce(bf16[1,1,524288]{2,1,0:T(2,128)(2,1)} %param.6, bf16[]{:T(256)} %constant.214), dimensions={0,1}, to_apply=%param.6.reduce_sub_computation | reduce | bytes 2097154 | tf_op args[0]
  30.6 1.5 copy.25
  32.2 7.8 %all-to-all-start = ((bf16[64,16,512]{2,0,1:T(8,128)(2,1)}), bf16[64,16,512]{2,0,1:T(8,128)(2,1)S(1)}, u32[]{:S(2)}, u32[]{:S(2)}) async-start(bf16[64,16,512]{2,0,1:T(8,128)(2,1)} %copy.25), calls=%async_computation | async-start | bytes 2097152 | tf_op jit(solution)/shard_map/all_to_all | solution.py:48
  41.9 13.9 %all-to-all-done = bf16[64,16,512]{2,0,1:T(8,128)(2,1)S(1)} async-done(((bf16[64,16,512]{2,0,1:T(8,128)(2,1)}), bf16[64,16,512]{2,0,1:T(8,128)(2,1)S(1)}, u32[]{:S(2)}, u32[]{:S(2)}) %all-to-all-start) | async-done | bytes 1048608 | tf_op jit(solution)/shard_map/all_to_all | solution.py:48
  55.9 2.0 gather_fusion
  58.8 4.2 %all-to-all-start.1 = ((bf16[16,32,512]{2,1,0:T(8,128)(2,1)}), bf16[16,32,512]{2,1,0:T(8,128)(2,1)S(1)}, u32[]{:S(2)}, u32[]{:S(2)}) async-start(bf16[16,32,512]{2,1,0:T(8,128)(2,1)} %broadcast_select_fusion.1), calls=%async_computation.1 | async-start | bytes 1048576 | tf_op jit(solution)/shard_map/all_to_all | solution.py:51
  63.2 2.7 %collective-permute-start = (bf16[512,512]{1,0:T(8,128)(2,1)S(1)}, bf16[512,512]{1,0:T(8,128)(2,1)S(1)}, u32[]{:S(2)}, u32[]{:S(2)}) collective-permute-start(bf16[512,512]{1,0:T(8,128)(2,1)S(1)} %broadcast_select_fusion), channel_id=1, source_target_pairs={{0,16},{16,0},{1,17},{17,1},{2,18},{18,2},{3,19},{19,3},{4,20},{20... | collective-permute-start | bytes 1572872 | tf_op jit(solution)/shard_map/ppermute | solution.py:53
  65.9 7.3 %all-to-all-done.1 = bf16[16,32,512]{2,1,0:T(8,128)(2,1)S(1)} async-done(((bf16[16,32,512]{2,1,0:T(8,128)(2,1)}), bf16[16,32,512]{2,1,0:T(8,128)(2,1)S(1)}, u32[]{:S(2)}, u32[]{:S(2)}) %all-to-all-start.1) | async-done | bytes 524320 | tf_op jit(solution)/shard_map/all_to_all | solution.py:51
  74.7 6.1 %all-to-all-start.2 = ((bf16[32,8,1024]{2,0,1:T(8,128)(2,1)}), bf16[32,8,1024]{2,0,1:T(8,128)(2,1)S(1)}, u32[]{:S(2)}, u32[]{:S(2)}) async-start(bf16[32,8,1024]{2,0,1:T(8,128)(2,1)} %copy.27), calls=%async_computation.2 | async-start | bytes 1048576 | tf_op jit(solution)/shard_map/all_to_all | solution.py:52
  80.8 2.8 %collective-permute-done = bf16[512,512]{1,0:T(8,128)(2,1)S(1)} collective-permute-done((bf16[512,512]{1,0:T(8,128)(2,1)S(1)}, bf16[512,512]{1,0:T(8,128)(2,1)S(1)}, u32[]{:S(2)}, u32[]{:S(2)}) %collective-permute-start) | collective-permute-done | bytes 524320 | tf_op jit(solution)/shard_map/ppermute | solution.py:53
  83.6 5.8 %all-to-all-done.2 = bf16[32,8,1024]{2,0,1:T(8,128)(2,1)S(1)} async-done(((bf16[32,8,1024]{2,0,1:T(8,128)(2,1)}), bf16[32,8,1024]{2,0,1:T(8,128)(2,1)S(1)}, u32[]{:S(2)}, u32[]{:S(2)}) %all-to-all-start.2) | async-done | bytes 524320 | tf_op jit(solution)/shard_map/all_to_all | solution.py:52
  90.5 2.4 broadcast_in_dim.47
  92.8 1.5 constant_dynamic-update-slice_fusion.3
  94.6 1.7 collective-permute-start.2
  97.6 20.3 %collective-permute-done.1 = bf16[2,512,512]{2,1,0:T(8,128)(2,1)S(1)} collective-permute-done((bf16[2,512,512]{2,1,0:T(8,128)(2,1)}, bf16[2,512,512]{2,1,0:T(8,128)(2,1)S(1)}, u32[]{:S(2)}, u32[]{:S(2)}) %collective-permute-start.1) | collective-permute-done | bytes 1048608 | tf_op jit(solution)/shard_map/ppermute | solution.py:59
  117.9 20.6 %collective-permute-done.2 = bf16[2,512,512]{2,1,0:T(8,128)(2,1)S(1)} collective-permute-done((bf16[2,512,512]{2,1,0:T(8,128)(2,1)}, bf16[2,512,512]{2,1,0:T(8,128)(2,1)S(1)}, u32[]{:S(2)}, u32[]{:S(2)}) %collective-permute-start.2) | collective-permute-done | bytes 1048608 | tf_op jit(solution)/shard_map/ppermute | solution.py:59
  138.5 4.5 %collective-permute-done.3 = bf16[2,512,512]{2,1,0:T(8,128)(2,1)S(1)} collective-permute-done((bf16[2,512,512]{2,1,0:T(8,128)(2,1)}, bf16[2,512,512]{2,1,0:T(8,128)(2,1)S(1)}, u32[]{:S(2)}, u32[]{:S(2)}) %collective-permute-start.3) | collective-permute-done | bytes 1048608 | tf_op jit(solution)/shard_map/ppermute | solution.py:59
  146.2 5.4 %fusion = bf16[512,512]{0,1:T(8,128)(2,1)} fusion(bf16[4096,512]{1,0:T(8,128)(2,1)} %bitcast.25, bf16[512,4096]{1,0:T(8,128)(2,1)S(1)} %copy-done.3), kind=kOutput, calls=%fused_computation.5 | convolution fusion | flops 2147745792 | bytes 8912896 | tf_op jit(solution)/shard_map/dot_general | solution.py:102
  151.8 6.0 %gather_fusion.1 = bf16[256,1024]{1,0:T(8,128)(2,1)S(1)} fusion(bf16[4096,1024]{1,0:T(8,128)(2,1)} %all-gather.3.cloned.1.call-done, s32[1024]{0:T(1024)S(1)} %pad_clamp_fusion), kind=kCustom, calls=%fused_computation.1 | custom fusion | bytes 1049600 | tf_op jit(solution)/shard_map/jit(_take)/gather | solution.py:78
  157.8 5.8 %fusion.9 = f32[4096,256]{1,0:T(8,128)S(1)} fusion(bf16[4096,1024]{1,0:T(8,128)(2,1)} %all-gather.3.cloned.1.call-done, bf16[256,1024]{1,0:T(8,128)(2,1)S(1)} %gather_fusion.1, pred[256]{0:T(512)(128)(4,1)S(1)} %compare_and_fusion.1), kind=kOutput, calls=%fused_computation.16 | convolution fusion | flops 2147745792 | bytes 13107456 | tf_op jit(solution)/shard_map/dot_general | solution.py:79
  166.3 4.7 %collective-permute-start.10 = (bf16[512,256]{1,0:T(8,128)(2,1)S(1)}, bf16[512,256]{1,0:T(8,128)(2,1)S(1)}, u32[]{:S(2)}, u32[]{:S(2)}) collective-permute-start(bf16[512,256]{1,0:T(8,128)(2,1)S(1)} %get-tuple-element.33), channel_id=1, source_target_pairs={{0,112},{16,0},{32,16},{48,32},{64,48},{80,64},{96,80},{112,96},{1... | collective-permute-start | bytes 786440 | tf_op jit(solution)/shard_map/ppermute | solution.py:86
  171.0 2.9 %copy.29 = bf16[16,8,32,512]{3,2,1,0:T(8,128)(2,1)S(1)} copy(bf16[16,8,32,512]{3,2,0,1:T(8,128)(2,1)} %bitcast.28) | data formatting | bytes 8388608 | tf_op jit(solution)/shard_map/transpose | solution.py:95
  174.0 3.9 %collective-permute-start.6 = (bf16[512,256]{1,0:T(8,128)(2,1)S(1)}, bf16[512,256]{1,0:T(8,128)(2,1)S(1)}, u32[]{:S(2)}, u32[]{:S(2)}) collective-permute-start(bf16[512,256]{1,0:T(8,128)(2,1)S(1)} %get-tuple-element.37), channel_id=1, source_target_pairs={{0,48},{16,64},{32,80},{48,96},{64,112},{80,0},{96,16},{112,32},{1... | collective-permute-start | bytes 786440 | tf_op jit(solution)/shard_map/ppermute | solution.py:86
  177.8 2.4 collective-permute-start.7
  180.3 6.4 %collective-permute-done.10 = bf16[512,256]{1,0:T(8,128)(2,1)S(1)} collective-permute-done((bf16[512,256]{1,0:T(8,128)(2,1)S(1)}, bf16[512,256]{1,0:T(8,128)(2,1)S(1)}, u32[]{:S(2)}, u32[]{:S(2)}) %collective-permute-start.10) | collective-permute-done | bytes 262176 | tf_op jit(solution)/shard_map/ppermute | solution.py:86
  186.7 6.6 %collective-permute-start.8 = (bf16[512,256]{1,0:T(8,128)(2,1)S(1)}, bf16[512,256]{1,0:T(8,128)(2,1)S(1)}, u32[]{:S(2)}, u32[]{:S(2)}) collective-permute-start(bf16[512,256]{1,0:T(8,128)(2,1)S(1)} %get-tuple-element.35), channel_id=1, source_target_pairs={{0,80},{16,96},{32,112},{48,0},{64,16},{80,32},{96,48},{112,64},{1... | collective-permute-start | bytes 786440 | tf_op jit(solution)/shard_map/ppermute | solution.py:86
  193.4 2.6 %collective-permute-start.9 = (bf16[512,256]{1,0:T(8,128)(2,1)S(1)}, bf16[512,256]{1,0:T(8,128)(2,1)S(1)}, u32[]{:S(2)}, u32[]{:S(2)}) collective-permute-start(bf16[512,256]{1,0:T(8,128)(2,1)S(1)} %get-tuple-element.34), channel_id=1, source_target_pairs={{0,96},{16,112},{32,0},{48,16},{64,32},{80,48},{96,64},{112,80},{1... | collective-permute-start | bytes 786440 | tf_op jit(solution)/shard_map/ppermute | solution.py:86
  196.0 5.8 %multiply_add_fusion = f32[512,1024]{1,0:T(8,128)} fusion(f32[512,1024]{1,0:T(8,128)S(1)} %copy-done.4, bf16[4096,512]{1,0:T(8,128)(2,1)S(1)} %bitcast.72, bf16[4096,1024]{1,0:T(8,128)(2,1)S(1)} %bitcast.75), kind=kOutput, calls=%fused_computation.2 | convolution fusion | flops 4296540160 | bytes 16777216 | tf_op jit(solution)/shard_map/dot_general | solution.py:98
  201.8 5.0 %collective-permute-done.9 = bf16[512,256]{1,0:T(8,128)(2,1)S(1)} collective-permute-done((bf16[512,256]{1,0:T(8,128)(2,1)S(1)}, bf16[512,256]{1,0:T(8,128)(2,1)S(1)}, u32[]{:S(2)}, u32[]{:S(2)}) %collective-permute-start.9) | collective-permute-done | bytes 262176 | tf_op jit(solution)/shard_map/ppermute | solution.py:86
  206.9 21.4 %all-gather.5.cloned.1.call-done = bf16[512,8192]{0,1:T(8,128)(2,1)} async-done(((bf16[512,512]{0,1:T(8,128)(2,1)}), bf16[512,8192]{0,1:T(8,128)(2,1)}) %all-gather.5.cloned.1.call-update) | async-done | bytes 8388624 | tf_op jit(solution)/shard_map/all_gather | solution.py:105
  228.3 11.1 %convolution_convert_fusion = bf16[512,512]{1,0:T(8,128)(2,1)} fusion(bf16[512,8192]{0,1:T(8,128)(2,1)} %all-gather.5.cloned.1.call-done, bf16[512,8192]{1,0:T(8,128)(2,1)} %param.11), kind=kOutput, calls=%fused_computation.3 | convolution fusion | flops 4295229440 | bytes 17301504 | tf_op jit(solution)/shard_map/dot_general | solution.py:110
  239.4 2.1 fusion.8
  (56 shorter events, 13.7 us)
Async XLA Ops:
  32.2 23.7 %all-to-all-start = ((bf16[64,16,512]{2,0,1:T(8,128)(2,1)}), bf16[64,16,512]{2,0,1:T(8,128)(2,1)S(1)}, u32[]{:S(2)}, u32[]{:S(2)}) async-start(bf16[64,16,512]{2,0,1:T(8,128)(2,1)} %copy.25), calls=%async_computation | async-start | bytes 2097152 | tf_op jit(solution)/shard_map/all_to_all | solution.py:48
  58.8 14.4 %all-to-all-start.1 = ((bf16[16,32,512]{2,1,0:T(8,128)(2,1)}), bf16[16,32,512]{2,1,0:T(8,128)(2,1)S(1)}, u32[]{:S(2)}, u32[]{:S(2)}) async-start(bf16[16,32,512]{2,1,0:T(8,128)(2,1)} %broadcast_select_fusion.1), calls=%async_computation.1 | async-start | bytes 1048576 | tf_op jit(solution)/shard_map/all_to_all | solution.py:51
  63.2 20.5 %collective-permute-start = (bf16[512,512]{1,0:T(8,128)(2,1)S(1)}, bf16[512,512]{1,0:T(8,128)(2,1)S(1)}, u32[]{:S(2)}, u32[]{:S(2)}) collective-permute-start(bf16[512,512]{1,0:T(8,128)(2,1)S(1)} %broadcast_select_fusion), channel_id=1, source_target_pairs={{0,16},{16,0},{1,17},{17,1},{2,18},{18,2},{3,19},{19,3},{4,20},{20... | collective-permute-start | bytes 1572872 | tf_op jit(solution)/shard_map/ppermute | solution.py:53
  74.7 14.7 %all-to-all-start.2 = ((bf16[32,8,1024]{2,0,1:T(8,128)(2,1)}), bf16[32,8,1024]{2,0,1:T(8,128)(2,1)S(1)}, u32[]{:S(2)}, u32[]{:S(2)}) async-start(bf16[32,8,1024]{2,0,1:T(8,128)(2,1)} %copy.27), calls=%async_computation.2 | async-start | bytes 1048576 | tf_op jit(solution)/shard_map/all_to_all | solution.py:52
  80.8 62.2 %all-gather.3.cloned.1.call-start = ((), (), s32[]{:S(2)}) async-start(), calls=%async_computation.3 | async-start | bytes 8912896 | tf_op jit(solution)/shard_map/all_gather | solution.py:62
  89.4 0.8 copy-start.1
  90.2 138.0 %all-gather.5.cloned.1.call-start = ((), (), s32[]{:S(2)}) async-start(), calls=%async_computation.4 | async-start | bytes 8912896 | tf_op jit(solution)/shard_map/all_gather | solution.py:105
  94.4 23.5 %collective-permute-start.1 = (bf16[2,512,512]{2,1,0:T(8,128)(2,1)}, bf16[2,512,512]{2,1,0:T(8,128)(2,1)S(1)}, u32[]{:S(2)}, u32[]{:S(2)}) collective-permute-start(bf16[2,512,512]{2,1,0:T(8,128)(2,1)} %get-tuple-element.41), channel_id=1, source_target_pairs={{0,32},{32,64},{64,96},{96,0},{1,33},{33,65},{65,97},{97,1},{2,34}... | collective-permute-start | bytes 3145736 | tf_op jit(solution)/shard_map/ppermute | solution.py:59
  94.6 43.9 %collective-permute-start.2 = (bf16[2,512,512]{2,1,0:T(8,128)(2,1)}, bf16[2,512,512]{2,1,0:T(8,128)(2,1)S(1)}, u32[]{:S(2)}, u32[]{:S(2)}) collective-permute-start(bf16[2,512,512]{2,1,0:T(8,128)(2,1)} %get-tuple-element.41), channel_id=1, source_target_pairs={{0,64},{32,96},{64,0},{96,32},{1,65},{33,97},{65,1},{97,33},{2,66}... | collective-permute-start | bytes 3145736 | tf_op jit(solution)/shard_map/ppermute | solution.py:59
  96.3 46.7 %collective-permute-start.3 = (bf16[2,512,512]{2,1,0:T(8,128)(2,1)}, bf16[2,512,512]{2,1,0:T(8,128)(2,1)S(1)}, u32[]{:S(2)}, u32[]{:S(2)}) collective-permute-start(bf16[2,512,512]{2,1,0:T(8,128)(2,1)} %get-tuple-element.41), channel_id=1, source_target_pairs={{0,96},{32,0},{64,32},{96,64},{1,97},{33,1},{65,33},{97,65},{2,98}... | collective-permute-start | bytes 3145736 | tf_op jit(solution)/shard_map/ppermute | solution.py:59
  143.0 3.2 %copy-start.3 = (bf16[512,4096]{1,0:T(8,128)(2,1)S(1)}, bf16[512,4096]{1,0:T(8,128)(2,1)}, u32[]{:S(2)}) copy-start(bf16[512,4096]{1,0:T(8,128)(2,1)} %param.10) | copy-start | bytes 12582916
  164.2 2.1 copy-start
  164.2 31.7 %slice-start = ((s8[8388608]{0:T(1024)(128)(4,1)}), s8[4194304]{0:T(1024)(128)(4,1)S(1)}, s32[]{:S(2)}) async-start(s8[8388608]{0:T(1024)(128)(4,1)} %bitcast.74), calls=%async_computation.5 | async-start | bytes 8388608
  164.7 31.2 %slice-start.1 = ((s8[8388608]{0:T(1024)(128)(4,1)}), s8[4194304]{0:T(1024)(128)(4,1)S(1)}, s32[]{:S(2)}) async-start(s8[8388608]{0:T(1024)(128)(4,1)} %bitcast.74), calls=%async_computation.6 | async-start | bytes 8388608
  166.3 20.4 %collective-permute-start.10 = (bf16[512,256]{1,0:T(8,128)(2,1)S(1)}, bf16[512,256]{1,0:T(8,128)(2,1)S(1)}, u32[]{:S(2)}, u32[]{:S(2)}) collective-permute-start(bf16[512,256]{1,0:T(8,128)(2,1)S(1)} %get-tuple-element.33), channel_id=1, source_target_pairs={{0,112},{16,0},{32,16},{48,32},{64,48},{80,64},{96,80},{112,96},{1... | collective-permute-start | bytes 786440 | tf_op jit(solution)/shard_map/ppermute | solution.py:86
  171.0 22.4 %collective-permute-start.4 = (bf16[512,256]{1,0:T(8,128)(2,1)S(1)}, bf16[512,256]{1,0:T(8,128)(2,1)S(1)}, u32[]{:S(2)}, u32[]{:S(2)}) collective-permute-start(bf16[512,256]{1,0:T(8,128)(2,1)S(1)} %get-tuple-element.39), channel_id=1, source_target_pairs={{0,16},{16,32},{32,48},{48,64},{64,80},{80,96},{96,112},{112,0},{1... | collective-permute-start | bytes 786440 | tf_op jit(solution)/shard_map/ppermute | solution.py:86
  171.0 24.9 %copy-start.4 = (f32[512,1024]{1,0:T(8,128)S(1)}, f32[512,1024]{1,0:T(8,128)}, u32[]{:S(2)}) copy-start(f32[512,1024]{1,0:T(8,128)} %param.9) | copy-start | bytes 6291460
  173.9 27.9 %collective-permute-start.5 = (bf16[512,256]{1,0:T(8,128)(2,1)S(1)}, bf16[512,256]{1,0:T(8,128)(2,1)S(1)}, u32[]{:S(2)}, u32[]{:S(2)}) collective-permute-start(bf16[512,256]{1,0:T(8,128)(2,1)S(1)} %get-tuple-element.38), channel_id=1, source_target_pairs={{0,32},{16,48},{32,64},{48,80},{64,96},{80,112},{96,0},{112,16},{1... | collective-permute-start | bytes 786440 | tf_op jit(solution)/shard_map/ppermute | solution.py:86
  174.0 27.8 %collective-permute-start.6 = (bf16[512,256]{1,0:T(8,128)(2,1)S(1)}, bf16[512,256]{1,0:T(8,128)(2,1)S(1)}, u32[]{:S(2)}, u32[]{:S(2)}) collective-permute-start(bf16[512,256]{1,0:T(8,128)(2,1)S(1)} %get-tuple-element.37), channel_id=1, source_target_pairs={{0,48},{16,64},{32,80},{48,96},{64,112},{80,0},{96,16},{112,32},{1... | collective-permute-start | bytes 786440 | tf_op jit(solution)/shard_map/ppermute | solution.py:86
  177.8 24.0 %collective-permute-start.7 = (bf16[512,256]{1,0:T(8,128)(2,1)S(1)}, bf16[512,256]{1,0:T(8,128)(2,1)S(1)}, u32[]{:S(2)}, u32[]{:S(2)}) collective-permute-start(bf16[512,256]{1,0:T(8,128)(2,1)S(1)} %get-tuple-element.36), channel_id=1, source_target_pairs={{0,64},{16,80},{32,96},{48,112},{64,0},{80,16},{96,32},{112,48},{1... | collective-permute-start | bytes 786440 | tf_op jit(solution)/shard_map/ppermute | solution.py:86
  186.7 15.1 %collective-permute-start.8 = (bf16[512,256]{1,0:T(8,128)(2,1)S(1)}, bf16[512,256]{1,0:T(8,128)(2,1)S(1)}, u32[]{:S(2)}, u32[]{:S(2)}) collective-permute-start(bf16[512,256]{1,0:T(8,128)(2,1)S(1)} %get-tuple-element.35), channel_id=1, source_target_pairs={{0,80},{16,96},{32,112},{48,0},{64,16},{80,32},{96,48},{112,64},{1... | collective-permute-start | bytes 786440 | tf_op jit(solution)/shard_map/ppermute | solution.py:86
  193.4 13.5 %collective-permute-start.9 = (bf16[512,256]{1,0:T(8,128)(2,1)S(1)}, bf16[512,256]{1,0:T(8,128)(2,1)S(1)}, u32[]{:S(2)}, u32[]{:S(2)}) collective-permute-start(bf16[512,256]{1,0:T(8,128)(2,1)S(1)} %get-tuple-element.34), channel_id=1, source_target_pairs={{0,96},{16,112},{32,0},{48,16},{64,32},{80,48},{96,64},{112,80},{1... | collective-permute-start | bytes 786440 | tf_op jit(solution)/shard_map/ppermute | solution.py:86
  201.8 37.6 %copy-start.2 = (f32[512,256]{1,0:T(8,128)S(1)}, f32[512,256]{1,0:T(8,128)}, u32[]{:S(2)}) copy-start(f32[512,256]{1,0:T(8,128)} %param.8) | copy-start | bytes 1572868
Sparse Core Ops, SparseCore 0:
  90.4 52.3 all-gather.2
  151.8 76.4 all-gather.4

commit v13 on v12

--- a/solution.py
+++ b/solution.py
@@ -60,7 +60,6 @@
         for s in range(1, x_count)
     ]
     row_block = lax.all_gather(block_piece, COL, axis=0, tiled=True)
-    moved, row_block = lax.optimization_barrier((moved, row_block))
     panel_parts = jnp.zeros((row_count, tile_rows, tile_cols), grad_tile.dtype)
     panel_parts = lax.dynamic_update_slice_in_dim(panel_parts, pair, 2 * x_index, 0)
     for s in range(1, x_count):
@@ -68,6 +67,12 @@
             panel_parts, moved[s - 1], 2 * ((x_index - s) % x_count), 0
         )
     column_panel = panel_parts.reshape(HQ, tile_cols)
+    left_mixed = jnp.dot(left_root, column_panel, preferred_element_type=jnp.float32).astype(
+        jnp.bfloat16
+    )
+    column_panel, left_mixed, row_block = lax.optimization_barrier(
+        (column_panel, left_mixed, row_block)
+    )
     col_index = lax.axis_index(COL)
     sub = jnp.arange(chunk, dtype=jnp.int32)
     sub_index = (
@@ -99,9 +104,6 @@
         panel_reordered, row_block, (((0,), (0,)), ((), ())), preferred_element_type=jnp.float32
     )
     right_new = stat_decay * right_stat + right_gram * (1.0 / math.sqrt(HQ))
-    left_mixed = jnp.dot(left_root, column_panel, preferred_element_type=jnp.float32).astype(
-        jnp.bfloat16
-    )
     mixed_rows = lax.all_gather(left_mixed, COL, axis=1, tiled=True)
     incoming, mixed_rows = lax.optimization_barrier((incoming, mixed_rows))
     left_sum = lax.dynamic_index_in_dim(left_part, row_index, 0, keepdims=False)

time: 249 us -> 247 us (level)
  starting transfers between devices: 44.4 us -> 40.2 us
    ppermute x7, waiting for transfers between devices: 11.5 us -> 15.8 us  [shards(): lax.ppermute(lax.dynamic_index_in_dim(outgoing, (row_index + s) % row_cou...]
    ppermute x7, starting transfers between devices: 20.3 us -> 16 us  [shards(): lax.ppermute(lax.dynamic_index_in_dim(outgoing, (row_index + s) % row_cou...]
  transfers between devices with their start and end apart: 16 -> 16, of which waited for: 10 -> 11; matrix products, arithmetic and copies ran while one was open for 12% -> 15% of each run, Pallas kernels for 0% -> 0%
where the time goes in v13:
time: 247 us; the launch traced here: 246 us
  waiting for transfers between devices  110 us (45%)
  starting transfers between devices  40.2 us (16%)
  other arithmetic  29.2 us (12%)
  matrix products  28.2 us (11%)
  local copies, waits for them, and re-layouts  23.9 us (10%)
  between operations  14.4 us (6%)
    ppermute x3, waiting for transfers between devices, shards(): lax.ppermute(pair, 'x', [(i, (i + s) % x_count) for i in range(x_count)])  43.3 us
    unnamed x2, other arithmetic  22.8 us
    all_gather x1, waiting for transfers between devices, shards(): mixed_rows = lax.all_gather(left_mixed, COL, axis=1, tiled=True)  21.4 us
    ppermute x7, starting transfers between devices, shards(): lax.ppermute(lax.dynamic_index_in_dim(outgoing, (row_index + s) % row_cou...  16 us
    ppermute x7, waiting for transfers between devices, shards(): lax.ppermute(lax.dynamic_index_in_dim(outgoing, (row_index + s) % row_cou...  15.8 us
    all_to_all x1, waiting for transfers between devices, shards(): lax.all_to_all(held_rows, COL, split_axis=1, concat_axis=0, tiled=True)  13.9 us
    dot_general x1, matrix products, shards(): lax.dot_general(mixed_rows, right_root, (((1,), (1,)), ((), ())), preferr...  11.1 us
    all_to_all x1, starting transfers between devices, shards(): lax.all_to_all(held_rows, COL, split_axis=1, concat_axis=0, tiled=True)  7.84 us
  transfers between devices with their start and end apart: 16, of which 11 were waited for; matrix products, arithmetic and copies ran while one was open for 15% of the time, Pallas kernels for 0%

profile of v13, /device:TPU:1, one launch (start us, length us, event | category | flops | bytes accessed | tf_op | source)
XLA Modules:
  0.0 246.3 jit_solution(15729284126487772599)
XLA Ops:
  7.2 22.8 %reduce = bf16[524288]{0:T(1024)(128)(2,1)S(1)} reduce(bf16[1,1,524288]{2,1,0:T(2,128)(2,1)} %param.6, bf16[]{:T(256)} %constant.214), dimensions={0,1}, to_apply=%param.6.reduce_sub_computation | reduce | bytes 2097154 | tf_op args[0]
  30.6 1.5 copy.25
  32.2 7.8 %all-to-all-start = ((bf16[64,16,512]{2,0,1:T(8,128)(2,1)}), bf16[64,16,512]{2,0,1:T(8,128)(2,1)S(1)}, u32[]{:S(2)}, u32[]{:S(2)}) async-start(bf16[64,16,512]{2,0,1:T(8,128)(2,1)} %copy.25), calls=%async_computation | async-start | bytes 2097152 | tf_op jit(solution)/shard_map/all_to_all | solution.py:48
  41.9 13.9 %all-to-all-done = bf16[64,16,512]{2,0,1:T(8,128)(2,1)S(1)} async-done(((bf16[64,16,512]{2,0,1:T(8,128)(2,1)}), bf16[64,16,512]{2,0,1:T(8,128)(2,1)S(1)}, u32[]{:S(2)}, u32[]{:S(2)}) %all-to-all-start) | async-done | bytes 1048608 | tf_op jit(solution)/shard_map/all_to_all | solution.py:48
  55.9 2.0 gather_fusion
  58.8 4.2 %all-to-all-start.1 = ((bf16[16,32,512]{2,1,0:T(8,128)(2,1)}), bf16[16,32,512]{2,1,0:T(8,128)(2,1)S(1)}, u32[]{:S(2)}, u32[]{:S(2)}) async-start(bf16[16,32,512]{2,1,0:T(8,128)(2,1)} %broadcast_select_fusion.1), calls=%async_computation.1 | async-start | bytes 1048576 | tf_op jit(solution)/shard_map/all_to_all | solution.py:51
  63.2 2.7 %collective-permute-start = (bf16[512,512]{1,0:T(8,128)(2,1)S(1)}, bf16[512,512]{1,0:T(8,128)(2,1)S(1)}, u32[]{:S(2)}, u32[]{:S(2)}) collective-permute-start(bf16[512,512]{1,0:T(8,128)(2,1)S(1)} %broadcast_select_fusion), channel_id=1, source_target_pairs={{0,16},{16,0},{1,17},{17,1},{2,18},{18,2},{3,19},{19,3},{4,20},{20... | collective-permute-start | bytes 1572872 | tf_op jit(solution)/shard_map/ppermute | solution.py:53
  65.9 7.3 %all-to-all-done.1 = bf16[16,32,512]{2,1,0:T(8,128)(2,1)S(1)} async-done(((bf16[16,32,512]{2,1,0:T(8,128)(2,1)}), bf16[16,32,512]{2,1,0:T(8,128)(2,1)S(1)}, u32[]{:S(2)}, u32[]{:S(2)}) %all-to-all-start.1) | async-done | bytes 524320 | tf_op jit(solution)/shard_map/all_to_all | solution.py:51
  74.7 6.1 %all-to-all-start.2 = ((bf16[32,8,1024]{2,0,1:T(8,128)(2,1)}), bf16[32,8,1024]{2,0,1:T(8,128)(2,1)S(1)}, u32[]{:S(2)}, u32[]{:S(2)}) async-start(bf16[32,8,1024]{2,0,1:T(8,128)(2,1)} %copy.27), calls=%async_computation.2 | async-start | bytes 1048576 | tf_op jit(solution)/shard_map/all_to_all | solution.py:52
  80.8 2.8 %collective-permute-done = bf16[512,512]{1,0:T(8,128)(2,1)S(1)} collective-permute-done((bf16[512,512]{1,0:T(8,128)(2,1)S(1)}, bf16[512,512]{1,0:T(8,128)(2,1)S(1)}, u32[]{:S(2)}, u32[]{:S(2)}) %collective-permute-start) | collective-permute-done | bytes 524320 | tf_op jit(solution)/shard_map/ppermute | solution.py:53
  83.6 5.8 %all-to-all-done.2 = bf16[32,8,1024]{2,0,1:T(8,128)(2,1)S(1)} async-done(((bf16[32,8,1024]{2,0,1:T(8,128)(2,1)}), bf16[32,8,1024]{2,0,1:T(8,128)(2,1)S(1)}, u32[]{:S(2)}, u32[]{:S(2)}) %all-to-all-start.2) | async-done | bytes 524320 | tf_op jit(solution)/shard_map/all_to_all | solution.py:52
  90.5 2.4 broadcast_in_dim.40
  92.8 1.5 pad_maximum_fusion
  94.6 1.7 collective-permute-start.2
  97.6 20.3 %collective-permute-done.1 = bf16[2,512,512]{2,1,0:T(8,128)(2,1)S(1)} collective-permute-done((bf16[2,512,512]{2,1,0:T(8,128)(2,1)}, bf16[2,512,512]{2,1,0:T(8,128)(2,1)S(1)}, u32[]{:S(2)}, u32[]{:S(2)}) %collective-permute-start.1) | collective-permute-done | bytes 1048608 | tf_op jit(solution)/shard_map/ppermute | solution.py:59
  119.0 19.5 %collective-permute-done.2 = bf16[2,512,512]{2,1,0:T(8,128)(2,1)S(1)} collective-permute-done((bf16[2,512,512]{2,1,0:T(8,128)(2,1)}, bf16[2,512,512]{2,1,0:T(8,128)(2,1)S(1)}, u32[]{:S(2)}, u32[]{:S(2)}) %collective-permute-start.2) | collective-permute-done | bytes 1048608 | tf_op jit(solution)/shard_map/ppermute | solution.py:59
  139.5 3.4 %collective-permute-done.3 = bf16[2,512,512]{2,1,0:T(8,128)(2,1)S(1)} collective-permute-done((bf16[2,512,512]{2,1,0:T(8,128)(2,1)}, bf16[2,512,512]{2,1,0:T(8,128)(2,1)S(1)}, u32[]{:S(2)}, u32[]{:S(2)}) %collective-permute-start.3) | collective-permute-done | bytes 1048608 | tf_op jit(solution)/shard_map/ppermute | solution.py:59
  144.0 5.4 %fusion = bf16[512,512]{0,1:T(8,128)(2,1)} fusion(bf16[4096,512]{1,0:T(8,128)(2,1)} %bitcast.12, bf16[512,4096]{1,0:T(8,128)(2,1)S(1)} %copy-done.3), kind=kOutput, calls=%fused_computation.5 | convolution fusion | flops 2147745792 | bytes 8912896 | tf_op jit(solution)/shard_map/dot_general | solution.py:70
  149.7 6.0 %gather_fusion.1 = bf16[256,1024]{1,0:T(8,128)(2,1)S(1)} fusion(bf16[4096,1024]{1,0:T(8,128)(2,1)} %all-gather.3.cloned.1.call-done, s32[1024]{0:T(1024)S(1)} %pad_clamp_fusion), kind=kCustom, calls=%fused_computation.1 | custom fusion | bytes 1049600 | tf_op jit(solution)/shard_map/jit(_take)/gather | solution.py:83
  155.7 5.8 %fusion.9 = f32[4096,256]{1,0:T(8,128)S(1)} fusion(bf16[4096,1024]{1,0:T(8,128)(2,1)} %all-gather.3.cloned.1.call-done, bf16[256,1024]{1,0:T(8,128)(2,1)S(1)} %gather_fusion.1, pred[256]{0:T(512)(128)(4,1)S(1)} %compare_and_fusion.1), kind=kOutput, calls=%fused_computation.16 | convolution fusion | flops 2147745792 | bytes 13107456 | tf_op jit(solution)/shard_map/dot_general | solution.py:84
  164.2 4.7 %collective-permute-start.10 = (bf16[512,256]{1,0:T(8,128)(2,1)S(1)}, bf16[512,256]{1,0:T(8,128)(2,1)S(1)}, u32[]{:S(2)}, u32[]{:S(2)}) collective-permute-start(bf16[512,256]{1,0:T(8,128)(2,1)S(1)} %get-tuple-element.31), channel_id=1, source_target_pairs={{0,112},{16,0},{32,16},{48,32},{64,48},{80,64},{96,80},{112,96},{1... | collective-permute-start | bytes 786440 | tf_op jit(solution)/shard_map/ppermute | solution.py:91
  168.9 2.9 %copy.29 = bf16[16,8,32,512]{3,2,1,0:T(8,128)(2,1)S(1)} copy(bf16[16,8,32,512]{3,2,0,1:T(8,128)(2,1)} %bitcast.28) | data formatting | bytes 8388608 | tf_op jit(solution)/shard_map/transpose | solution.py:100
  171.9 2.7 %collective-permute-start.6 = (bf16[512,256]{1,0:T(8,128)(2,1)S(1)}, bf16[512,256]{1,0:T(8,128)(2,1)S(1)}, u32[]{:S(2)}, u32[]{:S(2)}) collective-permute-start(bf16[512,256]{1,0:T(8,128)(2,1)S(1)} %get-tuple-element.35), channel_id=1, source_target_pairs={{0,48},{16,64},{32,80},{48,96},{64,112},{80,0},{96,16},{112,32},{1... | collective-permute-start | bytes 786440 | tf_op jit(solution)/shard_map/ppermute | solution.py:91
  174.5 3.7 %collective-permute-start.7 = (bf16[512,256]{1,0:T(8,128)(2,1)S(1)}, bf16[512,256]{1,0:T(8,128)(2,1)S(1)}, u32[]{:S(2)}, u32[]{:S(2)}) collective-permute-start(bf16[512,256]{1,0:T(8,128)(2,1)S(1)} %get-tuple-element.34), channel_id=1, source_target_pairs={{0,64},{16,80},{32,96},{48,112},{64,0},{80,16},{96,32},{112,48},{1... | collective-permute-start | bytes 786440 | tf_op jit(solution)/shard_map/ppermute | solution.py:91
  178.2 6.3 %collective-permute-done.10 = bf16[512,256]{1,0:T(8,128)(2,1)S(1)} collective-permute-done((bf16[512,256]{1,0:T(8,128)(2,1)S(1)}, bf16[512,256]{1,0:T(8,128)(2,1)S(1)}, u32[]{:S(2)}, u32[]{:S(2)}) %collective-permute-start.10) | collective-permute-done | bytes 262176 | tf_op jit(solution)/shard_map/ppermute | solution.py:91
  185.1 4.5 %collective-permute-done.4 = bf16[512,256]{1,0:T(8,128)(2,1)S(1)} collective-permute-done((bf16[512,256]{1,0:T(8,128)(2,1)S(1)}, bf16[512,256]{1,0:T(8,128)(2,1)S(1)}, u32[]{:S(2)}, u32[]{:S(2)}) %collective-permute-start.4) | collective-permute-done | bytes 262176 | tf_op jit(solution)/shard_map/ppermute | solution.py:91
  189.6 4.3 %collective-permute-start.9 = (bf16[512,256]{1,0:T(8,128)(2,1)S(1)}, bf16[512,256]{1,0:T(8,128)(2,1)S(1)}, u32[]{:S(2)}, u32[]{:S(2)}) collective-permute-start(bf16[512,256]{1,0:T(8,128)(2,1)S(1)} %get-tuple-element.32), channel_id=1, source_target_pairs={{0,96},{16,112},{32,0},{48,16},{64,32},{80,48},{96,64},{112,80},{1... | collective-permute-start | bytes 786440 | tf_op jit(solution)/shard_map/ppermute | solution.py:91
  193.9 5.8 %multiply_add_fusion = f32[512,1024]{1,0:T(8,128)} fusion(f32[512,1024]{1,0:T(8,128)S(1)} %copy-done.4, bf16[4096,512]{1,0:T(8,128)(2,1)S(1)} %bitcast.72, bf16[4096,1024]{1,0:T(8,128)(2,1)S(1)} %bitcast.75), kind=kOutput, calls=%fused_computation.2 | convolution fusion | flops 4296540160 | bytes 16777216 | tf_op jit(solution)/shard_map/dot_general | solution.py:103
  199.7 5.0 %collective-permute-done.9 = bf16[512,256]{1,0:T(8,128)(2,1)S(1)} collective-permute-done((bf16[512,256]{1,0:T(8,128)(2,1)S(1)}, bf16[512,256]{1,0:T(8,128)(2,1)S(1)}, u32[]{:S(2)}, u32[]{:S(2)}) %collective-permute-start.9) | collective-permute-done | bytes 262176 | tf_op jit(solution)/shard_map/ppermute | solution.py:91
  204.8 21.4 %all-gather.5.cloned.1.call-done = bf16[512,8192]{0,1:T(8,128)(2,1)} async-done(((bf16[512,512]{0,1:T(8,128)(2,1)}), bf16[512,8192]{0,1:T(8,128)(2,1)}) %all-gather.5.cloned.1.call-update) | async-done | bytes 8388624 | tf_op jit(solution)/shard_map/all_gather | solution.py:107
  226.2 11.1 %convolution_convert_fusion = bf16[512,512]{1,0:T(8,128)(2,1)} fusion(bf16[512,8192]{0,1:T(8,128)(2,1)} %all-gather.5.cloned.1.call-done, bf16[512,8192]{1,0:T(8,128)(2,1)} %param.11), kind=kOutput, calls=%fused_computation.3 | convolution fusion | flops 4295229440 | bytes 17301504 | tf_op jit(solution)/shard_map/dot_general | solution.py:112
  237.3 2.1 fusion.8
  (56 shorter events, 14.3 us)
Async XLA Ops:
  32.2 23.7 %all-to-all-start = ((bf16[64,16,512]{2,0,1:T(8,128)(2,1)}), bf16[64,16,512]{2,0,1:T(8,128)(2,1)S(1)}, u32[]{:S(2)}, u32[]{:S(2)}) async-start(bf16[64,16,512]{2,0,1:T(8,128)(2,1)} %copy.25), calls=%async_computation | async-start | bytes 2097152 | tf_op jit(solution)/shard_map/all_to_all | solution.py:48
  58.8 14.4 %all-to-all-start.1 = ((bf16[16,32,512]{2,1,0:T(8,128)(2,1)}), bf16[16,32,512]{2,1,0:T(8,128)(2,1)S(1)}, u32[]{:S(2)}, u32[]{:S(2)}) async-start(bf16[16,32,512]{2,1,0:T(8,128)(2,1)} %broadcast_select_fusion.1), calls=%async_computation.1 | async-start | bytes 1048576 | tf_op jit(solution)/shard_map/all_to_all | solution.py:51
  63.2 20.5 %collective-permute-start = (bf16[512,512]{1,0:T(8,128)(2,1)S(1)}, bf16[512,512]{1,0:T(8,128)(2,1)S(1)}, u32[]{:S(2)}, u32[]{:S(2)}) collective-permute-start(bf16[512,512]{1,0:T(8,128)(2,1)S(1)} %broadcast_select_fusion), channel_id=1, source_target_pairs={{0,16},{16,0},{1,17},{17,1},{2,18},{18,2},{3,19},{19,3},{4,20},{20... | collective-permute-start | bytes 1572872 | tf_op jit(solution)/shard_map/ppermute | solution.py:53
  74.7 14.7 %all-to-all-start.2 = ((bf16[32,8,1024]{2,0,1:T(8,128)(2,1)}), bf16[32,8,1024]{2,0,1:T(8,128)(2,1)S(1)}, u32[]{:S(2)}, u32[]{:S(2)}) async-start(bf16[32,8,1024]{2,0,1:T(8,128)(2,1)} %copy.27), calls=%async_computation.2 | async-start | bytes 1048576 | tf_op jit(solution)/shard_map/all_to_all | solution.py:52
  80.8 68.7 %all-gather.3.cloned.1.call-start = ((), (), s32[]{:S(2)}) async-start(), calls=%async_computation.3 | async-start | bytes 8912896 | tf_op jit(solution)/shard_map/all_gather | solution.py:62
  89.4 0.8 copy-start.1
  90.2 135.9 %all-gather.5.cloned.1.call-start = ((), (), s32[]{:S(2)}) async-start(), calls=%async_computation.4 | async-start | bytes 8912896 | tf_op jit(solution)/shard_map/all_gather | solution.py:107
  94.4 23.5 %collective-permute-start.1 = (bf16[2,512,512]{2,1,0:T(8,128)(2,1)}, bf16[2,512,512]{2,1,0:T(8,128)(2,1)S(1)}, u32[]{:S(2)}, u32[]{:S(2)}) collective-permute-start(bf16[2,512,512]{2,1,0:T(8,128)(2,1)} %get-tuple-element.38), channel_id=1, source_target_pairs={{0,32},{32,64},{64,96},{96,0},{1,33},{33,65},{65,97},{97,1},{2,34}... | collective-permute-start | bytes 3145736 | tf_op jit(solution)/shard_map/ppermute | solution.py:59
  94.6 43.9 %collective-permute-start.2 = (bf16[2,512,512]{2,1,0:T(8,128)(2,1)}, bf16[2,512,512]{2,1,0:T(8,128)(2,1)S(1)}, u32[]{:S(2)}, u32[]{:S(2)}) collective-permute-start(bf16[2,512,512]{2,1,0:T(8,128)(2,1)} %get-tuple-element.38), channel_id=1, source_target_pairs={{0,64},{32,96},{64,0},{96,32},{1,65},{33,97},{65,1},{97,33},{2,66}... | collective-permute-start | bytes 3145736 | tf_op jit(solution)/shard_map/ppermute | solution.py:59
  96.3 46.7 %collective-permute-start.3 = (bf16[2,512,512]{2,1,0:T(8,128)(2,1)}, bf16[2,512,512]{2,1,0:T(8,128)(2,1)S(1)}, u32[]{:S(2)}, u32[]{:S(2)}) collective-permute-start(bf16[2,512,512]{2,1,0:T(8,128)(2,1)} %get-tuple-element.38), channel_id=1, source_target_pairs={{0,96},{32,0},{64,32},{96,64},{1,97},{33,1},{65,33},{97,65},{2,98}... | collective-permute-start | bytes 3145736 | tf_op jit(solution)/shard_map/ppermute | solution.py:59
  97.6 46.5 %copy-start.3 = (bf16[512,4096]{1,0:T(8,128)(2,1)S(1)}, bf16[512,4096]{1,0:T(8,128)(2,1)}, u32[]{:S(2)}) copy-start(bf16[512,4096]{1,0:T(8,128)(2,1)} %param.10) | copy-start | bytes 12582916
  162.0 2.1 copy-start
  162.0 31.8 %slice-start = ((s8[8388608]{0:T(1024)(128)(4,1)}), s8[4194304]{0:T(1024)(128)(4,1)S(1)}, s32[]{:S(2)}) async-start(s8[8388608]{0:T(1024)(128)(4,1)} %bitcast.74), calls=%async_computation.5 | async-start | bytes 8388608
  162.5 31.3 %slice-start.1 = ((s8[8388608]{0:T(1024)(128)(4,1)}), s8[4194304]{0:T(1024)(128)(4,1)S(1)}, s32[]{:S(2)}) async-start(s8[8388608]{0:T(1024)(128)(4,1)} %bitcast.74), calls=%async_computation.6 | async-start | bytes 8388608
  164.2 20.3 %collective-permute-start.10 = (bf16[512,256]{1,0:T(8,128)(2,1)S(1)}, bf16[512,256]{1,0:T(8,128)(2,1)S(1)}, u32[]{:S(2)}, u32[]{:S(2)}) collective-permute-start(bf16[512,256]{1,0:T(8,128)(2,1)S(1)} %get-tuple-element.31), channel_id=1, source_target_pairs={{0,112},{16,0},{32,16},{48,32},{64,48},{80,64},{96,80},{112,96},{1... | collective-permute-start | bytes 786440 | tf_op jit(solution)/shard_map/ppermute | solution.py:91
  168.9 20.7 %collective-permute-start.4 = (bf16[512,256]{1,0:T(8,128)(2,1)S(1)}, bf16[512,256]{1,0:T(8,128)(2,1)S(1)}, u32[]{:S(2)}, u32[]{:S(2)}) collective-permute-start(bf16[512,256]{1,0:T(8,128)(2,1)S(1)} %get-tuple-element.37), channel_id=1, source_target_pairs={{0,16},{16,32},{32,48},{48,64},{64,80},{80,96},{96,112},{112,0},{1... | collective-permute-start | bytes 786440 | tf_op jit(solution)/shard_map/ppermute | solution.py:91
  168.9 25.0 %copy-start.4 = (f32[512,1024]{1,0:T(8,128)S(1)}, f32[512,1024]{1,0:T(8,128)}, u32[]{:S(2)}) copy-start(f32[512,1024]{1,0:T(8,128)} %param.9) | copy-start | bytes 6291460
  171.8 27.9 %collective-permute-start.5 = (bf16[512,256]{1,0:T(8,128)(2,1)S(1)}, bf16[512,256]{1,0:T(8,128)(2,1)S(1)}, u32[]{:S(2)}, u32[]{:S(2)}) collective-permute-start(bf16[512,256]{1,0:T(8,128)(2,1)S(1)} %get-tuple-element.36), channel_id=1, source_target_pairs={{0,32},{16,48},{32,64},{48,80},{64,96},{80,112},{96,0},{112,16},{1... | collective-permute-start | bytes 786440 | tf_op jit(solution)/shard_map/ppermute | solution.py:91
  171.9 27.9 %collective-permute-start.6 = (bf16[512,256]{1,0:T(8,128)(2,1)S(1)}, bf16[512,256]{1,0:T(8,128)(2,1)S(1)}, u32[]{:S(2)}, u32[]{:S(2)}) collective-permute-start(bf16[512,256]{1,0:T(8,128)(2,1)S(1)} %get-tuple-element.35), channel_id=1, source_target_pairs={{0,48},{16,64},{32,80},{48,96},{64,112},{80,0},{96,16},{112,32},{1... | collective-permute-start | bytes 786440 | tf_op jit(solution)/shard_map/ppermute | solution.py:91
  174.5 25.2 %collective-permute-start.7 = (bf16[512,256]{1,0:T(8,128)(2,1)S(1)}, bf16[512,256]{1,0:T(8,128)(2,1)S(1)}, u32[]{:S(2)}, u32[]{:S(2)}) collective-permute-start(bf16[512,256]{1,0:T(8,128)(2,1)S(1)} %get-tuple-element.34), channel_id=1, source_target_pairs={{0,64},{16,80},{32,96},{48,112},{64,0},{80,16},{96,32},{112,48},{1... | collective-permute-start | bytes 786440 | tf_op jit(solution)/shard_map/ppermute | solution.py:91
  184.5 15.3 %collective-permute-start.8 = (bf16[512,256]{1,0:T(8,128)(2,1)S(1)}, bf16[512,256]{1,0:T(8,128)(2,1)S(1)}, u32[]{:S(2)}, u32[]{:S(2)}) collective-permute-start(bf16[512,256]{1,0:T(8,128)(2,1)S(1)} %get-tuple-element.33), channel_id=1, source_target_pairs={{0,80},{16,96},{32,112},{48,0},{64,16},{80,32},{96,48},{112,64},{1... | collective-permute-start | bytes 786440 | tf_op jit(solution)/shard_map/ppermute | solution.py:91
  189.6 15.2 %collective-permute-start.9 = (bf16[512,256]{1,0:T(8,128)(2,1)S(1)}, bf16[512,256]{1,0:T(8,128)(2,1)S(1)}, u32[]{:S(2)}, u32[]{:S(2)}) collective-permute-start(bf16[512,256]{1,0:T(8,128)(2,1)S(1)} %get-tuple-element.32), channel_id=1, source_target_pairs={{0,96},{16,112},{32,0},{48,16},{64,32},{80,48},{96,64},{112,80},{1... | collective-permute-start | bytes 786440 | tf_op jit(solution)/shard_map/ppermute | solution.py:91
  199.7 37.6 %copy-start.2 = (f32[512,256]{1,0:T(8,128)S(1)}, f32[512,256]{1,0:T(8,128)}, u32[]{:S(2)}) copy-start(f32[512,256]{1,0:T(8,128)} %param.8) | copy-start | bytes 1572868
Sparse Core Ops, SparseCore 0:
  90.4 52.3 all-gather.2
  149.6 76.5 all-gather.4

commit v14 on v13

--- a/solution.py
+++ b/solution.py
@@ -86,14 +86,15 @@
     )
     left_part = left_part.reshape(col_count, row_count, slice_rows, chunk).transpose(1, 0, 2, 3)
     left_part = left_part.reshape(row_count, tile_rows, chunk)
-    outgoing = left_part.astype(jnp.bfloat16)
+    pair_parts = left_part.reshape(x_count, 2, tile_rows, chunk)
+    outgoing = pair_parts.astype(jnp.bfloat16)
     incoming = [
         lax.ppermute(
-            lax.dynamic_index_in_dim(outgoing, (row_index + s) % row_count, 0, keepdims=False),
-            ROW,
-            [(i, (i + s) % row_count) for i in range(row_count)],
+            lax.dynamic_index_in_dim(outgoing, (x_index + s) % x_count, 0, keepdims=False),
+            "x",
+            [(i, (i + s) % x_count) for i in range(x_count)],
         )
-        for s in range(1, row_count)
+        for s in range(1, x_count)
     ]
     panel_reordered = (
         column_panel.reshape(row_count, col_count, slice_rows, tile_cols)
@@ -106,9 +107,15 @@
     right_new = stat_decay * right_stat + right_gram * (1.0 / math.sqrt(HQ))
     mixed_rows = lax.all_gather(left_mixed, COL, axis=1, tiled=True)
     incoming, mixed_rows = lax.optimization_barrier((incoming, mixed_rows))
-    left_sum = lax.dynamic_index_in_dim(left_part, row_index, 0, keepdims=False)
+    x_sum = lax.dynamic_index_in_dim(pair_parts, x_index, 0, keepdims=False)
     for part in incoming:
-        left_sum = left_sum + part.astype(jnp.float32)
+        x_sum = x_sum + part.astype(jnp.float32)
+    across = lax.ppermute(
+        lax.dynamic_index_in_dim(x_sum, 1 - y_half, 0, keepdims=False).astype(jnp.bfloat16),
+        "yh",
+        [(0, 1), (1, 0)],
+    )
+    left_sum = lax.dynamic_index_in_dim(x_sum, y_half, 0, keepdims=False) + across.astype(jnp.float32)
     update_sum = lax.dot_general(
         mixed_rows,
         right_root,

time: 247 us -> 228 us (0.923)
  waiting for transfers between devices: 110 us -> 94.4 us
  starting transfers between devices: 40.2 us -> 31.4 us
  matrix products: 28.2 us -> 31.9 us
    all_gather x1, waiting for transfers between devices: 21.4 us -> 7.9 us  [shards(): mixed_rows = lax.all_gather(left_mixed, COL, axis=1, tiled=True)]
    ppermute x7 -> x4, starting transfers between devices: 16 us -> 7.21 us  [the longest x3 4.4 us: shards(): lax.ppermute(lax.dynamic_index_in_dim(outgoing, (x_index + s) % x_count,...]
    dot_general x1, matrix products: 5.84 us -> 9.46 us  [shards(): lax.dot_general(panel_reordered, row_block, (((0,), (0,)), ((), ())), pre...]
    ppermute x7 -> x4, waiting for transfers between devices: 15.8 us -> 13.3 us  [the longest x3 13.3 us: shards(): lax.ppermute(lax.dynamic_index_in_dim(outgoing, (x_index + s) % x_count,...]
    unnamed x2 -> x1, other arithmetic: 22.8 us -> 22.8 us
  transfers between devices with their start and end apart: 16 -> 13, of which waited for: 11 -> 9; matrix products, arithmetic and copies ran while one was open for 15% -> 24% of each run, Pallas kernels for 0% -> 0%
where the time goes in v14:
time: 228 us; the launch traced here: 227 us
  waiting for transfers between devices  94.4 us (41%)
  matrix products  31.9 us (14%)
  starting transfers between devices  31.4 us (14%)
  other arithmetic  29.1 us (13%)
  local copies, waits for them, and re-layouts  25.9 us (11%)
  between operations  14.3 us (6%)
    ppermute x3, waiting for transfers between devices, shards(): lax.ppermute(pair, 'x', [(i, (i + s) % x_count) for i in range(x_count)])  43.3 us
    unnamed x1, other arithmetic  22.8 us
    all_to_all x1, waiting for transfers between devices, shards(): lax.all_to_all(held_rows, COL, split_axis=1, concat_axis=0, tiled=True)  13.9 us
    ppermute x3, waiting for transfers between devices, shards(): lax.ppermute(lax.dynamic_index_in_dim(outgoing, (x_index + s) % x_count,...  13.3 us
    dot_general x1, matrix products, shards(): lax.dot_general(mixed_rows, right_root, (((1,), (1,)), ((), ())), preferr...  11.1 us
    dot_general x1, matrix products, shards(): lax.dot_general(panel_reordered, row_block, (((0,), (0,)), ((), ())), pre...  9.46 us
    all_gather x1, waiting for transfers between devices, shards(): mixed_rows = lax.all_gather(left_mixed, COL, axis=1, tiled=True)  7.9 us
    all_to_all x1, starting transfers between devices, shards(): lax.all_to_all(held_rows, COL, split_axis=1, concat_axis=0, tiled=True)  7.84 us
  transfers between devices with their start and end apart: 13, of which 9 were waited for; matrix products, arithmetic and copies ran while one was open for 24% of the time, Pallas kernels for 0%

profile of v14, /device:TPU:1, one launch (start us, length us, event | category | flops | bytes accessed | tf_op | source)
XLA Modules:
  0.0 226.9 jit_solution(9901679162960642926)
XLA Ops:
  7.2 22.8 %reduce = bf16[524288]{0:T(1024)(128)(2,1)S(1)} reduce(bf16[1,1,524288]{2,1,0:T(2,128)(2,1)} %param.6, bf16[]{:T(256)} %constant.189), dimensions={0,1}, to_apply=%param.6.reduce_sub_computation | reduce | bytes 2097154 | tf_op args[0]
  30.6 1.5 copy.25
  32.2 7.8 %all-to-all-start = ((bf16[64,16,512]{2,0,1:T(8,128)(2,1)}), bf16[64,16,512]{2,0,1:T(8,128)(2,1)S(1)}, u32[]{:S(2)}, u32[]{:S(2)}) async-start(bf16[64,16,512]{2,0,1:T(8,128)(2,1)} %copy.25), calls=%async_computation | async-start | bytes 2097152 | tf_op jit(solution)/shard_map/all_to_all | solution.py:48
  41.9 13.9 %all-to-all-done = bf16[64,16,512]{2,0,1:T(8,128)(2,1)S(1)} async-done(((bf16[64,16,512]{2,0,1:T(8,128)(2,1)}), bf16[64,16,512]{2,0,1:T(8,128)(2,1)S(1)}, u32[]{:S(2)}, u32[]{:S(2)}) %all-to-all-start) | async-done | bytes 1048608 | tf_op jit(solution)/shard_map/all_to_all | solution.py:48
  55.9 2.0 gather_fusion
  58.8 4.2 %all-to-all-start.1 = ((bf16[16,32,512]{2,1,0:T(8,128)(2,1)}), bf16[16,32,512]{2,1,0:T(8,128)(2,1)S(1)}, u32[]{:S(2)}, u32[]{:S(2)}) async-start(bf16[16,32,512]{2,1,0:T(8,128)(2,1)} %broadcast_select_fusion.1), calls=%async_computation.1 | async-start | bytes 1048576 | tf_op jit(solution)/shard_map/all_to_all | solution.py:51
  63.2 2.7 %collective-permute-start = (bf16[512,512]{1,0:T(8,128)(2,1)S(1)}, bf16[512,512]{1,0:T(8,128)(2,1)S(1)}, u32[]{:S(2)}, u32[]{:S(2)}) collective-permute-start(bf16[512,512]{1,0:T(8,128)(2,1)S(1)} %broadcast_select_fusion), channel_id=1, source_target_pairs={{0,16},{16,0},{1,17},{17,1},{2,18},{18,2},{3,19},{19,3},{4,20},{20... | collective-permute-start | bytes 1572872 | tf_op jit(solution)/shard_map/ppermute | solution.py:53
  65.9 7.3 %all-to-all-done.1 = bf16[16,32,512]{2,1,0:T(8,128)(2,1)S(1)} async-done(((bf16[16,32,512]{2,1,0:T(8,128)(2,1)}), bf16[16,32,512]{2,1,0:T(8,128)(2,1)S(1)}, u32[]{:S(2)}, u32[]{:S(2)}) %all-to-all-start.1) | async-done | bytes 524320 | tf_op jit(solution)/shard_map/all_to_all | solution.py:51
  73.6 1.1 copy.27
  74.7 6.1 %all-to-all-start.2 = ((bf16[32,8,1024]{2,0,1:T(8,128)(2,1)}), bf16[32,8,1024]{2,0,1:T(8,128)(2,1)S(1)}, u32[]{:S(2)}, u32[]{:S(2)}) async-start(bf16[32,8,1024]{2,0,1:T(8,128)(2,1)} %copy.27), calls=%async_computation.2 | async-start | bytes 1048576 | tf_op jit(solution)/shard_map/all_to_all | solution.py:52
  80.8 2.8 %collective-permute-done = bf16[512,512]{1,0:T(8,128)(2,1)S(1)} collective-permute-done((bf16[512,512]{1,0:T(8,128)(2,1)S(1)}, bf16[512,512]{1,0:T(8,128)(2,1)S(1)}, u32[]{:S(2)}, u32[]{:S(2)}) %collective-permute-start) | collective-permute-done | bytes 524320 | tf_op jit(solution)/shard_map/ppermute | solution.py:53
  83.6 5.8 %all-to-all-done.2 = bf16[32,8,1024]{2,0,1:T(8,128)(2,1)S(1)} async-done(((bf16[32,8,1024]{2,0,1:T(8,128)(2,1)}), bf16[32,8,1024]{2,0,1:T(8,128)(2,1)S(1)}, u32[]{:S(2)}, u32[]{:S(2)}) %all-to-all-start.2) | async-done | bytes 524320 | tf_op jit(solution)/shard_map/all_to_all | solution.py:52
  90.5 2.3 %broadcast_in_dim.40 = bf16[8,512,512]{2,1,0:T(8,128)(2,1)} broadcast(bf16[]{:T(256)} %constant.160.clone.1), dimensions={} | broadcast | bytes 4194306 | tf_op jit(solution)/shard_map/broadcast_in_dim | solution.py:63
  92.8 1.5 pad_maximum_fusion
  94.6 1.6 collective-permute-start.2
  96.2 1.3 collective-permute-start.3
  97.5 20.3 %collective-permute-done.1 = bf16[2,512,512]{2,1,0:T(8,128)(2,1)S(1)} collective-permute-done((bf16[2,512,512]{2,1,0:T(8,128)(2,1)}, bf16[2,512,512]{2,1,0:T(8,128)(2,1)S(1)}, u32[]{:S(2)}, u32[]{:S(2)}) %collective-permute-start.1) | collective-permute-done | bytes 1048608 | tf_op jit(solution)/shard_map/ppermute | solution.py:59
  118.9 19.5 %collective-permute-done.2 = bf16[2,512,512]{2,1,0:T(8,128)(2,1)S(1)} collective-permute-done((bf16[2,512,512]{2,1,0:T(8,128)(2,1)}, bf16[2,512,512]{2,1,0:T(8,128)(2,1)S(1)}, u32[]{:S(2)}, u32[]{:S(2)}) %collective-permute-start.2) | collective-permute-done | bytes 1048608 | tf_op jit(solution)/shard_map/ppermute | solution.py:59
  139.4 3.5 %collective-permute-done.3 = bf16[2,512,512]{2,1,0:T(8,128)(2,1)S(1)} collective-permute-done((bf16[2,512,512]{2,1,0:T(8,128)(2,1)}, bf16[2,512,512]{2,1,0:T(8,128)(2,1)S(1)}, u32[]{:S(2)}, u32[]{:S(2)}) %collective-permute-start.3) | collective-permute-done | bytes 1048608 | tf_op jit(solution)/shard_map/ppermute | solution.py:59
  144.0 5.4 %fusion = bf16[512,512]{0,1:T(8,128)(2,1)} fusion(bf16[4096,512]{1,0:T(8,128)(2,1)} %bitcast.12, bf16[512,4096]{1,0:T(8,128)(2,1)S(1)} %copy-done.4), kind=kOutput, calls=%fused_computation.5 | convolution fusion | flops 2147745792 | bytes 8912896 | tf_op jit(solution)/shard_map/dot_general | solution.py:70
  149.6 4.8 %copy.29 = bf16[16,8,32,512]{3,2,1,0:T(8,128)(2,1)} copy(bf16[16,8,32,512]{3,2,0,1:T(8,128)(2,1)} %bitcast.26) | data formatting | bytes 8388608 | tf_op jit(solution)/shard_map/transpose | solution.py:101
  154.3 6.0 %gather_fusion.1 = bf16[256,1024]{1,0:T(8,128)(2,1)S(1)} fusion(bf16[4096,1024]{1,0:T(8,128)(2,1)} %all-gather.3.cloned.1.call-done, s32[1024]{0:T(1024)S(1)} %pad_clamp_fusion), kind=kCustom, calls=%fused_computation.1 | custom fusion | bytes 1049600 | tf_op jit(solution)/shard_map/jit(_take)/gather | solution.py:83
  160.3 5.9 %fusion.5 = f32[4096,256]{1,0:T(8,128)S(1)} fusion(bf16[4096,1024]{1,0:T(8,128)(2,1)} %all-gather.3.cloned.1.call-done, bf16[256,1024]{1,0:T(8,128)(2,1)S(1)} %gather_fusion.1, pred[256]{0:T(512)(128)(4,1)S(1)} %compare_and_fusion.1), kind=kOutput, calls=%fused_computation.17 | convolution fusion | flops 2147745792 | bytes 13107456 | tf_op jit(solution)/shard_map/dot_general | solution.py:84
  167.0 1.8 copy-done
  168.7 1.4 collective-permute-start.4
  170.2 3.0 %collective-permute-start.5 = (bf16[2,512,256]{2,1,0:T(8,128)(2,1)S(1)}, bf16[2,512,256]{2,1,0:T(8,128)(2,1)S(1)}, u32[]{:S(2)}, u32[]{:S(2)}) collective-permute-start(bf16[2,512,256]{2,1,0:T(8,128)(2,1)S(1)} %get-tuple-element.24), channel_id=1, source_target_pairs={{0,64},{32,96},{64,0},{96,32},{1,65},{33,97},{65,1},{97,33},{2,66}... | collective-permute-start | bytes 1572872 | tf_op jit(solution)/shard_map/ppermute | solution.py:92
  173.1 9.5 %multiply_add_fusion = f32[512,1024]{1,0:T(8,128)} fusion(f32[512,1024]{1,0:T(8,128)S(1)} %copy-done.5, bf16[4096,512]{1,0:T(8,128)(2,1)S(1)} %bitcast.60, bf16[4096,1024]{1,0:T(8,128)(2,1)} %all-gather.3.cloned.1.call-done), kind=kOutput, calls=%fused_computation.2 | convolution fusion | flops 4296540160 | bytes 16777216 | tf_op jit(solution)/shard_map/dot_general | solution.py:104
  182.6 13.3 %collective-permute-done.5 = bf16[2,512,256]{2,1,0:T(8,128)(2,1)S(1)} collective-permute-done((bf16[2,512,256]{2,1,0:T(8,128)(2,1)S(1)}, bf16[2,512,256]{2,1,0:T(8,128)(2,1)S(1)}, u32[]{:S(2)}, u32[]{:S(2)}) %collective-permute-start.5) | collective-permute-done | bytes 524320 | tf_op jit(solution)/shard_map/ppermute | solution.py:92
  195.9 7.9 %all-gather.5.cloned.1.call-done = bf16[512,8192]{0,1:T(8,128)(2,1)} async-done(((bf16[512,512]{0,1:T(8,128)(2,1)}), bf16[512,8192]{0,1:T(8,128)(2,1)}) %all-gather.5.cloned.1.call-update) | async-done | bytes 8388624 | tf_op jit(solution)/shard_map/all_gather | solution.py:108
  203.8 1.4 fusion.2
  205.3 2.8 %collective-permute-start.7 = (bf16[512,256]{1,0:T(8,128)(2,1)S(1)}, bf16[512,256]{1,0:T(8,128)(2,1)S(1)}, u32[]{:S(2)}, u32[]{:S(2)}) collective-permute-start(bf16[512,256]{1,0:T(8,128)(2,1)S(1)} %fusion.8), channel_id=1, source_target_pairs={{0,16},{16,0},{1,17},{17,1},{2,18},{18,2},{3,19},{19,3},{4,20},{20... | collective-permute-start | bytes 786440 | tf_op jit(solution)/shard_map/ppermute | solution.py:113
  208.1 11.1 %convolution_convert_fusion = bf16[512,512]{1,0:T(8,128)(2,1)} fusion(bf16[512,8192]{0,1:T(8,128)(2,1)} %all-gather.5.cloned.1.call-done, bf16[512,8192]{1,0:T(8,128)(2,1)} %param.11), kind=kOutput, calls=%fused_computation.3 | convolution fusion | flops 4295229440 | bytes 17301504 | tf_op jit(solution)/shard_map/dot_general | solution.py:119
  (49 shorter events, 10.3 us)
Async XLA Ops:
  32.2 23.7 %all-to-all-start = ((bf16[64,16,512]{2,0,1:T(8,128)(2,1)}), bf16[64,16,512]{2,0,1:T(8,128)(2,1)S(1)}, u32[]{:S(2)}, u32[]{:S(2)}) async-start(bf16[64,16,512]{2,0,1:T(8,128)(2,1)} %copy.25), calls=%async_computation | async-start | bytes 2097152 | tf_op jit(solution)/shard_map/all_to_all | solution.py:48
  58.8 14.4 %all-to-all-start.1 = ((bf16[16,32,512]{2,1,0:T(8,128)(2,1)}), bf16[16,32,512]{2,1,0:T(8,128)(2,1)S(1)}, u32[]{:S(2)}, u32[]{:S(2)}) async-start(bf16[16,32,512]{2,1,0:T(8,128)(2,1)} %broadcast_select_fusion.1), calls=%async_computation.1 | async-start | bytes 1048576 | tf_op jit(solution)/shard_map/all_to_all | solution.py:51
  63.2 20.5 %collective-permute-start = (bf16[512,512]{1,0:T(8,128)(2,1)S(1)}, bf16[512,512]{1,0:T(8,128)(2,1)S(1)}, u32[]{:S(2)}, u32[]{:S(2)}) collective-permute-start(bf16[512,512]{1,0:T(8,128)(2,1)S(1)} %broadcast_select_fusion), channel_id=1, source_target_pairs={{0,16},{16,0},{1,17},{17,1},{2,18},{18,2},{3,19},{19,3},{4,20},{20... | collective-permute-start | bytes 1572872 | tf_op jit(solution)/shard_map/ppermute | solution.py:53
  74.7 14.7 %all-to-all-start.2 = ((bf16[32,8,1024]{2,0,1:T(8,128)(2,1)}), bf16[32,8,1024]{2,0,1:T(8,128)(2,1)S(1)}, u32[]{:S(2)}, u32[]{:S(2)}) async-start(bf16[32,8,1024]{2,0,1:T(8,128)(2,1)} %copy.27), calls=%async_computation.2 | async-start | bytes 1048576 | tf_op jit(solution)/shard_map/all_to_all | solution.py:52
  80.8 68.6 %all-gather.3.cloned.1.call-start = ((), (), s32[]{:S(2)}) async-start(), calls=%async_computation.3 | async-start | bytes 8912896 | tf_op jit(solution)/shard_map/all_gather | solution.py:62
  89.4 0.8 copy-start.2
  90.2 113.6 %all-gather.5.cloned.1.call-start = ((), (), s32[]{:S(2)}) async-start(), calls=%async_computation.4 | async-start | bytes 8912896 | tf_op jit(solution)/shard_map/all_gather | solution.py:108
  94.3 23.6 %collective-permute-start.1 = (bf16[2,512,512]{2,1,0:T(8,128)(2,1)}, bf16[2,512,512]{2,1,0:T(8,128)(2,1)S(1)}, u32[]{:S(2)}, u32[]{:S(2)}) collective-permute-start(bf16[2,512,512]{2,1,0:T(8,128)(2,1)} %get-tuple-element.26), channel_id=1, source_target_pairs={{0,32},{32,64},{64,96},{96,0},{1,33},{33,65},{65,97},{97,1},{2,34}... | collective-permute-start | bytes 3145736 | tf_op jit(solution)/shard_map/ppermute | solution.py:59
  94.6 43.8 %collective-permute-start.2 = (bf16[2,512,512]{2,1,0:T(8,128)(2,1)}, bf16[2,512,512]{2,1,0:T(8,128)(2,1)S(1)}, u32[]{:S(2)}, u32[]{:S(2)}) collective-permute-start(bf16[2,512,512]{2,1,0:T(8,128)(2,1)} %get-tuple-element.26), channel_id=1, source_target_pairs={{0,64},{32,96},{64,0},{96,32},{1,65},{33,97},{65,1},{97,33},{2,66}... | collective-permute-start | bytes 3145736 | tf_op jit(solution)/shard_map/ppermute | solution.py:59
  96.2 46.7 %collective-permute-start.3 = (bf16[2,512,512]{2,1,0:T(8,128)(2,1)}, bf16[2,512,512]{2,1,0:T(8,128)(2,1)S(1)}, u32[]{:S(2)}, u32[]{:S(2)}) collective-permute-start(bf16[2,512,512]{2,1,0:T(8,128)(2,1)} %get-tuple-element.26), channel_id=1, source_target_pairs={{0,96},{32,0},{64,32},{96,64},{1,97},{33,1},{65,33},{97,65},{2,98}... | collective-permute-start | bytes 3145736 | tf_op jit(solution)/shard_map/ppermute | solution.py:59
  97.5 46.5 %copy-start.4 = (bf16[512,4096]{1,0:T(8,128)(2,1)S(1)}, bf16[512,4096]{1,0:T(8,128)(2,1)}, u32[]{:S(2)}) copy-start(bf16[512,4096]{1,0:T(8,128)(2,1)} %param.10) | copy-start | bytes 12582916
  166.6 2.2 copy-start
  166.6 6.5 %copy-start.1 = (bf16[16,8,32,512]{3,2,1,0:T(8,128)(2,1)S(1)}, bf16[16,8,32,512]{3,2,1,0:T(8,128)(2,1)}, u32[]{:S(2)}) copy-start(bf16[16,8,32,512]{3,2,1,0:T(8,128)(2,1)} %copy.29) | copy-start | bytes 12582916
  166.6 6.5 %copy-start.5 = (f32[512,1024]{1,0:T(8,128)S(1)}, f32[512,1024]{1,0:T(8,128)}, u32[]{:S(2)}) copy-start(f32[512,1024]{1,0:T(8,128)} %param.9) | copy-start | bytes 6291460
  168.7 13.9 %collective-permute-start.4 = (bf16[2,512,256]{2,1,0:T(8,128)(2,1)S(1)}, bf16[2,512,256]{2,1,0:T(8,128)(2,1)S(1)}, u32[]{:S(2)}, u32[]{:S(2)}) collective-permute-start(bf16[2,512,256]{2,1,0:T(8,128)(2,1)S(1)} %get-tuple-element.25), channel_id=1, source_target_pairs={{0,32},{32,64},{64,96},{96,0},{1,33},{33,65},{65,97},{97,1},{2,34}... | collective-permute-start | bytes 1572872 | tf_op jit(solution)/shard_map/ppermute | solution.py:92
  170.2 25.7 %collective-permute-start.5 = (bf16[2,512,256]{2,1,0:T(8,128)(2,1)S(1)}, bf16[2,512,256]{2,1,0:T(8,128)(2,1)S(1)}, u32[]{:S(2)}, u32[]{:S(2)}) collective-permute-start(bf16[2,512,256]{2,1,0:T(8,128)(2,1)S(1)} %get-tuple-element.24), channel_id=1, source_target_pairs={{0,64},{32,96},{64,0},{96,32},{1,65},{33,97},{65,1},{97,33},{2,66}... | collective-permute-start | bytes 1572872 | tf_op jit(solution)/shard_map/ppermute | solution.py:92
  173.1 22.8 %collective-permute-start.6 = (bf16[2,512,256]{2,1,0:T(8,128)(2,1)S(1)}, bf16[2,512,256]{2,1,0:T(8,128)(2,1)S(1)}, u32[]{:S(2)}, u32[]{:S(2)}) collective-permute-start(bf16[2,512,256]{2,1,0:T(8,128)(2,1)S(1)} %get-tuple-element.23), channel_id=1, source_target_pairs={{0,96},{32,0},{64,32},{96,64},{1,97},{33,1},{65,33},{97,65},{2,98}... | collective-permute-start | bytes 1572872 | tf_op jit(solution)/shard_map/ppermute | solution.py:92
  205.3 13.9 %copy-start.3 = (f32[512,256]{1,0:T(8,128)S(1)}, f32[512,256]{1,0:T(8,128)}, u32[]{:S(2)}) copy-start(f32[512,256]{1,0:T(8,128)} %param.8) | copy-start | bytes 1572868
  205.3 13.9 %collective-permute-start.7 = (bf16[512,256]{1,0:T(8,128)(2,1)S(1)}, bf16[512,256]{1,0:T(8,128)(2,1)S(1)}, u32[]{:S(2)}, u32[]{:S(2)}) collective-permute-start(bf16[512,256]{1,0:T(8,128)(2,1)S(1)} %fusion.8), channel_id=1, source_target_pairs={{0,16},{16,0},{1,17},{17,1},{2,18},{18,2},{3,19},{19,3},{4,20},{20... | collective-permute-start | bytes 786440 | tf_op jit(solution)/shard_map/ppermute | solution.py:113
Sparse Core Ops, SparseCore 0:
  90.4 52.3 all-gather.2
  149.6 54.1 all-gather.4
